TPU v7x, 256 devices: a whole 4x4x8 slice. The times are simulated.
256 devices in a mesh: seq: 32 (over x, y, core), exp: 8 (over z).
Axes of the slice: x: 4, y: 4, z: 8, core: 2. Of those that a mesh axis runs over, the one named last changes fastest.
Arguments:
- query_rows: bfloat16 [2048, 8192], P('seq', 'exp'), may hold values from -6 to 6
- key_rows: bfloat16 [2048, 8192], P('seq', 'exp'), may hold values from -6 to 6
- value_rows: bfloat16 [2048, 8192], P('seq', 'exp'), may hold values from -120 to 120
- log_decay: float32 [2048, 64], P('seq', 'exp'), may hold values from -1.4625 to 0, as said below
- out_weight: bfloat16 [8192, 6144], P('exp', 'seq'), may hold values from -0.0625 to 0.0625
- residual: bfloat16 [2048, 6144], P('exp', 'seq'), may hold values from -18 to 18
- routes: int32 [2048, 2], P('exp'), may hold values from 0 to 7, all different within a row; in each aligned block of 256 rows (0 to 255, 256 to 511, ...) at most 128 rows name the same one
- gate_weight: bfloat16 [8, 9216, 6144], P('exp', 'seq'), may hold values from -0.078125 to 0.078125
- up_weight: bfloat16 [8, 9216, 6144], P('exp', 'seq'), may hold values from -0.078125 to 0.078125
Outputs:
- residual_out: bfloat16 [2048, 6144], P('exp', 'seq')
- expert_hidden: bfloat16 [8, 9216, 1024], P('exp', 'seq')
Inputs may be any that keep to these rules, and one draw needn't show every extreme that they name: `routes`: each token names 2 different experts; within one source group of 256 tokens no expert is named more than 128 times. `log_decay`: every entry is negative.
All inputs are finite; a program needn't handle non-finite values.
Results may differ from a plain program's by a relative error of at most 0.0065.
Values may be sent and summed in bfloat16 or wider, within the bound.
No kernel may reach another device: no remote copies, remote signals or barrier semaphores. Data moves between devices by JAX's collectives and lax.ppermute only.
A program may use at most 128 MiB of HBM per device.

v0:
```python
import jax
import jax.numpy as jnp
from jax import lax
from jax.sharding import Mesh
from jax.sharding import PartitionSpec as P

D = 6144
HEAD_DIM = 128
SEQ = ("seq_0", "seq_1", "seq_2")


precise = lax.Precision.HIGHEST
contract_last = (((1,), (1,)), ((), ()))


def nothing_yet(shard, identity):
    return jax.tree.map(
        lambda a, e: jnp.broadcast_to(jnp.asarray(e, a.dtype), a.shape), shard, identity
    )


def carried_in(shard, axes, combine, identity):
    before = start = nothing_yet(shard, identity)
    so_far = shard
    for axis in reversed(axes):
        peers, place = (lax.axis_size(axis), lax.axis_index(axis))
        pieces = jax.tree.map(lambda part: lax.all_gather(part, axis), so_far)
        inside, so_far = (start, start)
        for k in range(peers):
            passed = k < place
            so_far = combine(so_far, jax.tree.map(lambda part: part[k], pieces))
            inside = jax.tree.map(lambda new, old: jnp.where(passed, new, old), so_far, inside)
        before = combine(inside, before)
    return before


def link_states(earlier, later):
    return (earlier[0] * later[0], later[0][:, None, None] * earlier[1] + later[1])


def finish_rows(gate_sum, up_sum, squares):
    inv_rms = lax.rsqrt(squares / D + 1e-06)[None, :]
    return (jax.nn.silu(gate_sum * inv_rms) * (up_sum * inv_rms)).astype(jnp.bfloat16)


def body(
    query_rows,
    key_rows,
    value_rows,
    log_decay,
    out_weight,
    residual,
    routes,
    gate_weight,
    up_weight,
):
    positions, head_cols = query_rows.shape
    heads_here = head_cols // HEAD_DIM
    queries = query_rows.astype(jnp.float32).reshape(positions, heads_here, HEAD_DIM)
    keys_here = key_rows.astype(jnp.float32).reshape(positions, heads_here, HEAD_DIM)
    values_here = value_rows.astype(jnp.float32).reshape(positions, heads_here, HEAD_DIM)
    cumulative = jnp.cumsum(log_decay, axis=0)
    closing = cumulative[-1]
    key_scaled = keys_here * jnp.exp(closing[None, :] - cumulative)[:, :, None]
    local_state = jnp.einsum("shd,she->hde", key_scaled, values_here, precision=precise)
    identity = (
        jnp.ones((heads_here,), jnp.float32),
        jnp.zeros((heads_here, HEAD_DIM, HEAD_DIM), jnp.float32),
    )
    entering = carried_in((jnp.exp(closing), local_state), SEQ, link_states, identity)[1]
    later = lax.broadcasted_iota(jnp.int32, (positions, positions), 0)
    earlier = lax.broadcasted_iota(jnp.int32, (positions, positions), 1)
    causal = (later >= earlier)[None]
    carried = jnp.einsum(
        "thd,hde->the", queries * jnp.exp(cumulative)[:, :, None], entering, precision=precise
    )
    scores = jnp.einsum("thd,shd->hts", queries, keys_here, precision=precise)
    spread = cumulative.T[:, :, None] - cumulative.T[:, None, :]
    weights = jnp.where(causal, jnp.exp(jnp.where(causal, spread, 0.0)), 0.0)
    within = jnp.einsum("hts,she->the", scores * weights, values_here, precision=precise)
    head_raw = carried + within
    normed = head_raw * lax.rsqrt(jnp.mean(head_raw * head_raw, axis=-1, keepdims=True) + 1e-06)
    normed = normed.astype(jnp.bfloat16).reshape(positions, head_cols)
    gathered = lax.all_gather(normed, SEQ, axis=0, tiled=True)
    row_block = gathered
    attended = lax.psum_scatter(
        jnp.dot(row_block, out_weight, preferred_element_type=jnp.float32),
        "exp",
        scatter_dimension=0,
        tiled=True,
    )
    residual_out = (residual.astype(jnp.float32) + attended).astype(jnp.bfloat16)
    group_rows = routes.shape[0]
    choices_each = routes.shape[1]
    experts = lax.axis_size("exp")
    capacity = 4 * group_rows // experts
    route_flat = routes.reshape(-1)
    expert_ids = lax.broadcasted_iota(jnp.int32, (1, experts), 1)
    onehot = (route_flat[:, None] == expert_ids).astype(jnp.int32)
    slot_index = jnp.sum(jnp.cumsum(onehot, axis=0) * onehot, axis=1) - 1
    target = route_flat * capacity + slot_index
    w_gate = gate_weight[0]
    w_up = up_weight[0]
    hidden_rows = w_gate.shape[0]
    columns = residual_out.shape[1]
    buffer = jnp.zeros((experts * capacity, columns), jnp.bfloat16)
    buffer = buffer.at[target].set(jnp.repeat(residual_out, choices_each, axis=0))
    received = lax.all_to_all(
        buffer.reshape(experts, capacity, columns), "exp", split_axis=0, concat_axis=0, tiled=True
    )
    sources, entries, gathered_columns = received.shape
    slices = received.reshape(sources * entries, gathered_columns)
    row_block = lax.all_gather(slices, SEQ, axis=1, tiled=True)
    squares = jnp.einsum("rd,rd->r", row_block, row_block, preferred_element_type=jnp.float32)
    gate_sum = lax.dot_general(w_gate, row_block, contract_last, preferred_element_type=jnp.float32)
    up_sum = lax.dot_general(w_up, row_block, contract_last, preferred_element_type=jnp.float32)
    expert_hidden = finish_rows(gate_sum, up_sum, squares).reshape(hidden_rows, sources, entries)
    return (residual_out, expert_hidden.reshape(1, hidden_rows, experts * capacity))


def solution(mesh):
    torus = Mesh(
        mesh.devices.reshape(4, 4, 2, mesh.shape["exp"]), ("seq_0", "seq_1", "seq_2", "exp")
    )
    in_specs = (
        P(SEQ, "exp"),
        P(SEQ, "exp"),
        P(SEQ, "exp"),
        P(SEQ, "exp"),
        P("exp", SEQ),
        P("exp", SEQ),
        P("exp", None),
        P("exp", SEQ, None),
        P("exp", SEQ, None),
    )
    out_specs = (P("exp", SEQ), P("exp", SEQ, None))
    return jax.shard_map(body, mesh=torus, in_specs=in_specs, out_specs=out_specs, check_vma=False)
```

profile of v0, /device:TPU:1, one launch (start us, length us, event | category | flops | bytes accessed | tf_op | source)
XLA Modules:
  0.0 330.9 jit_solution(14114407358231520590)
XLA Ops:
  7.2 1.5 copy.69
  8.8 1.4 reduce_window_sum.26
  10.2 0.7 exponential_bitcast_fusion
  10.9 1.4 fusion.116
  12.3 0.8 copy.71
  13.1 2.4 fusion.78
  15.6 4.7 %all-gather.1 = f32[2,1,8]{2,1,0:T(1,128)S(1)} all-gather(f32[1,1,8]{2,1,0:T(1,128)S(1)} %get-tuple-element.6), channel_id=1, replica_groups=mesh['seq_0'=4,'seq_1'=4,'seq_2'=2,'exp'=8] {'seq_2'}, dimensions={0}, use_global_device_ids=true | all-gather | bytes 96 | tf_op jit(solution)/shard_map/all_gather | solution.py:27
  20.9 6.2 %all-gather.2 = f32[4,1,8]{2,1,0:T(1,128)S(1)} all-gather(f32[1,1,8]{2,1,0:T(1,128)S(1)} %get-tuple-element.18), channel_id=1, replica_groups=mesh['seq_0'=4,'seq_1'=4,'seq_2'=2,'exp'=8] {'seq_1'}, dimensions={0}, use_global_device_ids=true | all-gather | bytes 160 | tf_op jit(solution)/shard_map/all_gather | solution.py:27
  27.7 7.0 %all-gather.18.cloned.1.call-done = f32[16,128,128]{2,1,0:T(8,128)} async-done(((f32[8,128,128]{2,1,0:T(8,128)}), f32[16,128,128]{2,1,0:T(8,128)}) %all-gather.18.cloned.1.call-update) | async-done | bytes 1048592 | tf_op jit(solution)/shard_map/all_gather | solution.py:27
  34.6 2.1 bitcast_add_fusion.4
  37.4 33.6 %all-gather.10.cloned.1.call-done = f32[4,8,128,128]{3,2,1,0:T(8,128)} async-done(((f32[1,8,128,128]{3,2,1,0:T(8,128)}), f32[4,8,128,128]{3,2,1,0:T(8,128)}) %all-gather.10.cloned.1.call-update) | async-done | bytes 2097168 | tf_op jit(solution)/shard_map/all_gather | solution.py:27
  71.0 2.5 multiply_add_fusion
  73.6 7.7 %all-gather.3 = f32[4,1,8]{2,1,0:T(1,128)S(1)} all-gather(f32[1,1,8]{2,1,0:T(1,128)} %get-tuple-element.12), channel_id=1, replica_groups=mesh['seq_0'=4,'seq_1'=4,'seq_2'=2,'exp'=8] {'seq_0'}, dimensions={0}, use_global_device_ids=true | all-gather | bytes 160 | tf_op jit(solution)/shard_map/all_gather | solution.py:27
  81.3 0.8 copy.77
  82.1 0.8 copy.74
  83.6 1.9 convolution_multiply_fusion
  85.4 21.7 %all-gather.12.cloned.1.call-done = f32[4,8,128,128]{3,2,1,0:T(8,128)} async-done(((f32[1,8,128,128]{3,2,1,0:T(8,128)}), f32[4,8,128,128]{3,2,1,0:T(8,128)}) %all-gather.12.cloned.1.call-update) | async-done | bytes 2097168 | tf_op jit(solution)/shard_map/all_gather | solution.py:27
  107.1 3.8 %convolution_bitcast_fusion.1 = f32[64,8,128]{2,0,1:T(8,128)S(1)} fusion(f32[4,8,128,128]{3,2,1,0:T(8,128)} %all-gather.12.cloned.1.call-done, f32[4,8,128,128]{3,2,1,0:T(8,128)} %all-gather.10.cloned.1.call-done, f32[16,128,128]{2,1,0:T(8,128)} %all-gather.18.cloned.1.call-done, f32[8]{0:T(128)} %copy-done.5, f32[8]{0:T(128)} %get-tuple-element.19, ...), kind=kOutput, calls=%fused_computation.17 | convolution fusion | flops 104857600 | bytes 5638538 | tf_op jit(solution)/shard_map/thd,hde->the/dot_general | solution.py:74
  111.3 0.8 copy_bitcast_fusion.1
  112.2 51.7 %all-gather.14.cloned.1.call-done = bf16[2048,1024]{1,0:T(8,128)(2,1)} async-done(((bf16[64,1024]{1,0:T(8,128)(2,1)}), bf16[2048,1024]{1,0:T(8,128)(2,1)}) %all-gather.14.cloned.1.call-update) | async-done | bytes 4194320 | tf_op jit(solution)/shard_map/all_gather | solution.py:84
  163.9 5.0 %fusion.117 = f32[2048,192]{0,1:T(8,128)} fusion(bf16[2048,1024]{1,0:T(8,128)(2,1)} %all-gather.14.cloned.1.call-done, bf16[1024,192]{0,1:T(8,128)(2,1)} %param.13), kind=kOutput, calls=%fused_computation.152 | convolution fusion | flops 805306368 | bytes 6160384 | tf_op jit(solution)/shard_map/dot_general | solution.py:87
  168.9 0.8 copy.82
  169.7 1.0 eq.29
  170.7 1.6 eq.25
  172.4 0.8 copy.81
  173.2 1.6 mul.315
  174.8 0.6 fusion.112
  175.4 2.2 reduce-window.6
  177.6 0.8 slice_reduce_fusion
  178.4 1.3 reduce-window.9
  179.7 0.7 slice.91
  180.4 0.8 fusion.111
  181.2 0.7 compare_select_fusion
  181.9 22.6 %reduce-scatter.2.cloned.1.call-done = f32[256,192]{0,1:T(8,128)} async-done(((f32[2048,192]{0,1:T(8,128)}), f32[256,192]{0,1:T(8,128)}) %reduce-scatter.2.cloned.1.call-update) | async-done | bytes 196624 | tf_op jit(solution)/shard_map/reduce_scatter | solution.py:86
  204.5 1.6 add_convert_fusion
  206.1 1.6 copy.84
  207.8 1.7 broadcast_in_dim.47
  209.5 1.9 reshape.195
  211.4 3.5 %scatter_custom_fusion = bf16[1024,192]{1,0:T(8,128)(2,1)} fusion(s32[512]{0:T(512)S(1)} %bitcast.217, bf16[512,192]{1,0:T(8,128)(2,1)} %reshape.195, bf16[]{:T(256)} %constant.51.clone.1), kind=kCustom, calls=%fused_computation.64 | custom fusion | bytes 393728 | tf_op jit(solution)/shard_map/scatter | solution.py:107
  214.9 2.0 copy.86
  216.9 15.8 %all_to_all.5 = bf16[8,128,192]{1,2,0:T(8,128)(2,1)S(1)} all-to-all(bf16[8,128,192]{1,2,0:T(8,128)(2,1)} %copy.86), channel_id=1, replica_groups=mesh['seq_0'=4,'seq_1'=4,'seq_2'=2,'exp'=8] {'exp'}, dimensions={0} | all-to-all | bytes 786432 | tf_op jit(solution)/shard_map/all_to_all | solution.py:108
  232.7 0.8 copy_bitcast_fusion
  233.5 69.3 %all-gather.16.cloned.1.call-done = bf16[1024,6144]{0,1:T(8,128)(2,1)} async-done(((bf16[1024,192]{0,1:T(8,128)(2,1)}), bf16[1024,6144]{0,1:T(8,128)(2,1)}) %all-gather.16.cloned.1.call-update) | async-done | bytes 12582928 | tf_op jit(solution)/shard_map/all_gather | solution.py:113
  302.8 7.1 %fusion = f32[1024]{0:T(1024)S(1)} fusion(bf16[1024,6144]{0,1:T(8,128)(2,1)} %all-gather.16.cloned.1.call-done), kind=kLoop, calls=%fused_computation.2 | loop fusion | flops 18873344 | bytes 12587008 | tf_op jit(solution)/shard_map/rd,rd->r/dot_general | solution.py:114
  310.0 7.0 %fusion.17 = f32[288,1024]{1,0:T(8,128)S(1)} fusion(bf16[1024,6144]{0,1:T(8,128)(2,1)} %all-gather.16.cloned.1.call-done, bf16[1,288,6144]{2,1,0:T(8,128)(2,1)S(1)} %copy-done, f32[1024]{0:T(1024)S(1)} %add_rsqrt_fusion), kind=kOutput, calls=%fused_computation.11 | convolution fusion | flops 3624173568 | bytes 17305600 | tf_op jit(solution)/shard_map/dot_general | solution.py:115
  316.9 1.2 copy-done.1
  318.1 1.0 copy-done.7
  319.1 4.9 %fusion.23 = bf16[1,288,1024]{2,1,0:T(8,128)(2,1)} fusion(bf16[1024,6144]{0,1:T(8,128)(2,1)S(1)} %copy-done.1, bf16[1,288,6144]{2,1,0:T(8,128)(2,1)S(1)} %copy-done.7, f32[288,1024]{1,0:T(8,128)S(1)} %fusion.17, f32[1024]{0:T(1024)S(1)} %add_rsqrt_fusion), kind=kOutput, calls=%fused_computation.13 | convolution fusion | flops 3625943040 | bytes 17895424 | tf_op jit(solution)/shard_map/dot_general | solution.py:116
  (36 shorter events, 3.2 us)
Async XLA Ops:
  7.2 302.8 %copy-start = (bf16[1,288,6144]{2,1,0:T(8,128)(2,1)S(1)}, bf16[1,288,6144]{2,1,0:T(8,128)(2,1)}, u32[]{:S(2)}) copy-start(bf16[1,288,6144]{2,1,0:T(8,128)(2,1)} %param.16) | copy-start | bytes 10616836
  7.2 27.4 %all-gather.18.cloned.1.call-start = ((), (), s32[]{:S(2)}) async-start(), calls=%async_computation.7 | async-start | bytes 1572864 | tf_op jit(solution)/shard_map/all_gather | solution.py:27
  15.6 55.4 %all-gather.10.cloned.1.call-start = ((), (), s32[]{:S(2)}) async-start(), calls=%async_computation.2 | async-start | bytes 2621440 | tf_op jit(solution)/shard_map/all_gather | solution.py:27
  27.7 45.9 %copy-start.5 = (f32[8]{0:T(128)}, f32[8]{0:T(128)S(1)}, u32[]{:S(2)}) copy-start(f32[8]{0:T(128)S(1)} %get-tuple-element.17) | copy-start | bytes 100
  36.8 70.4 %all-gather.12.cloned.1.call-start = ((), (), s32[]{:S(2)}) async-start(), calls=%async_computation.3 | async-start | bytes 2621440 | tf_op jit(solution)/shard_map/all_gather | solution.py:27
  37.4 44.7 %copy-start.6 = (f32[8]{0:T(128)}, f32[8]{0:T(128)S(1)}, u32[]{:S(2)}) copy-start(f32[8]{0:T(128)S(1)} %get-tuple-element.13) | copy-start | bytes 100
  73.6 90.3 %all-gather.14.cloned.1.call-start = ((), (), s32[]{:S(2)}) async-start(), calls=%async_computation.4 | async-start | bytes 4325376 | tf_op jit(solution)/shard_map/all_gather | solution.py:84
  107.1 3.8 %copy-start.2 = (bf16[64,1024]{1,0:T(8,128)(2,1)S(1)}, bf16[64,1024]{1,0:T(8,128)(2,1)}, u32[]{:S(2)}) copy-start(bf16[64,1024]{1,0:T(8,128)(2,1)} %param.11) | copy-start | bytes 393220
  107.1 3.8 %copy-start.3 = (f32[8,64,64]{2,1,0:T(8,128)S(1)}, f32[8,64,64]{2,1,0:T(8,128)}, u32[]{:S(2)}) copy-start(f32[8,64,64]{2,1,0:T(8,128)} %convolution_multiply_fusion) | copy-start | bytes 393220
  112.1 56.8 %copy-start.4 = (s32[256,2]{0,1:T(2,128)S(1)}, s32[256,2]{0,1:T(2,128)}, u32[]{:S(2)}) copy-start(s32[256,2]{0,1:T(2,128)} %param.15) | copy-start | bytes 6148
  112.1 92.3 %reduce-scatter.2.cloned.1.call-start = ((), (), s32[]{:S(2)}) async-start(), calls=%async_computation.5 | async-start | bytes 1769472 | tf_op jit(solution)/shard_map/reduce_scatter | solution.py:86
  168.8 134.0 %all-gather.16.cloned.1.call-start = ((), (), s32[]{:S(2)}) async-start(), calls=%async_computation.6 | async-start | bytes 12976128 | tf_op jit(solution)/shard_map/all_gather | solution.py:113
  309.9 8.2 %copy-start.1 = (bf16[1024,6144]{0,1:T(8,128)(2,1)S(1)}, bf16[1024,6144]{0,1:T(8,128)(2,1)}, u32[]{:S(2)}) copy-start(bf16[1024,6144]{0,1:T(8,128)(2,1)} %all-gather.16.cloned.1.call-done) | copy-start | bytes 37748740
  309.9 9.2 %copy-start.7 = (bf16[1,288,6144]{2,1,0:T(8,128)(2,1)S(1)}, bf16[1,288,6144]{2,1,0:T(8,128)(2,1)}, u32[]{:S(2)}) copy-start(bf16[1,288,6144]{2,1,0:T(8,128)(2,1)} %param.17) | copy-start | bytes 10616836
Sparse Core Ops, SparseCore 0:
  15.7 18.8 all-gather.17
  37.0 33.9 all-gather.9
  73.7 33.3 all-gather.11
  112.3 51.5 all-gather.13
  169.0 35.4 reduce-scatter.1
  233.6 69.1 all-gather.15
where the time goes:
time: 332 us; the launch traced here: 331 us
  waiting for transfers between devices  206 us (62%)
  blocking collectives  34.3 us (10%)
  local copies, waits for them, and re-layouts  25.9 us (8%)
  matrix products  25.3 us (8%)
  other arithmetic  25 us (8%)
  between operations  14.2 us (4%)
    all_gather x1, waiting for transfers between devices, body(): row_block = lax.all_gather(slices, SEQ, axis=1, tiled=True)  69.3 us
    all_gather x3, waiting for transfers between devices, carried_in(): pieces = jax.tree.map(lambda part: lax.all_gather(part, axis), so_far)  62.2 us
    all_gather x1, waiting for transfers between devices, body(): gathered = lax.all_gather(normed, SEQ, axis=0, tiled=True)  51.7 us
    reduce_scatter x1, waiting for transfers between devices, body(): lax.psum_scatter(jnp.dot(row_block, out_weight, preferred_element_type=jn...  22.6 us
    all_gather x3, blocking collectives, carried_in(): pieces = jax.tree.map(lambda part: lax.all_gather(part, axis), so_far)  18.5 us
    all_to_all x1, blocking collectives, body(): lax.all_to_all(buffer.reshape(experts, capacity, columns), 'exp', split_a...  15.8 us
    dot_general x1, other arithmetic, body(): jnp.einsum('rd,rd->r', row_block, row_block, preferred_element_type=jnp.f...  7.08 us
    dot_general x1, matrix products, body(): lax.dot_general(w_gate, row_block, contract_last, preferred_element_type=...  6.96 us
  transfers between devices with their start and end apart: 6, of which 6 were waited for; matrix products, arithmetic and copies ran while one was open for 6% of the time, Pallas kernels for 0%

commit v1 on v0

--- a/solution.py
+++ b/solution.py
@@ -38,6 +38,51 @@
     return (earlier[0] * later[0], later[0][:, None, None] * earlier[1] + later[1])
 
 
+def swap_cores(tree):
+    return jax.tree.map(lambda part: lax.ppermute(part, "seq_2", [(0, 1), (1, 0)]), tree)
+
+
+def prefix_over(own, axis):
+    peers, place = (lax.axis_size(axis), lax.axis_index(axis))
+    shifted = [own] + [
+        jax.tree.map(
+            lambda part: lax.ppermute(part, axis, [(i, (i + d) % peers) for i in range(peers)]), own
+        )
+        for d in range(1, peers)
+    ]
+    start = nothing_yet(own, (1.0, 0.0))
+    before, total = (start, start)
+    for k in range(peers):
+        lag = (place - k) % peers
+        piece = jax.tree.map(
+            lambda *opts: jnp.select([lag == d for d in range(peers)], opts), *shifted
+        )
+        total = link_states(total, piece)
+        passed = k < place
+        before = jax.tree.map(lambda new, old: jnp.where(passed, new, old), total, before)
+    return before, total
+
+
+def entering_state(decay, state):
+    core = lax.axis_index("seq_2")
+    other = swap_cores((decay, state))
+    first = jax.tree.map(lambda mine, theirs: jnp.where(core == 0, mine, theirs), (decay, state), other)
+    second = jax.tree.map(lambda mine, theirs: jnp.where(core == 0, theirs, mine), (decay, state), other)
+    chip = link_states(first, second)
+    half = decay.shape[0] // 2
+    mine = jax.tree.map(lambda part: lax.dynamic_slice_in_dim(part, core * half, half, 0), chip)
+    along_y, row = prefix_over(mine, "seq_1")
+    along_x, _ = prefix_over(row, "seq_0")
+    chip_before = link_states(along_x, along_y)
+    theirs = swap_cores(chip_before)
+    whole = jax.tree.map(
+        lambda a, b: jnp.where(core == 0, jnp.concatenate([a, b], 0), jnp.concatenate([b, a], 0)),
+        chip_before,
+        theirs,
+    )
+    return jnp.where(core == 0, whole[1], first[0][:, None, None] * whole[1] + first[1])
+
+
 def finish_rows(gate_sum, up_sum, squares):
     inv_rms = lax.rsqrt(squares / D + 1e-06)[None, :]
     return (jax.nn.silu(gate_sum * inv_rms) * (up_sum * inv_rms)).astype(jnp.bfloat16)
@@ -63,11 +108,7 @@
     closing = cumulative[-1]
     key_scaled = keys_here * jnp.exp(closing[None, :] - cumulative)[:, :, None]
     local_state = jnp.einsum("shd,she->hde", key_scaled, values_here, precision=precise)
-    identity = (
-        jnp.ones((heads_here,), jnp.float32),
-        jnp.zeros((heads_here, HEAD_DIM, HEAD_DIM), jnp.float32),
-    )
-    entering = carried_in((jnp.exp(closing), local_state), SEQ, link_states, identity)[1]
+    entering = entering_state(jnp.exp(closing), local_state)
     later = lax.broadcasted_iota(jnp.int32, (positions, positions), 0)
     earlier = lax.broadcasted_iota(jnp.int32, (positions, positions), 1)
     causal = (later >= earlier)[None]

time: 332 us -> 313 us (0.943)
  waiting for transfers between devices: 206 us -> 163 us
  between operations: 14.2 us -> 33.7 us
  starting transfers between devices: 0.25 us -> 19.1 us
  blocking collectives: 34.3 us -> 15.8 us
  other arithmetic: 25 us -> 28.5 us
    all_gather x3 -> x0, waiting for transfers between devices: 62.2 us -> none  [carried_in(): pieces = jax.tree.map(lambda part: lax.all_gather(part, axis), so_far)]
    ppermute x0 -> x15, waiting for transfers between devices: none -> 19.6 us  [the longest x12 19.6 us: prefix_over(): lax.ppermute(part, axis, [(i, (i + d) % peers) for i in range(peers)])]
    ppermute x0 -> x15, starting transfers between devices: none -> 19 us  [the longest x12 15.2 us: prefix_over(): lax.ppermute(part, axis, [(i, (i + d) % peers) for i in range(peers)])]
    all_gather x3 -> x0, blocking collectives: 18.5 us -> none  [carried_in(): pieces = jax.tree.map(lambda part: lax.all_gather(part, axis), so_far)]
    another operation x2 -> x10, other arithmetic: 3.5 us -> 9.16 us  [the longest x8 5.66 us: prefix_over(): jnp.select([lag == d for d in range(peers)], opts)]
  transfers between devices with their start and end apart: 6 -> 18, of which waited for: 6 -> 8; matrix products, arithmetic and copies ran while one was open for 6% -> 10% of each run, Pallas kernels for 0% -> 0%
where the time goes in v1:
time: 313 us; the launch traced here: 311 us
  waiting for transfers between devices  163 us (52%)
  between operations  33.7 us (11%)
  other arithmetic  28.5 us (9%)
  local copies, waits for them, and re-layouts  27.5 us (9%)
  matrix products  23.6 us (8%)
  starting transfers between devices  19.1 us (6%)
  blocking collectives  15.8 us (5%)
    all_gather x1, waiting for transfers between devices, body(): row_block = lax.all_gather(slices, SEQ, axis=1, tiled=True)  69.3 us
    all_gather x1, waiting for transfers between devices, body(): gathered = lax.all_gather(normed, SEQ, axis=0, tiled=True)  51.6 us
    reduce_scatter x1, waiting for transfers between devices, body(): lax.psum_scatter(jnp.dot(row_block, out_weight, preferred_element_type=jn...  22.7 us
    ppermute x12, waiting for transfers between devices, prefix_over(): lax.ppermute(part, axis, [(i, (i + d) % peers) for i in range(peers)])  19.6 us
    all_to_all x1, blocking collectives, body(): lax.all_to_all(buffer.reshape(experts, capacity, columns), 'exp', split_a...  15.8 us
    ppermute x12, starting transfers between devices, prefix_over(): lax.ppermute(part, axis, [(i, (i + d) % peers) for i in range(peers)])  15.2 us
    dot_general x1, other arithmetic, body(): jnp.einsum('rd,rd->r', row_block, row_block, preferred_element_type=jnp.f...  7.08 us
    dot_general x1, matrix products, body(): lax.dot_general(w_gate, row_block, contract_last, preferred_element_type=...  6.96 us
  transfers between devices with their start and end apart: 18, of which 8 were waited for; matrix products, arithmetic and copies ran while one was open for 10% of the time, Pallas kernels for 0%

profile of v1, /device:TPU:1, one launch (start us, length us, event | category | flops | bytes accessed | tf_op | source)
XLA Modules:
  0.0 311.5 jit_solution(16042389560862939219)
XLA Ops:
  7.2 1.5 copy.69
  8.8 1.4 reduce_window_sum.26
  10.9 3.2 %collective-permute-start = (f32[8]{0:T(128)S(1)}, f32[8]{0:T(128)S(1)}, u32[]{:S(2)}, u32[]{:S(2)}) collective-permute-start(f32[8]{0:T(128)S(1)} %fusion.59), channel_id=1, source_target_pairs={{0,8},{8,0},{1,9},{9,1},{2,10},{10,2},{3,11},{11,3},{4,12},{12,4},... | collective-permute-start | bytes 104 | tf_op jit(solution)/shard_map/ppermute | solution.py:42
  14.8 1.4 fusion.61
  16.2 0.8 copy.71
  17.0 2.4 fusion.36
  45.7 0.8 copy.77
  47.4 1.2 collective-permute-start.2
  49.0 2.3 collective-permute-start.3
  51.4 1.1 broadcast_select_fusion
  52.5 1.3 fusion.30
  53.9 1.0 collective-permute-start.9
  55.4 2.5 collective-permute-start.6
  58.5 1.9 collective-permute-done.10
  60.3 1.2 collective-permute-start.4
  62.0 7.3 %collective-permute-done.8 = f32[4,128,128]{2,1,0:T(8,128)S(1)} collective-permute-done((f32[4,128,128]{2,1,0:T(8,128)S(1)}, f32[4,128,128]{2,1,0:T(8,128)S(1)}, u32[]{:S(2)}, u32[]{:S(2)}) %collective-permute-start.8) | collective-permute-done | bytes 262176 | tf_op jit(solution)/shard_map/ppermute | solution.py:49
  69.6 2.8 collective-permute-start.12
  72.8 2.4 collective-permute-start.13
  75.2 3.5 %collective-permute-done.12 = f32[4,128,128]{2,1,0:T(8,128)S(1)} collective-permute-done((f32[4,128,128]{2,1,0:T(8,128)S(1)}, f32[4,128,128]{2,1,0:T(8,128)S(1)}, u32[]{:S(2)}, u32[]{:S(2)}) %collective-permute-start.12) | collective-permute-done | bytes 262176 | tf_op jit(solution)/shard_map/ppermute | solution.py:49
  78.6 6.4 %collective-permute-done.11 = f32[4,128,128]{2,1,0:T(8,128)S(1)} collective-permute-done((f32[4,128,128]{2,1,0:T(8,128)S(1)}, f32[4,128,128]{2,1,0:T(8,128)S(1)}, u32[]{:S(2)}, u32[]{:S(2)}) %collective-permute-start.11) | collective-permute-done | bytes 262176 | tf_op jit(solution)/shard_map/ppermute | solution.py:49
  85.0 1.4 select_add_fusion
  87.1 0.9 convolution_multiply_fusion
  88.0 0.8 copy.74
  88.8 1.2 convolution_bitcast_fusion
  90.1 2.2 multiply_reduce_fusion
  93.2 51.6 %all-gather.3.cloned.1.call-done = bf16[2048,1024]{1,0:T(8,128)(2,1)} async-done(((bf16[64,1024]{1,0:T(8,128)(2,1)}), bf16[2048,1024]{1,0:T(8,128)(2,1)}) %all-gather.3.cloned.1.call-update) | async-done | bytes 4194320 | tf_op jit(solution)/shard_map/all_gather | solution.py:125
  144.8 5.0 %fusion.62 = f32[2048,192]{0,1:T(8,128)} fusion(bf16[2048,1024]{1,0:T(8,128)(2,1)} %all-gather.3.cloned.1.call-done, bf16[1024,192]{0,1:T(8,128)(2,1)} %param.13), kind=kOutput, calls=%fused_computation.128 | convolution fusion | flops 805306368 | bytes 6160384 | tf_op jit(solution)/shard_map/dot_general | solution.py:128
  150.7 1.0 eq.216
  151.7 1.6 eq.212
  153.3 0.8 copy.81
  154.1 1.6 mul.219
  156.3 2.2 reduce-window.6
  159.4 1.3 reduce-window.9
  162.8 22.7 %reduce-scatter.2.cloned.1.call-done = f32[256,192]{0,1:T(8,128)} async-done(((f32[2048,192]{0,1:T(8,128)}), f32[256,192]{0,1:T(8,128)}) %reduce-scatter.2.cloned.1.call-update) | async-done | bytes 196624 | tf_op jit(solution)/shard_map/reduce_scatter | solution.py:127
  185.4 1.6 add_convert_fusion
  187.1 1.6 copy.84
  188.7 1.7 broadcast_in_dim.122
  190.5 1.9 reshape.145
  192.3 3.5 %scatter_custom_fusion = bf16[1024,192]{1,0:T(8,128)(2,1)} fusion(s32[512]{0:T(512)S(1)} %bitcast.151, bf16[512,192]{1,0:T(8,128)(2,1)} %reshape.145, bf16[]{:T(256)} %constant.147.clone.1), kind=kCustom, calls=%fused_computation.26 | custom fusion | bytes 393728 | tf_op jit(solution)/shard_map/scatter | solution.py:148
  195.9 2.0 copy.86
  197.9 15.8 %all_to_all.5 = bf16[8,128,192]{1,2,0:T(8,128)(2,1)S(1)} all-to-all(bf16[8,128,192]{1,2,0:T(8,128)(2,1)} %copy.86), channel_id=1, replica_groups=mesh['seq_0'=4,'seq_1'=4,'seq_2'=2,'exp'=8] {'exp'}, dimensions={0} | all-to-all | bytes 786432 | tf_op jit(solution)/shard_map/all_to_all | solution.py:149
  213.6 0.8 copy_bitcast_fusion
  214.5 69.3 %all-gather.5.cloned.1.call-done = bf16[1024,6144]{0,1:T(8,128)(2,1)} async-done(((bf16[1024,192]{0,1:T(8,128)(2,1)}), bf16[1024,6144]{0,1:T(8,128)(2,1)}) %all-gather.5.cloned.1.call-update) | async-done | bytes 12582928 | tf_op jit(solution)/shard_map/all_gather | solution.py:154
  283.8 7.1 %fusion = f32[1024]{0:T(1024)S(1)} fusion(bf16[1024,6144]{0,1:T(8,128)(2,1)} %all-gather.5.cloned.1.call-done), kind=kLoop, calls=%fused_computation.2 | loop fusion | flops 18873344 | bytes 12587008 | tf_op jit(solution)/shard_map/rd,rd->r/dot_general | solution.py:155
  290.9 7.0 %fusion.17 = f32[288,1024]{1,0:T(8,128)S(1)} fusion(bf16[1024,6144]{0,1:T(8,128)(2,1)} %all-gather.5.cloned.1.call-done, bf16[1,288,6144]{2,1,0:T(8,128)(2,1)S(1)} %copy-done, f32[1024]{0:T(1024)S(1)} %add_rsqrt_fusion), kind=kOutput, calls=%fused_computation.11 | convolution fusion | flops 3624173568 | bytes 17305600 | tf_op jit(solution)/shard_map/dot_general | solution.py:156
  297.9 1.2 copy-done.1
  299.0 1.0 copy-done.5
  300.1 4.9 %fusion.23 = bf16[1,288,1024]{2,1,0:T(8,128)(2,1)} fusion(bf16[1024,6144]{0,1:T(8,128)(2,1)S(1)} %copy-done.1, bf16[1,288,6144]{2,1,0:T(8,128)(2,1)S(1)} %copy-done.5, f32[288,1024]{1,0:T(8,128)S(1)} %fusion.17, f32[1024]{0:T(1024)S(1)} %add_rsqrt_fusion), kind=kOutput, calls=%fused_computation.13 | convolution fusion | flops 3625943040 | bytes 17895424 | tf_op jit(solution)/shard_map/dot_general | solution.py:157
  (74 shorter events, 17.4 us)
Async XLA Ops:
  7.2 283.7 %copy-start = (bf16[1,288,6144]{2,1,0:T(8,128)(2,1)S(1)}, bf16[1,288,6144]{2,1,0:T(8,128)(2,1)}, u32[]{:S(2)}) copy-start(bf16[1,288,6144]{2,1,0:T(8,128)(2,1)} %param.16) | copy-start | bytes 10616836
  7.2 137.6 %all-gather.3.cloned.1.call-start = ((), (), s32[]{:S(2)}) async-start(), calls=%async_computation.2 | async-start | bytes 4325376 | tf_op jit(solution)/shard_map/all_gather | solution.py:125
  10.9 35.7 %collective-permute-start = (f32[8]{0:T(128)S(1)}, f32[8]{0:T(128)S(1)}, u32[]{:S(2)}, u32[]{:S(2)}) collective-permute-start(f32[8]{0:T(128)S(1)} %fusion.59), channel_id=1, source_target_pairs={{0,8},{8,0},{1,9},{9,1},{2,10},{10,2},{3,11},{11,3},{4,12},{12,4},... | collective-permute-start | bytes 104 | tf_op jit(solution)/shard_map/ppermute | solution.py:42
  19.5 31.9 %collective-permute-start.7 = (f32[8,128,128]{2,1,0:T(8,128)}, f32[8,128,128]{2,1,0:T(8,128)}, u32[]{:S(2)}, u32[]{:S(2)}) collective-permute-start(f32[8,128,128]{2,1,0:T(8,128)} %fusion.36), channel_id=1, source_target_pairs={{0,8},{8,0},{1,9},{9,1},{2,10},{10,2},{3,11},{11,3},{4,12},{12,4},... | collective-permute-start | bytes 1572872 | tf_op jit(solution)/shard_map/ppermute | solution.py:42
  46.6 40.5 %copy-start.3 = (bf16[64,1024]{1,0:T(8,128)(2,1)S(1)}, bf16[64,1024]{1,0:T(8,128)(2,1)}, u32[]{:S(2)}) copy-start(bf16[64,1024]{1,0:T(8,128)(2,1)} %param.10) | copy-start | bytes 393220
  46.6 40.5 %copy-start.6 = (bf16[64,1024]{1,0:T(8,128)(2,1)S(1)}, bf16[64,1024]{1,0:T(8,128)(2,1)}, u32[]{:S(2)}) copy-start(bf16[64,1024]{1,0:T(8,128)(2,1)} %param.9) | copy-start | bytes 393220
  47.4 7.4 %collective-permute-start.2 = (f32[4]{0:T(128)S(1)}, f32[4]{0:T(128)S(1)}, u32[]{:S(2)}, u32[]{:S(2)}) collective-permute-start(f32[4]{0:T(128)S(1)} %dynamic_slice.6), channel_id=1, source_target_pairs={{0,32},{16,48},{32,0},{48,16},{1,33},{17,49},{33,1},{49,17},{2,34}... | collective-permute-start | bytes 56 | tf_op jit(solution)/shard_map/ppermute | solution.py:49
  48.6 6.7 %collective-permute-start.1 = (f32[4]{0:T(128)S(1)}, f32[4]{0:T(128)S(1)}, u32[]{:S(2)}, u32[]{:S(2)}) collective-permute-start(f32[4]{0:T(128)S(1)} %dynamic_slice.6), channel_id=1, source_target_pairs={{0,16},{16,32},{32,48},{48,0},{1,17},{17,33},{33,49},{49,1},{2,18}... | collective-permute-start | bytes 56 | tf_op jit(solution)/shard_map/ppermute | solution.py:49
  49.0 6.3 %collective-permute-start.3 = (f32[4]{0:T(128)S(1)}, f32[4]{0:T(128)S(1)}, u32[]{:S(2)}, u32[]{:S(2)}) collective-permute-start(f32[4]{0:T(128)S(1)} %dynamic_slice.6), channel_id=1, source_target_pairs={{0,48},{16,0},{32,16},{48,32},{1,49},{17,1},{33,17},{49,33},{2,50}... | collective-permute-start | bytes 56 | tf_op jit(solution)/shard_map/ppermute | solution.py:49
  52.5 16.9 %copy-start.2 = (f32[8,128,128]{2,1,0:T(8,128)}, f32[8,128,128]{2,1,0:T(8,128)S(1)}, u32[]{:S(2)}) copy-start(f32[8,128,128]{2,1,0:T(8,128)S(1)} %broadcast_select_fusion) | copy-start | bytes 1572868
  53.8 6.5 %collective-permute-start.10 = (f32[4,128,128]{2,1,0:T(8,128)S(1)}, f32[4,128,128]{2,1,0:T(8,128)S(1)}, u32[]{:S(2)}, u32[]{:S(2)}) collective-permute-start(f32[4,128,128]{2,1,0:T(8,128)S(1)} %fusion.30), channel_id=1, source_target_pairs={{0,48},{16,0},{32,16},{48,32},{1,49},{17,1},{33,17},{49,33},{2,50}... | collective-permute-start | bytes 786440 | tf_op jit(solution)/shard_map/ppermute | solution.py:49
  53.9 8.1 %collective-permute-start.9 = (f32[4,128,128]{2,1,0:T(8,128)S(1)}, f32[4,128,128]{2,1,0:T(8,128)S(1)}, u32[]{:S(2)}, u32[]{:S(2)}) collective-permute-start(f32[4,128,128]{2,1,0:T(8,128)S(1)} %fusion.30), channel_id=1, source_target_pairs={{0,32},{16,48},{32,0},{48,16},{1,33},{17,49},{33,1},{49,17},{2,34}... | collective-permute-start | bytes 786440 | tf_op jit(solution)/shard_map/ppermute | solution.py:49
  54.9 14.5 %collective-permute-start.8 = (f32[4,128,128]{2,1,0:T(8,128)S(1)}, f32[4,128,128]{2,1,0:T(8,128)S(1)}, u32[]{:S(2)}, u32[]{:S(2)}) collective-permute-start(f32[4,128,128]{2,1,0:T(8,128)S(1)} %fusion.30), channel_id=1, source_target_pairs={{0,16},{16,32},{32,48},{48,0},{1,17},{17,33},{33,49},{49,1},{2,18}... | collective-permute-start | bytes 786440 | tf_op jit(solution)/shard_map/ppermute | solution.py:49
  55.4 17.3 %collective-permute-start.6 = (f32[4]{0:T(128)S(1)}, f32[4]{0:T(128)S(1)}, u32[]{:S(2)}, u32[]{:S(2)}) collective-permute-start(f32[4]{0:T(128)S(1)} %get-tuple-element.19), channel_id=1, source_target_pairs={{0,192},{64,0},{128,64},{192,128},{1,193},{65,1},{129,65},{193,129... | collective-permute-start | bytes 56 | tf_op jit(solution)/shard_map/ppermute | solution.py:49
  57.9 17.2 %collective-permute-start.5 = (f32[4]{0:T(128)S(1)}, f32[4]{0:T(128)S(1)}, u32[]{:S(2)}, u32[]{:S(2)}) collective-permute-start(f32[4]{0:T(128)S(1)} %get-tuple-element.19), channel_id=1, source_target_pairs={{0,128},{64,192},{128,0},{192,64},{1,129},{65,193},{129,1},{193,65... | collective-permute-start | bytes 56 | tf_op jit(solution)/shard_map/ppermute | solution.py:49
  60.3 14.8 %collective-permute-start.4 = (f32[4]{0:T(128)S(1)}, f32[4]{0:T(128)S(1)}, u32[]{:S(2)}, u32[]{:S(2)}) collective-permute-start(f32[4]{0:T(128)S(1)} %get-tuple-element.19), channel_id=1, source_target_pairs={{0,64},{64,128},{128,192},{192,0},{1,65},{65,129},{129,193},{193,1... | collective-permute-start | bytes 56 | tf_op jit(solution)/shard_map/ppermute | solution.py:49
  69.6 9.0 %collective-permute-start.12 = (f32[4,128,128]{2,1,0:T(8,128)S(1)}, f32[4,128,128]{2,1,0:T(8,128)S(1)}, u32[]{:S(2)}, u32[]{:S(2)}) collective-permute-start(f32[4,128,128]{2,1,0:T(8,128)S(1)} %select_add_fusion.1), channel_id=1, source_target_pairs={{0,128},{64,192},{128,0},{192,64},{1,129},{65,193},{129,1},{193,65... | collective-permute-start | bytes 786440 | tf_op jit(solution)/shard_map/ppermute | solution.py:49
  72.4 12.6 %collective-permute-start.11 = (f32[4,128,128]{2,1,0:T(8,128)S(1)}, f32[4,128,128]{2,1,0:T(8,128)S(1)}, u32[]{:S(2)}, u32[]{:S(2)}) collective-permute-start(f32[4,128,128]{2,1,0:T(8,128)S(1)} %select_add_fusion.1), channel_id=1, source_target_pairs={{0,64},{64,128},{128,192},{192,0},{1,65},{65,129},{129,193},{193,1... | collective-permute-start | bytes 786440 | tf_op jit(solution)/shard_map/ppermute | solution.py:49
  72.8 12.3 %collective-permute-start.13 = (f32[4,128,128]{2,1,0:T(8,128)S(1)}, f32[4,128,128]{2,1,0:T(8,128)S(1)}, u32[]{:S(2)}, u32[]{:S(2)}) collective-permute-start(f32[4,128,128]{2,1,0:T(8,128)S(1)} %select_add_fusion.1), channel_id=1, source_target_pairs={{0,192},{64,0},{128,64},{192,128},{1,193},{65,1},{129,65},{193,129... | collective-permute-start | bytes 786440 | tf_op jit(solution)/shard_map/ppermute | solution.py:49
  86.5 3.6 %collective-permute-start.14 = (f32[4,128,128]{2,1,0:T(8,128)}, f32[4,128,128]{2,1,0:T(8,128)}, u32[]{:S(2)}, u32[]{:S(2)}) collective-permute-start(f32[4,128,128]{2,1,0:T(8,128)} %select_add_fusion), channel_id=1, source_target_pairs={{0,8},{8,0},{1,9},{9,1},{2,10},{10,2},{3,11},{11,3},{4,12},{12,4},... | collective-permute-start | bytes 786440 | tf_op jit(solution)/shard_map/ppermute | solution.py:42
  93.1 56.7 %copy-start.4 = (s32[256,2]{0,1:T(2,128)S(1)}, s32[256,2]{0,1:T(2,128)}, u32[]{:S(2)}) copy-start(s32[256,2]{0,1:T(2,128)} %param.15) | copy-start | bytes 6148
  93.1 92.3 %reduce-scatter.2.cloned.1.call-start = ((), (), s32[]{:S(2)}) async-start(), calls=%async_computation.3 | async-start | bytes 1769472 | tf_op jit(solution)/shard_map/reduce_scatter | solution.py:127
  149.8 134.0 %all-gather.5.cloned.1.call-start = ((), (), s32[]{:S(2)}) async-start(), calls=%async_computation.4 | async-start | bytes 12976128 | tf_op jit(solution)/shard_map/all_gather | solution.py:154
  290.9 8.2 %copy-start.1 = (bf16[1024,6144]{0,1:T(8,128)(2,1)S(1)}, bf16[1024,6144]{0,1:T(8,128)(2,1)}, u32[]{:S(2)}) copy-start(bf16[1024,6144]{0,1:T(8,128)(2,1)} %all-gather.5.cloned.1.call-done) | copy-start | bytes 37748740
  290.9 9.2 %copy-start.5 = (bf16[1,288,6144]{2,1,0:T(8,128)(2,1)S(1)}, bf16[1,288,6144]{2,1,0:T(8,128)(2,1)}, u32[]{:S(2)}) copy-start(bf16[1,288,6144]{2,1,0:T(8,128)(2,1)} %param.17) | copy-start | bytes 10616836
Sparse Core Ops, SparseCore 0:
  93.2 51.5 all-gather.2
  149.9 35.4 reduce-scatter.1
  214.6 69.1 all-gather.4

commit v2 on v1

--- a/solution.py
+++ b/solution.py
@@ -51,16 +51,16 @@
         for d in range(1, peers)
     ]
     start = nothing_yet(own, (1.0, 0.0))
-    before, total = (start, start)
-    for k in range(peers):
-        lag = (place - k) % peers
-        piece = jax.tree.map(
-            lambda *opts: jnp.select([lag == d for d in range(peers)], opts), *shifted
-        )
-        total = link_states(total, piece)
-        passed = k < place
-        before = jax.tree.map(lambda new, old: jnp.where(passed, new, old), total, before)
-    return before, total
+    before, after = (start, start)
+    for d in range(1, peers):
+        taken = d <= place
+        grown = link_states(shifted[d], before)
+        before = jax.tree.map(lambda new, old: jnp.where(taken, new, old), grown, before)
+    for d in range(peers - 1, 0, -1):
+        taken = d > place
+        grown = link_states(after, shifted[d])
+        after = jax.tree.map(lambda new, old: jnp.where(taken, new, old), grown, after)
+    return before, link_states(link_states(before, own), after)
 
 
 def entering_state(decay, state):
@@ -144,8 +144,14 @@
     w_up = up_weight[0]
     hidden_rows = w_gate.shape[0]
     columns = residual_out.shape[1]
-    buffer = jnp.zeros((experts * capacity, columns), jnp.bfloat16)
-    buffer = buffer.at[target].set(jnp.repeat(residual_out, choices_each, axis=0))
+    slots = lax.broadcasted_iota(jnp.int32, (experts * capacity, 1), 0)
+    placed = target.reshape(group_rows, choices_each)
+    picks = jnp.zeros((experts * capacity, group_rows), jnp.bool_)
+    for j in range(choices_each):
+        picks = picks | (slots == placed[None, :, j])
+    buffer = jnp.dot(
+        picks.astype(jnp.bfloat16), residual_out, preferred_element_type=jnp.float32
+    ).astype(jnp.bfloat16)
     received = lax.all_to_all(
         buffer.reshape(experts, capacity, columns), "exp", split_axis=0, concat_axis=0, tiled=True
     )

time: 313 us -> 281 us (0.90)
  between operations: 33.7 us -> 13.9 us
  local copies, waits for them, and re-layouts: 27.5 us -> 17.3 us
    another operation x10 -> x2, other arithmetic: 9.16 us -> 3.5 us  [the longest x8 5.66 us: prefix_over(): jnp.select([lag == d for d in range(peers)], opts)]
    ppermute x12 -> x11, waiting for transfers between devices: 19.6 us -> 14.1 us  [prefix_over(): lax.ppermute(part, axis, [(i, (i + d) % peers) for i in range(peers)])]
    scatter x1 -> x0, local copies, waits for them, and re-layouts: 3.53 us -> none  [body(): buffer.at[target].set(jnp.repeat(residual_out, choices_each, axis=0))]
    add x3, other arithmetic: 3.02 us -> 6.16 us  [link_states(): later[0][:, None, None] * earlier[1] + later[1]]
    ppermute x12 -> x11, starting transfers between devices: 15.2 us -> 13.9 us  [prefix_over(): lax.ppermute(part, axis, [(i, (i + d) % peers) for i in range(peers)])]
  transfers between devices with their start and end apart: 18 -> 17, of which waited for: 8 -> 8; matrix products, arithmetic and copies ran while one was open for 10% -> 7% of each run, Pallas kernels for 0% -> 0%
where the time goes in v2:
time: 281 us; the launch traced here: 280 us
  waiting for transfers between devices  162 us (58%)
  other arithmetic  26.5 us (9%)
  matrix products  25 us (9%)
  starting transfers between devices  20.6 us (7%)
  local copies, waits for them, and re-layouts  17.3 us (6%)
  blocking collectives  14.7 us (5%)
  between operations  13.9 us (5%)
    all_gather x1, waiting for transfers between devices, body(): row_block = lax.all_gather(slices, SEQ, axis=1, tiled=True)  70.1 us
    all_gather x1, waiting for transfers between devices, body(): gathered = lax.all_gather(normed, SEQ, axis=0, tiled=True)  53.1 us
    reduce_scatter x1, waiting for transfers between devices, body(): lax.psum_scatter(jnp.dot(row_block, out_weight, preferred_element_type=jn...  23.3 us
    all_to_all x1, blocking collectives, body(): lax.all_to_all(buffer.reshape(experts, capacity, columns), 'exp', split_a...  14.7 us
    ppermute x11, waiting for transfers between devices, prefix_over(): lax.ppermute(part, axis, [(i, (i + d) % peers) for i in range(peers)])  14.1 us
    ppermute x11, starting transfers between devices, prefix_over(): lax.ppermute(part, axis, [(i, (i + d) % peers) for i in range(peers)])  13.9 us
    dot_general x1, other arithmetic, body(): jnp.einsum('rd,rd->r', row_block, row_block, preferred_element_type=jnp.f...  7.08 us
    dot_general x1, matrix products, body(): lax.dot_general(w_gate, row_block, contract_last, preferred_element_type=...  6.96 us
  transfers between devices with their start and end apart: 17, of which 8 were waited for; matrix products, arithmetic and copies ran while one was open for 7% of the time, Pallas kernels for 0%

profile of v2, /device:TPU:1, one launch (start us, length us, event | category | flops | bytes accessed | tf_op | source)
XLA Modules:
  0.0 279.9 jit_solution(14804248638005709880)
XLA Ops:
  7.2 1.5 copy.85
  8.8 1.4 reduce_window_sum.26
  10.9 1.4 fusion.65
  12.3 0.8 copy.87
  13.1 2.4 fusion.41
  15.5 3.2 %collective-permute-start.6 = (f32[8,128,128]{2,1,0:T(8,128)}, f32[8,128,128]{2,1,0:T(8,128)}, u32[]{:S(2)}, u32[]{:S(2)}) collective-permute-start(f32[8,128,128]{2,1,0:T(8,128)} %fusion.41), channel_id=1, source_target_pairs={{0,8},{8,0},{1,9},{9,1},{2,10},{10,2},{3,11},{11,3},{4,12},{12,4},... | collective-permute-start | bytes 1572872 | tf_op jit(solution)/shard_map/ppermute | solution.py:42
  19.5 1.1 collective-permute-done
  20.6 1.3 fusion.64
  21.9 1.1 broadcast_select_fusion
  23.8 1.8 fusion.37
  25.6 2.2 collective-permute-start.8
  27.8 1.1 collective-permute-start.7
  29.3 1.4 collective-permute-start.2
  30.8 6.6 %collective-permute-done.3 = f32[4]{0:T(128)S(1)} collective-permute-done((f32[4]{0:T(128)S(1)}, f32[4]{0:T(128)S(1)}, u32[]{:S(2)}, u32[]{:S(2)}) %collective-permute-start.3) | collective-permute-done | bytes 48 | tf_op jit(solution)/shard_map/ppermute | solution.py:49
  37.4 2.9 %collective-permute-start.1 = (f32[4]{0:T(128)S(1)}, f32[4]{0:T(128)S(1)}, u32[]{:S(2)}, u32[]{:S(2)}) collective-permute-start(f32[4]{0:T(128)S(1)} %dynamic_slice.6), channel_id=1, source_target_pairs={{0,48},{16,0},{32,16},{48,32},{1,49},{17,1},{33,17},{49,33},{2,50}... | collective-permute-start | bytes 56 | tf_op jit(solution)/shard_map/ppermute | solution.py:49
  41.7 2.2 select_add_fusion
  43.9 1.2 collective-permute-start.12
  45.1 2.5 collective-permute-start.11
  47.5 1.2 collective-permute-start.10
  48.7 1.4 copy.93
  50.4 0.9 collective-permute-start.4
  51.3 3.2 %collective-permute-done.5 = f32[4]{0:T(128)S(1)} collective-permute-done((f32[4]{0:T(128)}, f32[4]{0:T(128)S(1)}, u32[]{:S(2)}, u32[]{:S(2)}) %collective-permute-start.5) | collective-permute-done | bytes 48 | tf_op jit(solution)/shard_map/ppermute | solution.py:49
  54.4 3.6 %collective-permute-done.4 = f32[4]{0:T(128)S(1)} collective-permute-done((f32[4]{0:T(128)}, f32[4]{0:T(128)S(1)}, u32[]{:S(2)}, u32[]{:S(2)}) %collective-permute-start.4) | collective-permute-done | bytes 48 | tf_op jit(solution)/shard_map/ppermute | solution.py:49
  58.1 2.1 fusion.36
  60.2 3.3 %collective-permute-start.13 = (f32[4,128,128]{2,1,0:T(8,128)}, f32[4,128,128]{2,1,0:T(8,128)}, u32[]{:S(2)}, u32[]{:S(2)}) collective-permute-start(f32[4,128,128]{2,1,0:T(8,128)} %fusion.36), channel_id=1, source_target_pairs={{0,8},{8,0},{1,9},{9,1},{2,10},{10,2},{3,11},{11,3},{4,12},{12,4},... | collective-permute-start | bytes 786440 | tf_op jit(solution)/shard_map/ppermute | solution.py:42
  63.5 1.9 convolution_multiply_fusion
  65.4 0.8 copy.90
  66.2 1.2 convolution_bitcast_fusion
  67.5 2.2 multiply_reduce_fusion
  70.6 53.1 %all-gather.3.cloned.1.call-done = bf16[2048,1024]{1,0:T(8,128)(2,1)} async-done(((bf16[64,1024]{1,0:T(8,128)(2,1)}), bf16[2048,1024]{1,0:T(8,128)(2,1)}) %all-gather.3.cloned.1.call-update) | async-done | bytes 4194320 | tf_op jit(solution)/shard_map/all_gather | solution.py:125
  123.7 5.0 %fusion.67 = f32[2048,192]{0,1:T(8,128)} fusion(bf16[2048,1024]{1,0:T(8,128)(2,1)} %all-gather.3.cloned.1.call-done, bf16[1024,192]{0,1:T(8,128)(2,1)} %param.13), kind=kOutput, calls=%fused_computation.97 | convolution fusion | flops 805306368 | bytes 6160384 | tf_op jit(solution)/shard_map/dot_general | solution.py:128
  128.7 0.8 copy.97
  129.5 1.0 eq.69
  130.6 1.6 eq.65
  132.8 2.2 reduce-window.6
  135.8 1.3 reduce-window.9
  138.6 0.8 sub.37
  139.4 1.0 copy.99
  141.0 23.3 %reduce-scatter.2.cloned.1.call-done = f32[256,192]{0,1:T(8,128)} async-done(((f32[2048,192]{0,1:T(8,128)}), f32[256,192]{0,1:T(8,128)}) %reduce-scatter.2.cloned.1.call-update) | async-done | bytes 196624 | tf_op jit(solution)/shard_map/reduce_scatter | solution.py:127
  164.3 1.0 add_convert_fusion
  166.5 14.7 %all_to_all.5 = bf16[8,128,192]{1,2,0:T(8,128)(2,1)S(1)} all-to-all(bf16[8,128,192]{1,2,0:T(8,128)(2,1)S(1)} %bitcast.120), channel_id=1, replica_groups=mesh['seq_0'=4,'seq_1'=4,'seq_2'=2,'exp'=8] {'exp'}, dimensions={0} | all-to-all | bytes 786432 | tf_op jit(solution)/shard_map/all_to_all | solution.py:155
  181.2 0.8 copy_bitcast_fusion
  182.0 70.1 %all-gather.5.cloned.1.call-done = bf16[1024,6144]{0,1:T(8,128)(2,1)} async-done(((bf16[1024,192]{0,1:T(8,128)(2,1)}), bf16[1024,6144]{0,1:T(8,128)(2,1)}) %all-gather.5.cloned.1.call-update) | async-done | bytes 12582928 | tf_op jit(solution)/shard_map/all_gather | solution.py:160
  252.2 7.1 %fusion = f32[1024]{0:T(1024)S(1)} fusion(bf16[1024,6144]{0,1:T(8,128)(2,1)} %all-gather.5.cloned.1.call-done), kind=kLoop, calls=%fused_computation.1 | loop fusion | flops 18873344 | bytes 12587008 | tf_op jit(solution)/shard_map/rd,rd->r/dot_general | solution.py:161
  259.3 7.0 %fusion.17 = f32[288,1024]{1,0:T(8,128)S(1)} fusion(bf16[1024,6144]{0,1:T(8,128)(2,1)} %all-gather.5.cloned.1.call-done, bf16[1,288,6144]{2,1,0:T(8,128)(2,1)S(1)} %copy-done, f32[1024]{0:T(1024)S(1)} %add_rsqrt_fusion), kind=kOutput, calls=%fused_computation.10 | convolution fusion | flops 3624173568 | bytes 17305600 | tf_op jit(solution)/shard_map/dot_general | solution.py:162
  266.3 1.2 copy-done.1
  267.4 1.0 copy-done.5
  268.5 4.9 %fusion.23 = bf16[1,288,1024]{2,1,0:T(8,128)(2,1)} fusion(bf16[1024,6144]{0,1:T(8,128)(2,1)S(1)} %copy-done.1, bf16[1,288,6144]{2,1,0:T(8,128)(2,1)S(1)} %copy-done.5, f32[288,1024]{1,0:T(8,128)S(1)} %fusion.17, f32[1024]{0:T(1024)S(1)} %add_rsqrt_fusion), kind=kOutput, calls=%fused_computation.12 | convolution fusion | flops 3625943040 | bytes 17895424 | tf_op jit(solution)/shard_map/dot_general | solution.py:163
  (49 shorter events, 10.1 us)
Async XLA Ops:
  7.2 252.1 %copy-start = (bf16[1,288,6144]{2,1,0:T(8,128)(2,1)S(1)}, bf16[1,288,6144]{2,1,0:T(8,128)(2,1)}, u32[]{:S(2)}) copy-start(bf16[1,288,6144]{2,1,0:T(8,128)(2,1)} %param.16) | copy-start | bytes 10616836
  7.2 116.5 %all-gather.3.cloned.1.call-start = ((), (), s32[]{:S(2)}) async-start(), calls=%async_computation.2 | async-start | bytes 4325376 | tf_op jit(solution)/shard_map/all_gather | solution.py:125
  15.5 6.4 %collective-permute-start.6 = (f32[8,128,128]{2,1,0:T(8,128)}, f32[8,128,128]{2,1,0:T(8,128)}, u32[]{:S(2)}, u32[]{:S(2)}) collective-permute-start(f32[8,128,128]{2,1,0:T(8,128)} %fusion.41), channel_id=1, source_target_pairs={{0,8},{8,0},{1,9},{9,1},{2,10},{10,2},{3,11},{11,3},{4,12},{12,4},... | collective-permute-start | bytes 1572872 | tf_op jit(solution)/shard_map/ppermute | solution.py:42
  19.4 1.1 collective-permute-start
  23.0 0.8 copy-start.2
  25.6 16.0 %collective-permute-start.9 = (f32[4,128,128]{2,1,0:T(8,128)}, f32[4,128,128]{2,1,0:T(8,128)}, u32[]{:S(2)}, u32[]{:S(2)}) collective-permute-start(f32[4,128,128]{2,1,0:T(8,128)} %fusion.37), channel_id=1, source_target_pairs={{0,16},{16,32},{32,48},{48,0},{1,17},{17,33},{33,49},{49,1},{2,18}... | collective-permute-start | bytes 786440 | tf_op jit(solution)/shard_map/ppermute | solution.py:49
  25.6 16.0 %collective-permute-start.8 = (f32[4,128,128]{2,1,0:T(8,128)}, f32[4,128,128]{2,1,0:T(8,128)}, u32[]{:S(2)}, u32[]{:S(2)}) collective-permute-start(f32[4,128,128]{2,1,0:T(8,128)} %fusion.37), channel_id=1, source_target_pairs={{0,32},{16,48},{32,0},{48,16},{1,33},{17,49},{33,1},{49,17},{2,34}... | collective-permute-start | bytes 786440 | tf_op jit(solution)/shard_map/ppermute | solution.py:49
  27.8 13.9 %collective-permute-start.7 = (f32[4,128,128]{2,1,0:T(8,128)}, f32[4,128,128]{2,1,0:T(8,128)}, u32[]{:S(2)}, u32[]{:S(2)}) collective-permute-start(f32[4,128,128]{2,1,0:T(8,128)} %fusion.37), channel_id=1, source_target_pairs={{0,48},{16,0},{32,16},{48,32},{1,49},{17,1},{33,17},{49,33},{2,50}... | collective-permute-start | bytes 786440 | tf_op jit(solution)/shard_map/ppermute | solution.py:49
  28.9 8.4 %collective-permute-start.3 = (f32[4]{0:T(128)S(1)}, f32[4]{0:T(128)S(1)}, u32[]{:S(2)}, u32[]{:S(2)}) collective-permute-start(f32[4]{0:T(128)S(1)} %dynamic_slice.6), channel_id=1, source_target_pairs={{0,16},{16,32},{32,48},{48,0},{1,17},{17,33},{33,49},{49,1},{2,18}... | collective-permute-start | bytes 56 | tf_op jit(solution)/shard_map/ppermute | solution.py:49
  29.3 10.9 %collective-permute-start.2 = (f32[4]{0:T(128)S(1)}, f32[4]{0:T(128)S(1)}, u32[]{:S(2)}, u32[]{:S(2)}) collective-permute-start(f32[4]{0:T(128)S(1)} %dynamic_slice.6), channel_id=1, source_target_pairs={{0,32},{16,48},{32,0},{48,16},{1,33},{17,49},{33,1},{49,17},{2,34}... | collective-permute-start | bytes 56 | tf_op jit(solution)/shard_map/ppermute | solution.py:49
  37.4 3.6 %collective-permute-start.1 = (f32[4]{0:T(128)S(1)}, f32[4]{0:T(128)S(1)}, u32[]{:S(2)}, u32[]{:S(2)}) collective-permute-start(f32[4]{0:T(128)S(1)} %dynamic_slice.6), channel_id=1, source_target_pairs={{0,48},{16,0},{32,16},{48,32},{1,49},{17,1},{33,17},{49,33},{2,50}... | collective-permute-start | bytes 56 | tf_op jit(solution)/shard_map/ppermute | solution.py:49
  43.9 14.2 %collective-permute-start.12 = (f32[4,128,128]{2,1,0:T(8,128)}, f32[4,128,128]{2,1,0:T(8,128)}, u32[]{:S(2)}, u32[]{:S(2)}) collective-permute-start(f32[4,128,128]{2,1,0:T(8,128)} %select_add_fusion), channel_id=1, source_target_pairs={{0,64},{64,128},{128,192},{192,0},{1,65},{65,129},{129,193},{193,1... | collective-permute-start | bytes 786440 | tf_op jit(solution)/shard_map/ppermute | solution.py:49
  45.1 13.0 %collective-permute-start.11 = (f32[4,128,128]{2,1,0:T(8,128)}, f32[4,128,128]{2,1,0:T(8,128)}, u32[]{:S(2)}, u32[]{:S(2)}) collective-permute-start(f32[4,128,128]{2,1,0:T(8,128)} %select_add_fusion), channel_id=1, source_target_pairs={{0,128},{64,192},{128,0},{192,64},{1,129},{65,193},{129,1},{193,65... | collective-permute-start | bytes 786440 | tf_op jit(solution)/shard_map/ppermute | solution.py:49
  47.5 10.6 %collective-permute-start.10 = (f32[4,128,128]{2,1,0:T(8,128)}, f32[4,128,128]{2,1,0:T(8,128)}, u32[]{:S(2)}, u32[]{:S(2)}) collective-permute-start(f32[4,128,128]{2,1,0:T(8,128)} %select_add_fusion), channel_id=1, source_target_pairs={{0,192},{64,0},{128,64},{192,128},{1,193},{65,1},{129,65},{193,129... | collective-permute-start | bytes 786440 | tf_op jit(solution)/shard_map/ppermute | solution.py:49
  50.1 4.4 %collective-permute-start.5 = (f32[4]{0:T(128)}, f32[4]{0:T(128)S(1)}, u32[]{:S(2)}, u32[]{:S(2)}) collective-permute-start(f32[4]{0:T(128)} %get-tuple-element.4), channel_id=1, source_target_pairs={{0,64},{64,128},{128,192},{192,0},{1,65},{65,129},{129,193},{193,1... | collective-permute-start | bytes 56 | tf_op jit(solution)/shard_map/ppermute | solution.py:49
  50.4 7.7 %collective-permute-start.4 = (f32[4]{0:T(128)}, f32[4]{0:T(128)S(1)}, u32[]{:S(2)}, u32[]{:S(2)}) collective-permute-start(f32[4]{0:T(128)} %get-tuple-element.4), channel_id=1, source_target_pairs={{0,128},{64,192},{128,0},{192,64},{1,129},{65,193},{129,1},{193,65... | collective-permute-start | bytes 56 | tf_op jit(solution)/shard_map/ppermute | solution.py:49
  60.2 7.3 %collective-permute-start.13 = (f32[4,128,128]{2,1,0:T(8,128)}, f32[4,128,128]{2,1,0:T(8,128)}, u32[]{:S(2)}, u32[]{:S(2)}) collective-permute-start(f32[4,128,128]{2,1,0:T(8,128)} %fusion.36), channel_id=1, source_target_pairs={{0,8},{8,0},{1,9},{9,1},{2,10},{10,2},{3,11},{11,3},{4,12},{12,4},... | collective-permute-start | bytes 786440 | tf_op jit(solution)/shard_map/ppermute | solution.py:42
  70.5 58.2 %copy-start.4 = (s32[256,2]{0,1:T(2,128)S(1)}, s32[256,2]{0,1:T(2,128)}, u32[]{:S(2)}) copy-start(s32[256,2]{0,1:T(2,128)} %param.15) | copy-start | bytes 6148
  70.5 93.8 %reduce-scatter.2.cloned.1.call-start = ((), (), s32[]{:S(2)}) async-start(), calls=%async_computation.3 | async-start | bytes 1769472 | tf_op jit(solution)/shard_map/reduce_scatter | solution.py:127
  128.7 123.5 %all-gather.5.cloned.1.call-start = ((), (), s32[]{:S(2)}) async-start(), calls=%async_computation.4 | async-start | bytes 12976128 | tf_op jit(solution)/shard_map/all_gather | solution.py:160
  165.3 0.6 copy-start.3
  259.3 8.2 %copy-start.1 = (bf16[1024,6144]{0,1:T(8,128)(2,1)S(1)}, bf16[1024,6144]{0,1:T(8,128)(2,1)}, u32[]{:S(2)}) copy-start(bf16[1024,6144]{0,1:T(8,128)(2,1)} %all-gather.5.cloned.1.call-done) | copy-start | bytes 37748740
  259.3 9.2 %copy-start.5 = (bf16[1,288,6144]{2,1,0:T(8,128)(2,1)S(1)}, bf16[1,288,6144]{2,1,0:T(8,128)(2,1)}, u32[]{:S(2)}) copy-start(bf16[1,288,6144]{2,1,0:T(8,128)(2,1)} %param.17) | copy-start | bytes 10616836
Sparse Core Ops, SparseCore 0:
  70.6 53.0 all-gather.2
  128.8 35.4 reduce-scatter.1
  182.2 69.9 all-gather.4

commit v3 on v2

--- a/solution.py
+++ b/solution.py
@@ -38,17 +38,32 @@
     return (earlier[0] * later[0], later[0][:, None, None] * earlier[1] + later[1])
 
 
-def swap_cores(tree):
-    return jax.tree.map(lambda part: lax.ppermute(part, "seq_2", [(0, 1), (1, 0)]), tree)
+def send(pair, axis, perm):
+    decay, state = pair
+    heads, rows, cols = state.shape
+    packed = jnp.concatenate(
+        [state, jnp.broadcast_to(decay[:, None, None], (heads, 8, cols))], axis=1
+    )
+    moved = lax.ppermute(packed, axis, perm)
+    return (moved[:, rows, 0], moved[:, :rows])
+
+
+def swap_cores(pair):
+    return send(pair, "seq_2", [(0, 1), (1, 0)])
+
+
+def ring_sum(part, axis):
+    peers = lax.axis_size(axis)
+    total = part
+    for d in range(1, peers):
+        total = total + lax.ppermute(part, axis, [(i, (i + d) % peers) for i in range(peers)])
+    return total
 
 
 def prefix_over(own, axis):
     peers, place = (lax.axis_size(axis), lax.axis_index(axis))
     shifted = [own] + [
-        jax.tree.map(
-            lambda part: lax.ppermute(part, axis, [(i, (i + d) % peers) for i in range(peers)]), own
-        )
-        for d in range(1, peers)
+        send(own, axis, [(i, (i + d) % peers) for i in range(peers)]) for d in range(1, peers)
     ]
     start = nothing_yet(own, (1.0, 0.0))
     before, after = (start, start)
@@ -158,7 +173,9 @@
     sources, entries, gathered_columns = received.shape
     slices = received.reshape(sources * entries, gathered_columns)
     row_block = lax.all_gather(slices, SEQ, axis=1, tiled=True)
-    squares = jnp.einsum("rd,rd->r", row_block, row_block, preferred_element_type=jnp.float32)
+    squares = jnp.einsum("rd,rd->r", slices, slices, preferred_element_type=jnp.float32)
+    for axis in reversed(SEQ):
+        squares = ring_sum(squares, axis)
     gate_sum = lax.dot_general(w_gate, row_block, contract_last, preferred_element_type=jnp.float32)
     up_sum = lax.dot_general(w_up, row_block, contract_last, preferred_element_type=jnp.float32)
     expert_hidden = finish_rows(gate_sum, up_sum, squares).reshape(hidden_rows, sources, entries)

time: 281 us -> 281 us (level)
  waiting for transfers between devices: 162 us -> 157 us
  starting transfers between devices: 20.6 us -> 24.8 us
  local copies, waits for them, and re-layouts: 17.3 us -> 20.5 us
    all_gather x1, waiting for transfers between devices: 70.1 us -> 48.7 us  [body(): row_block = lax.all_gather(slices, SEQ, axis=1, tiled=True)]
    ppermute x14 -> x15, waiting for transfers between devices: 15.3 us -> 32.1 us  [the longest x8 25.1 us: send(): moved = lax.ppermute(packed, axis, perm)]
    dot_general x1, other arithmetic: 7.08 us -> 1.09 us  [body(): jnp.einsum('rd,rd->r', slices, slices, preferred_element_type=jnp.float32)]
    ppermute x14 -> x15, starting transfers between devices: 20.5 us -> 24.7 us  [the longest x7 12.5 us: ring_sum(): lax.ppermute(part, axis, [(i, (i + d) % peers) for i in range(peers)])]
    concatenate x0 -> x4, other arithmetic: none -> 3 us  [send(): jnp.concatenate([state, jnp.broadcast_to(decay[:, None, None], (heads, 8,...]
    unnamed x14 -> x24, local copies, waits for them, and re-layouts: 5.97 us -> 8.4 us
  transfers between devices with their start and end apart: 17 -> 18, of which waited for: 8 -> 15; matrix products, arithmetic and copies ran while one was open for 7% -> 6% of each run, Pallas kernels for 0% -> 0%
where the time goes in v3:
time: 281 us; the launch traced here: 280 us
  waiting for transfers between devices  157 us (56%)
  other arithmetic  25.3 us (9%)
  starting transfers between devices  24.8 us (9%)
  matrix products  23.2 us (8%)
  local copies, waits for them, and re-layouts  20.5 us (7%)
  blocking collectives  15.5 us (6%)
  between operations  14 us (5%)
    all_gather x1, waiting for transfers between devices, body(): gathered = lax.all_gather(normed, SEQ, axis=0, tiled=True)  52.6 us
    all_gather x1, waiting for transfers between devices, body(): row_block = lax.all_gather(slices, SEQ, axis=1, tiled=True)  48.7 us
    ppermute x8, waiting for transfers between devices, send(): moved = lax.ppermute(packed, axis, perm)  25.1 us
    reduce_scatter x1, waiting for transfers between devices, body(): lax.psum_scatter(jnp.dot(row_block, out_weight, preferred_element_type=jn...  23.3 us
    all_to_all x1, blocking collectives, body(): lax.all_to_all(buffer.reshape(experts, capacity, columns), 'exp', split_a...  15.5 us
    ppermute x7, starting transfers between devices, ring_sum(): lax.ppermute(part, axis, [(i, (i + d) % peers) for i in range(peers)])  12.5 us
    ppermute x8, starting transfers between devices, send(): moved = lax.ppermute(packed, axis, perm)  12.2 us
    unnamed x24, local copies, waits for them, and re-layouts  8.4 us
  transfers between devices with their start and end apart: 18, of which 15 were waited for; matrix products, arithmetic and copies ran while one was open for 6% of the time, Pallas kernels for 0%

profile of v3, /device:TPU:1, one launch (start us, length us, event | category | flops | bytes accessed | tf_op | source)
XLA Modules:
  0.0 280.0 jit_solution(3335917781134832960)
XLA Ops:
  7.2 1.5 copy.96
  8.8 1.4 reduce_window_sum.26
  11.6 1.4 fusion.77
  13.8 1.7 fusion.41
  17.1 3.2 %collective-permute-start = (f32[8,136,128]{2,1,0:T(8,128)}, f32[8,136,128]{2,1,0:T(8,128)}, u32[]{:S(2)}, u32[]{:S(2)}) collective-permute-start(f32[8,136,128]{2,1,0:T(8,128)} %pad_maximum_fusion), channel_id=1, source_target_pairs={{0,8},{8,0},{1,9},{9,1},{2,10},{10,2},{3,11},{11,3},{4,12},{12,4},... | collective-permute-start | bytes 1671176 | tf_op jit(solution)/shard_map/ppermute | solution.py:47
  20.4 1.8 collective-permute-done
  22.2 1.5 fusion.63
  25.0 1.1 fusion.76
  26.2 1.2 fusion.37
  28.8 2.2 collective-permute-start.2
  31.0 1.1 collective-permute-start.1
  32.1 6.5 %collective-permute-done.3 = f32[4,136,128]{2,1,0:T(8,128)} collective-permute-done((f32[4,136,128]{2,1,0:T(8,128)}, f32[4,136,128]{2,1,0:T(8,128)}, u32[]{:S(2)}, u32[]{:S(2)}) %collective-permute-start.3) | collective-permute-done | bytes 278560 | tf_op jit(solution)/shard_map/ppermute | solution.py:47
  38.5 5.0 %collective-permute-done.2 = f32[4,136,128]{2,1,0:T(8,128)} collective-permute-done((f32[4,136,128]{2,1,0:T(8,128)}, f32[4,136,128]{2,1,0:T(8,128)}, u32[]{:S(2)}, u32[]{:S(2)}) %collective-permute-start.2) | collective-permute-done | bytes 278560 | tf_op jit(solution)/shard_map/ppermute | solution.py:47
  43.6 0.9 collective-permute-done.1
  44.5 0.9 fusion.66
  46.0 1.5 select_add_fusion
  48.6 2.5 collective-permute-start.4
  51.1 1.2 collective-permute-start.6
  52.2 4.2 %collective-permute-done.5 = f32[4,136,128]{2,1,0:T(8,128)} collective-permute-done((f32[4,136,128]{2,1,0:T(8,128)}, f32[4,136,128]{2,1,0:T(8,128)}, u32[]{:S(2)}, u32[]{:S(2)}) %collective-permute-start.5) | collective-permute-done | bytes 278560 | tf_op jit(solution)/shard_map/ppermute | solution.py:47
  56.5 6.2 %collective-permute-done.4 = f32[4,136,128]{2,1,0:T(8,128)} collective-permute-done((f32[4,136,128]{2,1,0:T(8,128)}, f32[4,136,128]{2,1,0:T(8,128)}, u32[]{:S(2)}, u32[]{:S(2)}) %collective-permute-start.4) | collective-permute-done | bytes 278560 | tf_op jit(solution)/shard_map/ppermute | solution.py:47
  64.0 0.9 fusion.74
  64.8 1.6 fusion.36
  67.8 1.8 collective-permute-start.7
  71.3 1.2 convolution_multiply_fusion
  72.5 1.0 slice.95
  73.5 2.0 convolution_bitcast_fusion.1
  75.5 1.3 multiply_reduce_fusion
  77.6 52.6 %all-gather.3.cloned.1.call-done = bf16[2048,1024]{1,0:T(8,128)(2,1)} async-done(((bf16[64,1024]{1,0:T(8,128)(2,1)}), bf16[2048,1024]{1,0:T(8,128)(2,1)}) %all-gather.3.cloned.1.call-update) | async-done | bytes 4194320 | tf_op jit(solution)/shard_map/all_gather | solution.py:140
  130.2 5.0 %fusion.79 = f32[2048,192]{0,1:T(8,128)} fusion(bf16[2048,1024]{1,0:T(8,128)(2,1)} %all-gather.3.cloned.1.call-done, bf16[1024,192]{0,1:T(8,128)(2,1)} %param.13), kind=kOutput, calls=%fused_computation.130 | convolution fusion | flops 805306368 | bytes 6160384 | tf_op jit(solution)/shard_map/dot_general | solution.py:143
  136.1 1.0 eq.69
  137.1 1.6 eq.65
  139.4 2.2 reduce-window.6
  142.4 1.3 reduce-window.9
  145.9 1.0 copy.111
  147.6 23.3 %reduce-scatter.2.cloned.1.call-done = f32[256,192]{0,1:T(8,128)} async-done(((f32[2048,192]{0,1:T(8,128)}), f32[256,192]{0,1:T(8,128)}) %reduce-scatter.2.cloned.1.call-update) | async-done | bytes 196624 | tf_op jit(solution)/shard_map/reduce_scatter | solution.py:142
  170.9 1.0 add_convert_fusion
  173.0 15.5 %all_to_all.5 = bf16[8,128,192]{1,2,0:T(8,128)(2,1)S(1)} all-to-all(bf16[8,128,192]{1,2,0:T(8,128)(2,1)S(1)} %bitcast.122), channel_id=1, replica_groups=mesh['seq_0'=4,'seq_1'=4,'seq_2'=2,'exp'=8] {'exp'}, dimensions={0} | all-to-all | bytes 786432 | tf_op jit(solution)/shard_map/all_to_all | solution.py:170
  190.1 1.1 fusion.29
  191.2 5.3 %collective-permute-start.8 = (f32[1024]{0:T(1024)S(1)}, f32[1024]{0:T(1024)S(1)}, u32[]{:S(2)}, u32[]{:S(2)}) collective-permute-start(f32[1024]{0:T(1024)S(1)} %fusion.29), channel_id=1, source_target_pairs={{0,8},{8,0},{1,9},{9,1},{2,10},{10,2},{3,11},{11,3},{4,12},{12,4},... | collective-permute-start | bytes 12296 | tf_op jit(solution)/shard_map/ppermute | solution.py:59
  197.4 2.5 collective-permute-start.11
  201.0 2.8 %collective-permute-done.10 = f32[1024]{0:T(1024)S(1)} collective-permute-done((f32[1024]{0:T(1024)S(1)}, f32[1024]{0:T(1024)S(1)}, u32[]{:S(2)}, u32[]{:S(2)}) %collective-permute-start.10) | collective-permute-done | bytes 4128 | tf_op jit(solution)/shard_map/ppermute | solution.py:59
  204.1 2.5 collective-permute-start.14
  207.7 2.9 %collective-permute-done.13 = f32[1024]{0:T(1024)S(1)} collective-permute-done((f32[1024]{0:T(1024)S(1)}, f32[1024]{0:T(1024)S(1)}, u32[]{:S(2)}, u32[]{:S(2)}) %collective-permute-start.13) | collective-permute-done | bytes 4128 | tf_op jit(solution)/shard_map/ppermute | solution.py:59
  210.7 48.7 %all-gather.5.cloned.1.call-done = bf16[1024,6144]{0,1:T(8,128)(2,1)} async-done(((bf16[1024,192]{0,1:T(8,128)(2,1)}), bf16[1024,6144]{0,1:T(8,128)(2,1)}) %all-gather.5.cloned.1.call-update) | async-done | bytes 12582928 | tf_op jit(solution)/shard_map/all_gather | solution.py:175
  259.5 6.9 %fusion.16 = f32[288,1024]{1,0:T(8,128)S(1)} fusion(bf16[1024,6144]{0,1:T(8,128)(2,1)} %all-gather.5.cloned.1.call-done, bf16[1,288,6144]{2,1,0:T(8,128)(2,1)S(1)} %copy-done, f32[1024]{0:T(1024)S(1)} %add_rsqrt_fusion), kind=kOutput, calls=%fused_computation.8 | convolution fusion | flops 3624173568 | bytes 17305600 | tf_op jit(solution)/shard_map/dot_general | solution.py:179
  266.4 1.2 copy-done.9
  267.6 1.0 copy-done.10
  268.6 4.8 %fusion.22 = bf16[1,288,1024]{2,1,0:T(8,128)(2,1)} fusion(bf16[1024,6144]{0,1:T(8,128)(2,1)S(1)} %copy-done.9, bf16[1,288,6144]{2,1,0:T(8,128)(2,1)S(1)} %copy-done.10, f32[288,1024]{1,0:T(8,128)S(1)} %fusion.16, f32[1024]{0:T(1024)S(1)} %add_rsqrt_fusion), kind=kOutput, calls=%fused_computation.10 | convolution fusion | flops 3625943040 | bytes 17895424 | tf_op jit(solution)/shard_map/dot_general | solution.py:180
  (76 shorter events, 25.1 us)
Async XLA Ops:
  7.2 252.3 %copy-start = (bf16[1,288,6144]{2,1,0:T(8,128)(2,1)S(1)}, bf16[1,288,6144]{2,1,0:T(8,128)(2,1)}, u32[]{:S(2)}) copy-start(bf16[1,288,6144]{2,1,0:T(8,128)(2,1)} %param.16) | copy-start | bytes 10616836
  7.2 123.1 %all-gather.3.cloned.1.call-start = ((), (), s32[]{:S(2)}) async-start(), calls=%async_computation.2 | async-start | bytes 4325376 | tf_op jit(solution)/shard_map/all_gather | solution.py:140
  15.4 0.8 copy-start.1
  17.1 5.2 %collective-permute-start = (f32[8,136,128]{2,1,0:T(8,128)}, f32[8,136,128]{2,1,0:T(8,128)}, u32[]{:S(2)}, u32[]{:S(2)}) collective-permute-start(f32[8,136,128]{2,1,0:T(8,128)} %pad_maximum_fusion), channel_id=1, source_target_pairs={{0,8},{8,0},{1,9},{9,1},{2,10},{10,2},{3,11},{11,3},{4,12},{12,4},... | collective-permute-start | bytes 1671176 | tf_op jit(solution)/shard_map/ppermute | solution.py:47
  24.4 0.5 copy-start.8
  26.1 2.7 copy-start.4
  27.4 0.7 copy-start.3
  28.8 9.7 %collective-permute-start.3 = (f32[4,136,128]{2,1,0:T(8,128)}, f32[4,136,128]{2,1,0:T(8,128)}, u32[]{:S(2)}, u32[]{:S(2)}) collective-permute-start(f32[4,136,128]{2,1,0:T(8,128)} %pad_maximum_fusion.1), channel_id=1, source_target_pairs={{0,16},{16,32},{32,48},{48,0},{1,17},{17,33},{33,49},{49,1},{2,18}... | collective-permute-start | bytes 835592 | tf_op jit(solution)/shard_map/ppermute | solution.py:47
  28.8 14.7 %collective-permute-start.2 = (f32[4,136,128]{2,1,0:T(8,128)}, f32[4,136,128]{2,1,0:T(8,128)}, u32[]{:S(2)}, u32[]{:S(2)}) collective-permute-start(f32[4,136,128]{2,1,0:T(8,128)} %pad_maximum_fusion.1), channel_id=1, source_target_pairs={{0,32},{16,48},{32,0},{48,16},{1,33},{17,49},{33,1},{49,17},{2,34}... | collective-permute-start | bytes 835592 | tf_op jit(solution)/shard_map/ppermute | solution.py:47
  31.0 13.5 %collective-permute-start.1 = (f32[4,136,128]{2,1,0:T(8,128)}, f32[4,136,128]{2,1,0:T(8,128)}, u32[]{:S(2)}, u32[]{:S(2)}) collective-permute-start(f32[4,136,128]{2,1,0:T(8,128)} %pad_maximum_fusion.1), channel_id=1, source_target_pairs={{0,48},{16,0},{32,16},{48,32},{1,49},{17,1},{33,17},{49,33},{2,50}... | collective-permute-start | bytes 835592 | tf_op jit(solution)/shard_map/ppermute | solution.py:47
  48.3 8.1 %collective-permute-start.5 = (f32[4,136,128]{2,1,0:T(8,128)}, f32[4,136,128]{2,1,0:T(8,128)}, u32[]{:S(2)}, u32[]{:S(2)}) collective-permute-start(f32[4,136,128]{2,1,0:T(8,128)} %pad_maximum_fusion.2), channel_id=1, source_target_pairs={{0,64},{64,128},{128,192},{192,0},{1,65},{65,129},{129,193},{193,1... | collective-permute-start | bytes 835592 | tf_op jit(solution)/shard_map/ppermute | solution.py:47
  48.6 14.0 %collective-permute-start.4 = (f32[4,136,128]{2,1,0:T(8,128)}, f32[4,136,128]{2,1,0:T(8,128)}, u32[]{:S(2)}, u32[]{:S(2)}) collective-permute-start(f32[4,136,128]{2,1,0:T(8,128)} %pad_maximum_fusion.2), channel_id=1, source_target_pairs={{0,128},{64,192},{128,0},{192,64},{1,129},{65,193},{129,1},{193,65... | collective-permute-start | bytes 835592 | tf_op jit(solution)/shard_map/ppermute | solution.py:47
  51.1 12.9 %collective-permute-start.6 = (f32[4,136,128]{2,1,0:T(8,128)}, f32[4,136,128]{2,1,0:T(8,128)}, u32[]{:S(2)}, u32[]{:S(2)}) collective-permute-start(f32[4,136,128]{2,1,0:T(8,128)} %pad_maximum_fusion.2), channel_id=1, source_target_pairs={{0,192},{64,0},{128,64},{192,128},{1,193},{65,1},{129,65},{193,129... | collective-permute-start | bytes 835592 | tf_op jit(solution)/shard_map/ppermute | solution.py:47
  66.4 0.7 copy-start.5
  67.8 4.7 %collective-permute-start.7 = (f32[4,136,128]{2,1,0:T(8,128)}, f32[4,136,128]{2,1,0:T(8,128)}, u32[]{:S(2)}, u32[]{:S(2)}) collective-permute-start(f32[4,136,128]{2,1,0:T(8,128)} %pad_maximum_fusion.3), channel_id=1, source_target_pairs={{0,8},{8,0},{1,9},{9,1},{2,10},{10,2},{3,11},{11,3},{4,12},{12,4},... | collective-permute-start | bytes 835592 | tf_op jit(solution)/shard_map/ppermute | solution.py:47
  77.6 57.7 %copy-start.7 = (s32[256,2]{0,1:T(2,128)S(1)}, s32[256,2]{0,1:T(2,128)}, u32[]{:S(2)}) copy-start(s32[256,2]{0,1:T(2,128)} %param.15) | copy-start | bytes 6148
  77.6 93.3 %reduce-scatter.2.cloned.1.call-start = ((), (), s32[]{:S(2)}) async-start(), calls=%async_computation.3 | async-start | bytes 1769472 | tf_op jit(solution)/shard_map/reduce_scatter | solution.py:142
  135.2 124.2 %all-gather.5.cloned.1.call-start = ((), (), s32[]{:S(2)}) async-start(), calls=%async_computation.4 | async-start | bytes 12976128 | tf_op jit(solution)/shard_map/all_gather | solution.py:175
  171.9 0.6 copy-start.6
  188.5 0.8 copy-start.2
  191.2 6.2 %collective-permute-start.8 = (f32[1024]{0:T(1024)S(1)}, f32[1024]{0:T(1024)S(1)}, u32[]{:S(2)}, u32[]{:S(2)}) collective-permute-start(f32[1024]{0:T(1024)S(1)} %fusion.29), channel_id=1, source_target_pairs={{0,8},{8,0},{1,9},{9,1},{2,10},{10,2},{3,11},{11,3},{4,12},{12,4},... | collective-permute-start | bytes 12296 | tf_op jit(solution)/shard_map/ppermute | solution.py:59
  197.4 3.6 %collective-permute-start.11 = (f32[1024]{0:T(1024)S(1)}, f32[1024]{0:T(1024)S(1)}, u32[]{:S(2)}, u32[]{:S(2)}) collective-permute-start(f32[1024]{0:T(1024)S(1)} %add.115), channel_id=1, source_target_pairs={{0,48},{16,0},{32,16},{48,32},{1,49},{17,1},{33,17},{49,33},{2,50}... | collective-permute-start | bytes 12296 | tf_op jit(solution)/shard_map/ppermute | solution.py:59
  199.9 4.0 %collective-permute-start.10 = (f32[1024]{0:T(1024)S(1)}, f32[1024]{0:T(1024)S(1)}, u32[]{:S(2)}, u32[]{:S(2)}) collective-permute-start(f32[1024]{0:T(1024)S(1)} %add.115), channel_id=1, source_target_pairs={{0,32},{16,48},{32,0},{48,16},{1,33},{17,49},{33,1},{49,17},{2,34}... | collective-permute-start | bytes 12296 | tf_op jit(solution)/shard_map/ppermute | solution.py:59
  200.4 3.7 %collective-permute-start.9 = (f32[1024]{0:T(1024)S(1)}, f32[1024]{0:T(1024)S(1)}, u32[]{:S(2)}, u32[]{:S(2)}) collective-permute-start(f32[1024]{0:T(1024)S(1)} %add.115), channel_id=1, source_target_pairs={{0,16},{16,32},{32,48},{48,0},{1,17},{17,33},{33,49},{49,1},{2,18}... | collective-permute-start | bytes 12296 | tf_op jit(solution)/shard_map/ppermute | solution.py:59
  204.1 3.6 %collective-permute-start.14 = (f32[1024]{0:T(1024)S(1)}, f32[1024]{0:T(1024)S(1)}, u32[]{:S(2)}, u32[]{:S(2)}) collective-permute-start(f32[1024]{0:T(1024)S(1)} %add_add_fusion), channel_id=1, source_target_pairs={{0,192},{64,0},{128,64},{192,128},{1,193},{65,1},{129,65},{193,129... | collective-permute-start | bytes 12296 | tf_op jit(solution)/shard_map/ppermute | solution.py:59
  206.6 4.0 %collective-permute-start.13 = (f32[1024]{0:T(1024)S(1)}, f32[1024]{0:T(1024)S(1)}, u32[]{:S(2)}, u32[]{:S(2)}) collective-permute-start(f32[1024]{0:T(1024)S(1)} %add_add_fusion), channel_id=1, source_target_pairs={{0,128},{64,192},{128,0},{192,64},{1,129},{65,193},{129,1},{193,65... | collective-permute-start | bytes 12296 | tf_op jit(solution)/shard_map/ppermute | solution.py:59
  207.1 3.7 %collective-permute-start.12 = (f32[1024]{0:T(1024)S(1)}, f32[1024]{0:T(1024)S(1)}, u32[]{:S(2)}, u32[]{:S(2)}) collective-permute-start(f32[1024]{0:T(1024)S(1)} %add_add_fusion), channel_id=1, source_target_pairs={{0,64},{64,128},{128,192},{192,0},{1,65},{65,129},{129,193},{193,1... | collective-permute-start | bytes 12296 | tf_op jit(solution)/shard_map/ppermute | solution.py:59
  259.5 8.2 %copy-start.9 = (bf16[1024,6144]{0,1:T(8,128)(2,1)S(1)}, bf16[1024,6144]{0,1:T(8,128)(2,1)}, u32[]{:S(2)}) copy-start(bf16[1024,6144]{0,1:T(8,128)(2,1)} %all-gather.5.cloned.1.call-done) | copy-start | bytes 37748740
  259.5 9.2 %copy-start.10 = (bf16[1,288,6144]{2,1,0:T(8,128)(2,1)S(1)}, bf16[1,288,6144]{2,1,0:T(8,128)(2,1)}, u32[]{:S(2)}) copy-start(bf16[1,288,6144]{2,1,0:T(8,128)(2,1)} %param.17) | copy-start | bytes 10616836
Sparse Core Ops, SparseCore 0:
  77.7 52.4 all-gather.2
  135.3 35.4 reduce-scatter.1
  190.2 69.1 all-gather.4

commit v4 on v3

--- a/solution.py
+++ b/solution.py
@@ -40,16 +40,12 @@
 
 def send(pair, axis, perm):
     decay, state = pair
-    heads, rows, cols = state.shape
-    packed = jnp.concatenate(
-        [state, jnp.broadcast_to(decay[:, None, None], (heads, 8, cols))], axis=1
-    )
-    moved = lax.ppermute(packed, axis, perm)
-    return (moved[:, rows, 0], moved[:, :rows])
+    moved = lax.ppermute(state.astype(jnp.bfloat16), axis, perm)
+    return (lax.ppermute(decay, axis, perm), moved.astype(jnp.float32))
 
 
 def swap_cores(pair):
-    return send(pair, "seq_2", [(0, 1), (1, 0)])
+    return jax.tree.map(lambda part: lax.ppermute(part, "seq_2", [(0, 1), (1, 0)]), pair)
 
 
 def ring_sum(part, axis):

time: 281 us -> 260 us (0.925)
  waiting for transfers between devices: 157 us -> 138 us
  other arithmetic: 25.3 us -> 15.9 us
  starting transfers between devices: 24.8 us -> 34.1 us
  local copies, waits for them, and re-layouts: 20.5 us -> 17.6 us
    ppermute x8 -> x14, waiting for transfers between devices: 25.1 us -> 5.13 us  [the longest x6 4.84 us: send(): moved = lax.ppermute(state.astype(jnp.bfloat16), axis, perm)]
    ppermute x8 -> x14, starting transfers between devices: 12.2 us -> 21.5 us  [the longest x6 9 us: send(): moved = lax.ppermute(state.astype(jnp.bfloat16), axis, perm)]
    add x3 -> x1, other arithmetic: 4.33 us -> 1.07 us  [link_states(): later[0][:, None, None] * earlier[1] + later[1]]
    concatenate x4 -> x0, other arithmetic: 3 us -> none  [send(): jnp.concatenate([state, jnp.broadcast_to(decay[:, None, None], (heads, 8,...]
    unnamed x24 -> x20, local copies, waits for them, and re-layouts: 8.4 us -> 6.8 us
  transfers between devices with their start and end apart: 18 -> 24, of which waited for: 15 -> 13; matrix products, arithmetic and copies ran while one was open for 6% -> 8% of each run, Pallas kernels for 0% -> 0%
where the time goes in v4:
time: 260 us; the launch traced here: 259 us
  waiting for transfers between devices  138 us (53%)
  starting transfers between devices  34.1 us (13%)
  matrix products  24 us (9%)
  local copies, waits for them, and re-layouts  17.6 us (7%)
  other arithmetic  15.9 us (6%)
  blocking collectives  15.4 us (6%)
  between operations  13.9 us (5%)
    all_gather x1, waiting for transfers between devices, body(): gathered = lax.all_gather(normed, SEQ, axis=0, tiled=True)  53.8 us
    all_gather x1, waiting for transfers between devices, body(): row_block = lax.all_gather(slices, SEQ, axis=1, tiled=True)  48.9 us
    reduce_scatter x1, waiting for transfers between devices, body(): lax.psum_scatter(jnp.dot(row_block, out_weight, preferred_element_type=jn...  23.3 us
    all_to_all x1, blocking collectives, body(): lax.all_to_all(buffer.reshape(experts, capacity, columns), 'exp', split_a...  15.4 us
    ppermute x7, starting transfers between devices, ring_sum(): lax.ppermute(part, axis, [(i, (i + d) % peers) for i in range(peers)])  12.5 us
    ppermute x6, starting transfers between devices, send(): moved = lax.ppermute(state.astype(jnp.bfloat16), axis, perm)  9 us
    dot_general x1, matrix products, body(): lax.dot_general(w_gate, row_block, contract_last, preferred_element_type=...  6.94 us
    ppermute x7, waiting for transfers between devices, ring_sum(): lax.ppermute(part, axis, [(i, (i + d) % peers) for i in range(peers)])  6.88 us
  transfers between devices with their start and end apart: 24, of which 13 were waited for; matrix products, arithmetic and copies ran while one was open for 8% of the time, Pallas kernels for 0%

profile of v4, /device:TPU:1, one launch (start us, length us, event | category | flops | bytes accessed | tf_op | source)
XLA Modules:
  0.0 259.0 jit_solution(1776242517446501573)
XLA Ops:
  7.2 1.5 copy.85
  8.8 1.4 reduce_window_sum.26
  10.9 1.4 fusion.73
  12.3 0.8 copy.87
  13.1 2.4 fusion.47
  15.5 3.2 %collective-permute-start.6 = (f32[8,128,128]{2,1,0:T(8,128)}, f32[8,128,128]{2,1,0:T(8,128)}, u32[]{:S(2)}, u32[]{:S(2)}) collective-permute-start(f32[8,128,128]{2,1,0:T(8,128)} %fusion.47), channel_id=1, source_target_pairs={{0,8},{8,0},{1,9},{9,1},{2,10},{10,2},{3,11},{11,3},{4,12},{12,4},... | collective-permute-start | bytes 1572872 | tf_op jit(solution)/shard_map/ppermute | solution.py:48
  19.5 0.8 copy.93
  21.4 2.2 collective-permute-start.2
  23.6 1.1 collective-permute-start.1
  24.7 1.1 broadcast_select_fusion
  26.6 1.1 fusion.71
  28.2 1.5 collective-permute-start.8
  29.7 2.0 collective-permute-start.7
  32.0 2.5 collective-permute-start.4
  36.5 1.5 collective-permute-start.12
  38.0 2.5 collective-permute-start.11
  40.4 1.2 collective-permute-start.10
  41.6 2.7 %collective-permute-done.11 = bf16[4,128,128]{2,1,0:T(8,128)(2,1)S(1)} collective-permute-done((bf16[4,128,128]{2,1,0:T(8,128)(2,1)S(1)}, bf16[4,128,128]{2,1,0:T(8,128)(2,1)S(1)}, u32[]{:S(2)}, u32[]{:S(2)}) %collective-permute-start.11) | collective-permute-done | bytes 131104 | tf_op jit(solution)/shard_map/ppermute | solution.py:43
  44.9 1.1 fusion.42
  46.0 3.2 %collective-permute-start.13 = (f32[4,128,128]{2,1,0:T(8,128)}, f32[4,128,128]{2,1,0:T(8,128)}, u32[]{:S(2)}, u32[]{:S(2)}) collective-permute-start(f32[4,128,128]{2,1,0:T(8,128)} %fusion.42), channel_id=1, source_target_pairs={{0,8},{8,0},{1,9},{9,1},{2,10},{10,2},{3,11},{11,3},{4,12},{12,4},... | collective-permute-start | bytes 786440 | tf_op jit(solution)/shard_map/ppermute | solution.py:48
  49.3 0.9 convolution_multiply_fusion
  50.2 0.8 copy.90
  51.0 1.2 convolution_bitcast_fusion
  52.2 2.2 multiply_reduce_fusion
  55.3 53.8 %all-gather.3.cloned.1.call-done = bf16[2048,1024]{1,0:T(8,128)(2,1)} async-done(((bf16[64,1024]{1,0:T(8,128)(2,1)}), bf16[2048,1024]{1,0:T(8,128)(2,1)}) %all-gather.3.cloned.1.call-update) | async-done | bytes 4194320 | tf_op jit(solution)/shard_map/all_gather | solution.py:136
  109.2 5.0 %fusion.75 = f32[2048,192]{0,1:T(8,128)} fusion(bf16[2048,1024]{1,0:T(8,128)(2,1)} %all-gather.3.cloned.1.call-done, bf16[1024,192]{0,1:T(8,128)(2,1)} %param.13), kind=kOutput, calls=%fused_computation.110 | convolution fusion | flops 805306368 | bytes 6160384 | tf_op jit(solution)/shard_map/dot_general | solution.py:139
  114.2 0.8 copy.97
  115.0 1.0 eq.69
  116.1 1.6 eq.65
  118.3 2.2 reduce-window.6
  121.3 1.3 reduce-window.9
  124.9 1.0 copy.99
  126.5 23.3 %reduce-scatter.2.cloned.1.call-done = f32[256,192]{0,1:T(8,128)} async-done(((f32[2048,192]{0,1:T(8,128)}), f32[256,192]{0,1:T(8,128)}) %reduce-scatter.2.cloned.1.call-update) | async-done | bytes 196624 | tf_op jit(solution)/shard_map/reduce_scatter | solution.py:138
  149.9 1.0 add_convert_fusion
  152.0 15.4 %all_to_all.5 = bf16[8,128,192]{1,2,0:T(8,128)(2,1)S(1)} all-to-all(bf16[8,128,192]{1,2,0:T(8,128)(2,1)S(1)} %bitcast.124), channel_id=1, replica_groups=mesh['seq_0'=4,'seq_1'=4,'seq_2'=2,'exp'=8] {'exp'}, dimensions={0} | all-to-all | bytes 786432 | tf_op jit(solution)/shard_map/all_to_all | solution.py:166
  168.2 0.8 copy_bitcast_fusion
  169.0 1.1 fusion.29
  170.1 5.2 %collective-permute-start.14 = (f32[1024]{0:T(1024)S(1)}, f32[1024]{0:T(1024)S(1)}, u32[]{:S(2)}, u32[]{:S(2)}) collective-permute-start(f32[1024]{0:T(1024)S(1)} %fusion.29), channel_id=1, source_target_pairs={{0,8},{8,0},{1,9},{9,1},{2,10},{10,2},{3,11},{11,3},{4,12},{12,4},... | collective-permute-start | bytes 12296 | tf_op jit(solution)/shard_map/ppermute | solution.py:55
  175.4 0.8 collective-permute-done.14
  176.2 2.5 collective-permute-start.17
  179.8 2.8 %collective-permute-done.16 = f32[1024]{0:T(1024)S(1)} collective-permute-done((f32[1024]{0:T(1024)S(1)}, f32[1024]{0:T(1024)S(1)}, u32[]{:S(2)}, u32[]{:S(2)}) %collective-permute-start.16) | collective-permute-done | bytes 4128 | tf_op jit(solution)/shard_map/ppermute | solution.py:55
  182.9 2.4 collective-permute-start.20
  186.5 2.8 %collective-permute-done.19 = f32[1024]{0:T(1024)S(1)} collective-permute-done((f32[1024]{0:T(1024)S(1)}, f32[1024]{0:T(1024)S(1)}, u32[]{:S(2)}, u32[]{:S(2)}) %collective-permute-start.19) | collective-permute-done | bytes 4128 | tf_op jit(solution)/shard_map/ppermute | solution.py:55
  189.5 48.9 %all-gather.5.cloned.1.call-done = bf16[1024,6144]{0,1:T(8,128)(2,1)} async-done(((bf16[1024,192]{0,1:T(8,128)(2,1)}), bf16[1024,6144]{0,1:T(8,128)(2,1)}) %all-gather.5.cloned.1.call-update) | async-done | bytes 12582928 | tf_op jit(solution)/shard_map/all_gather | solution.py:171
  238.4 6.9 %fusion.16 = f32[288,1024]{1,0:T(8,128)S(1)} fusion(bf16[1024,6144]{0,1:T(8,128)(2,1)} %all-gather.5.cloned.1.call-done, bf16[1,288,6144]{2,1,0:T(8,128)(2,1)S(1)} %copy-done, f32[1024]{0:T(1024)S(1)} %add_rsqrt_fusion), kind=kOutput, calls=%fused_computation.8 | convolution fusion | flops 3624173568 | bytes 17305600 | tf_op jit(solution)/shard_map/dot_general | solution.py:175
  245.4 1.2 copy-done.6
  246.6 1.0 copy-done.7
  247.6 4.8 %fusion.22 = bf16[1,288,1024]{2,1,0:T(8,128)(2,1)} fusion(bf16[1024,6144]{0,1:T(8,128)(2,1)S(1)} %copy-done.6, bf16[1,288,6144]{2,1,0:T(8,128)(2,1)S(1)} %copy-done.7, f32[288,1024]{1,0:T(8,128)S(1)} %fusion.16, f32[1024]{0:T(1024)S(1)} %add_rsqrt_fusion), kind=kOutput, calls=%fused_computation.10 | convolution fusion | flops 3625943040 | bytes 17895424 | tf_op jit(solution)/shard_map/dot_general | solution.py:176
  (71 shorter events, 16.9 us)
Async XLA Ops:
  7.2 231.3 %copy-start = (bf16[1,288,6144]{2,1,0:T(8,128)(2,1)S(1)}, bf16[1,288,6144]{2,1,0:T(8,128)(2,1)}, u32[]{:S(2)}) copy-start(bf16[1,288,6144]{2,1,0:T(8,128)(2,1)} %param.16) | copy-start | bytes 10616836
  7.2 102.0 %all-gather.3.cloned.1.call-start = ((), (), s32[]{:S(2)}) async-start(), calls=%async_computation.2 | async-start | bytes 4325376 | tf_op jit(solution)/shard_map/all_gather | solution.py:136
  15.5 9.2 %collective-permute-start.6 = (f32[8,128,128]{2,1,0:T(8,128)}, f32[8,128,128]{2,1,0:T(8,128)}, u32[]{:S(2)}, u32[]{:S(2)}) collective-permute-start(f32[8,128,128]{2,1,0:T(8,128)} %fusion.47), channel_id=1, source_target_pairs={{0,8},{8,0},{1,9},{9,1},{2,10},{10,2},{3,11},{11,3},{4,12},{12,4},... | collective-permute-start | bytes 1572872 | tf_op jit(solution)/shard_map/ppermute | solution.py:48
  19.5 1.1 collective-permute-start
  20.3 28.9 %copy-start.3 = (bf16[64,1024]{1,0:T(8,128)(2,1)S(1)}, bf16[64,1024]{1,0:T(8,128)(2,1)}, u32[]{:S(2)}) copy-start(bf16[64,1024]{1,0:T(8,128)(2,1)} %param.10) | copy-start | bytes 393220
  20.3 28.9 %copy-start.8 = (bf16[64,1024]{1,0:T(8,128)(2,1)S(1)}, bf16[64,1024]{1,0:T(8,128)(2,1)}, u32[]{:S(2)}) copy-start(bf16[64,1024]{1,0:T(8,128)(2,1)} %param.9) | copy-start | bytes 393220
  21.4 8.4 %collective-permute-start.3 = (f32[4]{0:T(128)S(1)}, f32[4]{0:T(128)S(1)}, u32[]{:S(2)}, u32[]{:S(2)}) collective-permute-start(f32[4]{0:T(128)S(1)} %dynamic_slice.6), channel_id=1, source_target_pairs={{0,16},{16,32},{32,48},{48,0},{1,17},{17,33},{33,49},{49,1},{2,18}... | collective-permute-start | bytes 56 | tf_op jit(solution)/shard_map/ppermute | solution.py:44
  21.4 10.3 %collective-permute-start.2 = (f32[4]{0:T(128)S(1)}, f32[4]{0:T(128)S(1)}, u32[]{:S(2)}, u32[]{:S(2)}) collective-permute-start(f32[4]{0:T(128)S(1)} %dynamic_slice.6), channel_id=1, source_target_pairs={{0,32},{16,48},{32,0},{48,16},{1,33},{17,49},{33,1},{49,17},{2,34}... | collective-permute-start | bytes 56 | tf_op jit(solution)/shard_map/ppermute | solution.py:44
  23.6 8.1 %collective-permute-start.1 = (f32[4]{0:T(128)S(1)}, f32[4]{0:T(128)S(1)}, u32[]{:S(2)}, u32[]{:S(2)}) collective-permute-start(f32[4]{0:T(128)S(1)} %dynamic_slice.6), channel_id=1, source_target_pairs={{0,48},{16,0},{32,16},{48,32},{1,49},{17,1},{33,17},{49,33},{2,50}... | collective-permute-start | bytes 56 | tf_op jit(solution)/shard_map/ppermute | solution.py:44
  25.8 0.8 copy-start.2
  27.8 6.7 %collective-permute-start.9 = (bf16[4,128,128]{2,1,0:T(8,128)(2,1)S(1)}, bf16[4,128,128]{2,1,0:T(8,128)(2,1)S(1)}, u32[]{:S(2)}, u32[]{:S(2)}) collective-permute-start(bf16[4,128,128]{2,1,0:T(8,128)(2,1)S(1)} %get-tuple-element.12), channel_id=1, source_target_pairs={{0,16},{16,32},{32,48},{48,0},{1,17},{17,33},{33,49},{49,1},{2,18}... | collective-permute-start | bytes 393224 | tf_op jit(solution)/shard_map/ppermute | solution.py:43
  28.2 7.0 %collective-permute-start.8 = (bf16[4,128,128]{2,1,0:T(8,128)(2,1)S(1)}, bf16[4,128,128]{2,1,0:T(8,128)(2,1)S(1)}, u32[]{:S(2)}, u32[]{:S(2)}) collective-permute-start(bf16[4,128,128]{2,1,0:T(8,128)(2,1)S(1)} %get-tuple-element.12), channel_id=1, source_target_pairs={{0,32},{16,48},{32,0},{48,16},{1,33},{17,49},{33,1},{49,17},{2,34}... | collective-permute-start | bytes 393224 | tf_op jit(solution)/shard_map/ppermute | solution.py:43
  29.7 6.3 %collective-permute-start.7 = (bf16[4,128,128]{2,1,0:T(8,128)(2,1)S(1)}, bf16[4,128,128]{2,1,0:T(8,128)(2,1)S(1)}, u32[]{:S(2)}, u32[]{:S(2)}) collective-permute-start(bf16[4,128,128]{2,1,0:T(8,128)(2,1)S(1)} %get-tuple-element.12), channel_id=1, source_target_pairs={{0,48},{16,0},{32,16},{48,32},{1,49},{17,1},{33,17},{49,33},{2,50}... | collective-permute-start | bytes 393224 | tf_op jit(solution)/shard_map/ppermute | solution.py:43
  31.8 9.8 %collective-permute-start.5 = (f32[4]{0:T(128)S(1)}, f32[4]{0:T(128)S(1)}, u32[]{:S(2)}, u32[]{:S(2)}) collective-permute-start(f32[4]{0:T(128)S(1)} %get-tuple-element.4), channel_id=1, source_target_pairs={{0,64},{64,128},{128,192},{192,0},{1,65},{65,129},{129,193},{193,1... | collective-permute-start | bytes 56 | tf_op jit(solution)/shard_map/ppermute | solution.py:44
  32.0 9.6 %collective-permute-start.4 = (f32[4]{0:T(128)S(1)}, f32[4]{0:T(128)S(1)}, u32[]{:S(2)}, u32[]{:S(2)}) collective-permute-start(f32[4]{0:T(128)S(1)} %get-tuple-element.4), channel_id=1, source_target_pairs={{0,128},{64,192},{128,0},{192,64},{1,129},{65,193},{129,1},{193,65... | collective-permute-start | bytes 56 | tf_op jit(solution)/shard_map/ppermute | solution.py:44
  36.5 5.1 %collective-permute-start.12 = (bf16[4,128,128]{2,1,0:T(8,128)(2,1)S(1)}, bf16[4,128,128]{2,1,0:T(8,128)(2,1)S(1)}, u32[]{:S(2)}, u32[]{:S(2)}) collective-permute-start(bf16[4,128,128]{2,1,0:T(8,128)(2,1)S(1)} %fusion.40), channel_id=1, source_target_pairs={{0,64},{64,128},{128,192},{192,0},{1,65},{65,129},{129,193},{193,1... | collective-permute-start | bytes 393224 | tf_op jit(solution)/shard_map/ppermute | solution.py:43
  38.0 6.3 %collective-permute-start.11 = (bf16[4,128,128]{2,1,0:T(8,128)(2,1)S(1)}, bf16[4,128,128]{2,1,0:T(8,128)(2,1)S(1)}, u32[]{:S(2)}, u32[]{:S(2)}) collective-permute-start(bf16[4,128,128]{2,1,0:T(8,128)(2,1)S(1)} %fusion.40), channel_id=1, source_target_pairs={{0,128},{64,192},{128,0},{192,64},{1,129},{65,193},{129,1},{193,65... | collective-permute-start | bytes 393224 | tf_op jit(solution)/shard_map/ppermute | solution.py:43
  40.4 4.5 %collective-permute-start.10 = (bf16[4,128,128]{2,1,0:T(8,128)(2,1)S(1)}, bf16[4,128,128]{2,1,0:T(8,128)(2,1)S(1)}, u32[]{:S(2)}, u32[]{:S(2)}) collective-permute-start(bf16[4,128,128]{2,1,0:T(8,128)(2,1)S(1)} %fusion.40), channel_id=1, source_target_pairs={{0,192},{64,0},{128,64},{192,128},{1,193},{65,1},{129,65},{193,129... | collective-permute-start | bytes 393224 | tf_op jit(solution)/shard_map/ppermute | solution.py:43
  46.0 6.2 %collective-permute-start.13 = (f32[4,128,128]{2,1,0:T(8,128)}, f32[4,128,128]{2,1,0:T(8,128)}, u32[]{:S(2)}, u32[]{:S(2)}) collective-permute-start(f32[4,128,128]{2,1,0:T(8,128)} %fusion.42), channel_id=1, source_target_pairs={{0,8},{8,0},{1,9},{9,1},{2,10},{10,2},{3,11},{11,3},{4,12},{12,4},... | collective-permute-start | bytes 786440 | tf_op jit(solution)/shard_map/ppermute | solution.py:48
  55.3 59.0 %copy-start.5 = (s32[256,2]{0,1:T(2,128)S(1)}, s32[256,2]{0,1:T(2,128)}, u32[]{:S(2)}) copy-start(s32[256,2]{0,1:T(2,128)} %param.15) | copy-start | bytes 6148
  55.3 94.6 %reduce-scatter.2.cloned.1.call-start = ((), (), s32[]{:S(2)}) async-start(), calls=%async_computation.3 | async-start | bytes 1769472 | tf_op jit(solution)/shard_map/reduce_scatter | solution.py:138
  114.2 124.2 %all-gather.5.cloned.1.call-start = ((), (), s32[]{:S(2)}) async-start(), calls=%async_computation.4 | async-start | bytes 12976128 | tf_op jit(solution)/shard_map/all_gather | solution.py:171
  150.9 0.6 copy-start.4
  167.4 0.8 copy-start.1
  170.1 6.1 %collective-permute-start.14 = (f32[1024]{0:T(1024)S(1)}, f32[1024]{0:T(1024)S(1)}, u32[]{:S(2)}, u32[]{:S(2)}) collective-permute-start(f32[1024]{0:T(1024)S(1)} %fusion.29), channel_id=1, source_target_pairs={{0,8},{8,0},{1,9},{9,1},{2,10},{10,2},{3,11},{11,3},{4,12},{12,4},... | collective-permute-start | bytes 12296 | tf_op jit(solution)/shard_map/ppermute | solution.py:55
  176.2 3.6 %collective-permute-start.17 = (f32[1024]{0:T(1024)S(1)}, f32[1024]{0:T(1024)S(1)}, u32[]{:S(2)}, u32[]{:S(2)}) collective-permute-start(f32[1024]{0:T(1024)S(1)} %add.115), channel_id=1, source_target_pairs={{0,48},{16,0},{32,16},{48,32},{1,49},{17,1},{33,17},{49,33},{2,50}... | collective-permute-start | bytes 12296 | tf_op jit(solution)/shard_map/ppermute | solution.py:55
  178.6 4.0 %collective-permute-start.16 = (f32[1024]{0:T(1024)S(1)}, f32[1024]{0:T(1024)S(1)}, u32[]{:S(2)}, u32[]{:S(2)}) collective-permute-start(f32[1024]{0:T(1024)S(1)} %add.115), channel_id=1, source_target_pairs={{0,32},{16,48},{32,0},{48,16},{1,33},{17,49},{33,1},{49,17},{2,34}... | collective-permute-start | bytes 12296 | tf_op jit(solution)/shard_map/ppermute | solution.py:55
  179.2 3.7 %collective-permute-start.15 = (f32[1024]{0:T(1024)S(1)}, f32[1024]{0:T(1024)S(1)}, u32[]{:S(2)}, u32[]{:S(2)}) collective-permute-start(f32[1024]{0:T(1024)S(1)} %add.115), channel_id=1, source_target_pairs={{0,16},{16,32},{32,48},{48,0},{1,17},{17,33},{33,49},{49,1},{2,18}... | collective-permute-start | bytes 12296 | tf_op jit(solution)/shard_map/ppermute | solution.py:55
  182.9 3.7 %collective-permute-start.20 = (f32[1024]{0:T(1024)S(1)}, f32[1024]{0:T(1024)S(1)}, u32[]{:S(2)}, u32[]{:S(2)}) collective-permute-start(f32[1024]{0:T(1024)S(1)} %add_add_fusion), channel_id=1, source_target_pairs={{0,192},{64,0},{128,64},{192,128},{1,193},{65,1},{129,65},{193,129... | collective-permute-start | bytes 12296 | tf_op jit(solution)/shard_map/ppermute | solution.py:55
  185.3 4.1 %collective-permute-start.19 = (f32[1024]{0:T(1024)S(1)}, f32[1024]{0:T(1024)S(1)}, u32[]{:S(2)}, u32[]{:S(2)}) collective-permute-start(f32[1024]{0:T(1024)S(1)} %add_add_fusion), channel_id=1, source_target_pairs={{0,128},{64,192},{128,0},{192,64},{1,129},{65,193},{129,1},{193,65... | collective-permute-start | bytes 12296 | tf_op jit(solution)/shard_map/ppermute | solution.py:55
  185.8 3.7 %collective-permute-start.18 = (f32[1024]{0:T(1024)S(1)}, f32[1024]{0:T(1024)S(1)}, u32[]{:S(2)}, u32[]{:S(2)}) collective-permute-start(f32[1024]{0:T(1024)S(1)} %add_add_fusion), channel_id=1, source_target_pairs={{0,64},{64,128},{128,192},{192,0},{1,65},{65,129},{129,193},{193,1... | collective-permute-start | bytes 12296 | tf_op jit(solution)/shard_map/ppermute | solution.py:55
  238.4 8.2 %copy-start.6 = (bf16[1024,6144]{0,1:T(8,128)(2,1)S(1)}, bf16[1024,6144]{0,1:T(8,128)(2,1)}, u32[]{:S(2)}) copy-start(bf16[1024,6144]{0,1:T(8,128)(2,1)} %all-gather.5.cloned.1.call-done) | copy-start | bytes 37748740
  238.4 9.2 %copy-start.7 = (bf16[1,288,6144]{2,1,0:T(8,128)(2,1)S(1)}, bf16[1,288,6144]{2,1,0:T(8,128)(2,1)}, u32[]{:S(2)}) copy-start(bf16[1,288,6144]{2,1,0:T(8,128)(2,1)} %param.17) | copy-start | bytes 10616836
Sparse Core Ops, SparseCore 0:
  55.4 53.7 all-gather.2
  114.3 35.5 reduce-scatter.1
  169.1 69.2 all-gather.4

commit v5 on v4

--- a/solution.py
+++ b/solution.py
@@ -136,11 +136,11 @@
     gathered = lax.all_gather(normed, SEQ, axis=0, tiled=True)
     row_block = gathered
     attended = lax.psum_scatter(
-        jnp.dot(row_block, out_weight, preferred_element_type=jnp.float32),
+        lax.dot_general(out_weight, row_block, (((0,), (1,)), ((), ())), preferred_element_type=jnp.float32),
         "exp",
-        scatter_dimension=0,
+        scatter_dimension=1,
         tiled=True,
-    )
+    ).T
     residual_out = (residual.astype(jnp.float32) + attended).astype(jnp.bfloat16)
     group_rows = routes.shape[0]
     choices_each = routes.shape[1]
@@ -172,8 +172,10 @@
     squares = jnp.einsum("rd,rd->r", slices, slices, preferred_element_type=jnp.float32)
     for axis in reversed(SEQ):
         squares = ring_sum(squares, axis)
-    gate_sum = lax.dot_general(w_gate, row_block, contract_last, preferred_element_type=jnp.float32)
-    up_sum = lax.dot_general(w_up, row_block, contract_last, preferred_element_type=jnp.float32)
+    both = lax.dot_general(
+        jnp.concatenate([w_gate, w_up], 0), row_block, contract_last, preferred_element_type=jnp.float32
+    )
+    gate_sum, up_sum = (both[:hidden_rows], both[hidden_rows:])
     expert_hidden = finish_rows(gate_sum, up_sum, squares).reshape(hidden_rows, sources, entries)
     return (residual_out, expert_hidden.reshape(1, hidden_rows, experts * capacity))
 

time: 260 us -> 245 us (0.942)
  local copies, waits for them, and re-layouts: 17.6 us -> 2.99 us
  waiting for transfers between devices: 138 us -> 151 us
  other arithmetic: 15.9 us -> 5.59 us
  matrix products: 24 us -> 20.8 us
    reduce_scatter x1, waiting for transfers between devices: 23.3 us -> 33.4 us  [body(): lax.psum_scatter(lax.dot_general(out_weight, row_block, (((0,), (1,)), ((...]
    unnamed x20 -> x16, local copies, waits for them, and re-layouts: 6.8 us -> 1.04 us
    dot_general x3 -> x2, matrix products: 16.7 us -> 17.4 us  [the longest x1 12.5 us: body(): lax.dot_general(jnp.concatenate([w_gate, w_up], 0), row_block, contract_l...]
  transfers between devices with their start and end apart: 24 -> 24, of which waited for: 13 -> 14; matrix products, arithmetic and copies ran while one was open for 8% -> 2% of each run, Pallas kernels for 0% -> 0%
where the time goes in v5:
time: 245 us; the launch traced here: 244 us
  waiting for transfers between devices  151 us (62%)
  starting transfers between devices  34.6 us (14%)
  matrix products  20.8 us (8%)
  blocking collectives  15.4 us (6%)
  between operations  14 us (6%)
  other arithmetic  5.59 us (2%)
  local copies, waits for them, and re-layouts  2.99 us (1%)
    all_gather x1, waiting for transfers between devices, body(): gathered = lax.all_gather(normed, SEQ, axis=0, tiled=True)  54 us
    all_gather x1, waiting for transfers between devices, body(): row_block = lax.all_gather(slices, SEQ, axis=1, tiled=True)  49.5 us
    reduce_scatter x1, waiting for transfers between devices, body(): lax.psum_scatter(lax.dot_general(out_weight, row_block, (((0,), (1,)), ((...  33.4 us
    all_to_all x1, blocking collectives, body(): lax.all_to_all(buffer.reshape(experts, capacity, columns), 'exp', split_a...  15.4 us
    dot_general x1, matrix products, body(): lax.dot_general(jnp.concatenate([w_gate, w_up], 0), row_block, contract_l...  12.5 us
    ppermute x7, starting transfers between devices, ring_sum(): lax.ppermute(part, axis, [(i, (i + d) % peers) for i in range(peers)])  12.4 us
    ppermute x6, starting transfers between devices, send(): moved = lax.ppermute(state.astype(jnp.bfloat16), axis, perm)  9.05 us
    ppermute x7, waiting for transfers between devices, ring_sum(): lax.ppermute(part, axis, [(i, (i + d) % peers) for i in range(peers)])  7.37 us
  transfers between devices with their start and end apart: 24, of which 14 were waited for; matrix products, arithmetic and copies ran while one was open for 2% of the time, Pallas kernels for 0%

profile of v5, /device:TPU:1, one launch (start us, length us, event | category | flops | bytes accessed | tf_op | source)
XLA Modules:
  0.0 244.3 jit_solution(11798377388783028705)
XLA Ops:
  7.3 0.9 copy.85
  8.3 1.7 fusion.29
  10.0 3.3 %collective-permute-start.6 = (f32[8,128,128]{2,1,0:T(8,128)S(1)}, f32[8,128,128]{2,1,0:T(8,128)S(1)}, u32[]{:S(2)}, u32[]{:S(2)}) collective-permute-start(f32[8,128,128]{2,1,0:T(8,128)S(1)} %fusion.29), channel_id=1, source_target_pairs={{0,8},{8,0},{1,9},{9,1},{2,10},{10,2},{3,11},{11,3},{4,12},{12,4},... | collective-permute-start | bytes 1572872 | tf_op jit(solution)/shard_map/ppermute | solution.py:48
  13.5 1.3 collective-permute-done
  14.9 2.2 collective-permute-start.2
  17.1 1.1 collective-permute-start.1
  18.4 0.5 collective-permute-start.9
  18.9 1.5 collective-permute-start.8
  20.4 2.0 collective-permute-start.7
  22.5 0.3 collective-permute-start.5
  22.7 2.5 %collective-permute-start.4 = (f32[4]{0:T(128)S(1)}, f32[4]{0:T(128)S(1)}, u32[]{:S(2)}, u32[]{:S(2)}) collective-permute-start(f32[4]{0:T(128)S(1)} %get-tuple-element.4), channel_id=1, source_target_pairs={{0,128},{64,192},{128,0},{192,64},{1,129},{65,193},{129,1},{193,65... | collective-permute-start | bytes 56 | tf_op jit(solution)/shard_map/ppermute | solution.py:44
  25.2 0.8 collective-permute-done.8
  25.9 0.7 collective-permute-done.7
  26.6 0.5 fusion.22
  27.1 1.5 collective-permute-start.12
  28.6 2.5 %collective-permute-start.11 = (bf16[4,128,128]{2,1,0:T(8,128)(2,1)S(1)}, bf16[4,128,128]{2,1,0:T(8,128)(2,1)S(1)}, u32[]{:S(2)}, u32[]{:S(2)}) collective-permute-start(bf16[4,128,128]{2,1,0:T(8,128)(2,1)S(1)} %fusion.22), channel_id=1, source_target_pairs={{0,128},{64,192},{128,0},{192,64},{1,129},{65,193},{129,1},{193,65... | collective-permute-start | bytes 393224 | tf_op jit(solution)/shard_map/ppermute | solution.py:43
  31.1 1.2 collective-permute-start.10
  32.2 2.7 %collective-permute-done.11 = bf16[4,128,128]{2,1,0:T(8,128)(2,1)S(1)} collective-permute-done((bf16[4,128,128]{2,1,0:T(8,128)(2,1)S(1)}, bf16[4,128,128]{2,1,0:T(8,128)(2,1)S(1)}, u32[]{:S(2)}, u32[]{:S(2)}) %collective-permute-start.11) | collective-permute-done | bytes 131104 | tf_op jit(solution)/shard_map/ppermute | solution.py:43
  34.9 0.6 collective-permute-done.10
  35.5 0.4 fusion.24
  35.9 3.6 %collective-permute-start.13 = (f32[4,128,128]{2,1,0:T(8,128)S(1)}, f32[4,128,128]{2,1,0:T(8,128)S(1)}, u32[]{:S(2)}, u32[]{:S(2)}) collective-permute-start(f32[4,128,128]{2,1,0:T(8,128)S(1)} %fusion.24), channel_id=1, source_target_pairs={{0,8},{8,0},{1,9},{9,1},{2,10},{10,2},{3,11},{11,3},{4,12},{12,4},... | collective-permute-start | bytes 786440 | tf_op jit(solution)/shard_map/ppermute | solution.py:48
  39.8 0.3 convolution_bitcast_fusion.1
  40.0 0.6 collective-permute-done.13
  40.6 0.8 multiply_reduce_fusion
  41.5 0.8 copy_bitcast_fusion.2
  42.4 54.0 %all-gather.3.cloned.1.call-done = bf16[2048,1024]{1,0:T(8,128)(2,1)} async-done(((bf16[64,1024]{1,0:T(8,128)(2,1)}), bf16[2048,1024]{1,0:T(8,128)(2,1)}) %all-gather.3.cloned.1.call-update) | async-done | bytes 4194320 | tf_op jit(solution)/shard_map/all_gather | solution.py:136
  96.3 4.9 %convolution_bitcast_fusion = f32[192,2048]{1,0:T(8,128)} fusion(bf16[2048,1024]{1,0:T(8,128)(2,1)} %all-gather.3.cloned.1.call-done, bf16[1024,192]{0,1:T(8,128)(2,1)S(1)} %copy-done), kind=kOutput, calls=%fused_computation.4 | convolution fusion | flops 805306368 | bytes 6160384 | tf_op jit(solution)/shard_map/dot_general | solution.py:139
  101.8 1.1 reduce-window.6
  103.5 33.4 %reduce-scatter.2.cloned.1.call-done = f32[192,256]{1,0:T(8,128)} async-done(((f32[192,2048]{1,0:T(8,128)}), f32[192,256]{1,0:T(8,128)}) %reduce-scatter.2.cloned.1.call-update) | async-done | bytes 196624 | tf_op jit(solution)/shard_map/reduce_scatter | solution.py:138
  137.0 0.9 fusion.33
  137.9 0.4 fusion.4
  138.4 15.4 %all_to_all.5 = bf16[8,128,192]{1,2,0:T(8,128)(2,1)S(1)} all-to-all(bf16[8,128,192]{1,2,0:T(8,128)(2,1)S(1)} %bitcast.101), channel_id=1, replica_groups=mesh['seq_0'=4,'seq_1'=4,'seq_2'=2,'exp'=8] {'exp'}, dimensions={0} | all-to-all | bytes 786432 | tf_op jit(solution)/shard_map/all_to_all | solution.py:166
  153.9 0.8 copy_bitcast_fusion
  154.8 5.2 %collective-permute-start.14 = (f32[1024]{0:T(1024)S(1)}, f32[1024]{0:T(1024)S(1)}, u32[]{:S(2)}, u32[]{:S(2)}) collective-permute-start(f32[1024]{0:T(1024)S(1)} %fusion.10), channel_id=1, source_target_pairs={{0,8},{8,0},{1,9},{9,1},{2,10},{10,2},{3,11},{11,3},{4,12},{12,4},... | collective-permute-start | bytes 12296 | tf_op jit(solution)/shard_map/ppermute | solution.py:55
  160.0 0.8 collective-permute-done.14
  160.9 2.5 %collective-permute-start.17 = (f32[1024]{0:T(1024)S(1)}, f32[1024]{0:T(1024)S(1)}, u32[]{:S(2)}, u32[]{:S(2)}) collective-permute-start(f32[1024]{0:T(1024)S(1)} %add.115), channel_id=1, source_target_pairs={{0,48},{16,0},{32,16},{48,32},{1,49},{17,1},{33,17},{49,33},{2,50}... | collective-permute-start | bytes 12296 | tf_op jit(solution)/shard_map/ppermute | solution.py:55
  163.3 0.5 collective-permute-start.16
  163.8 0.6 collective-permute-start.15
  164.5 2.8 %collective-permute-done.16 = f32[1024]{0:T(1024)S(1)} collective-permute-done((f32[1024]{0:T(1024)S(1)}, f32[1024]{0:T(1024)S(1)}, u32[]{:S(2)}, u32[]{:S(2)}) %collective-permute-start.16) | collective-permute-done | bytes 4128 | tf_op jit(solution)/shard_map/ppermute | solution.py:55
  167.3 0.2 collective-permute-done.15
  167.5 2.5 %collective-permute-start.20 = (f32[1024]{0:T(1024)S(1)}, f32[1024]{0:T(1024)S(1)}, u32[]{:S(2)}, u32[]{:S(2)}) collective-permute-start(f32[1024]{0:T(1024)S(1)} %add_add_fusion), channel_id=1, source_target_pairs={{0,192},{64,0},{128,64},{192,128},{1,193},{65,1},{129,65},{193,129... | collective-permute-start | bytes 12296 | tf_op jit(solution)/shard_map/ppermute | solution.py:55
  170.0 0.5 collective-permute-start.19
  170.5 0.6 collective-permute-start.18
  171.1 3.0 %collective-permute-done.19 = f32[1024]{0:T(1024)S(1)} collective-permute-done((f32[1024]{0:T(1024)S(1)}, f32[1024]{0:T(1024)S(1)}, u32[]{:S(2)}, u32[]{:S(2)}) %collective-permute-start.19) | collective-permute-done | bytes 4128 | tf_op jit(solution)/shard_map/ppermute | solution.py:55
  174.1 0.5 collective-permute-done.18
  174.6 49.5 %all-gather.5.cloned.1.call-done = bf16[1024,6144]{0,1:T(8,128)(2,1)} async-done(((bf16[1024,192]{0,1:T(8,128)(2,1)}), bf16[1024,6144]{0,1:T(8,128)(2,1)}) %all-gather.5.cloned.1.call-update) | async-done | bytes 12582928 | tf_op jit(solution)/shard_map/all_gather | solution.py:171
  224.1 12.5 %fusion = f32[576,1024]{1,0:T(8,128)S(1)} fusion(bf16[1024,6144]{0,1:T(8,128)(2,1)} %all-gather.5.cloned.1.call-done, bf16[288,6144]{1,0:T(8,128)(2,1)} %bitcast.105, bf16[288,6144]{1,0:T(8,128)(2,1)} %bitcast.106), kind=kOutput, calls=%fused_computation | convolution fusion | flops 7261913088 | bytes 22020096 | tf_op jit(solution)/shard_map/dot_general | solution.py:175
  236.6 1.2 fusion.11
  (67 shorter events, 2.5 us)
Async XLA Ops:
  7.2 89.2 %copy-start = (bf16[1024,192]{0,1:T(8,128)(2,1)S(1)}, bf16[1024,192]{0,1:T(8,128)(2,1)}, u32[]{:S(2)}) copy-start(bf16[1024,192]{0,1:T(8,128)(2,1)} %param.13) | copy-start | bytes 1179652
  7.2 32.6 %copy-start.1 = (bf16[64,1024]{1,0:T(8,128)(2,1)S(1)}, bf16[64,1024]{1,0:T(8,128)(2,1)}, u32[]{:S(2)}) copy-start(bf16[64,1024]{1,0:T(8,128)(2,1)} %param.11) | copy-start | bytes 393220
  7.2 32.3 %copy-start.2 = (bf16[64,1024]{1,0:T(8,128)(2,1)S(1)}, bf16[64,1024]{1,0:T(8,128)(2,1)}, u32[]{:S(2)}) copy-start(bf16[64,1024]{1,0:T(8,128)(2,1)} %param.10) | copy-start | bytes 393220
  7.2 32.3 %copy-start.6 = (bf16[64,1024]{1,0:T(8,128)(2,1)S(1)}, bf16[64,1024]{1,0:T(8,128)(2,1)}, u32[]{:S(2)}) copy-start(bf16[64,1024]{1,0:T(8,128)(2,1)} %param.9) | copy-start | bytes 393220
  7.2 89.1 %all-gather.3.cloned.1.call-start = ((), (), s32[]{:S(2)}) async-start(), calls=%async_computation.2 | async-start | bytes 4325376 | tf_op jit(solution)/shard_map/all_gather | solution.py:136
  10.0 8.3 %collective-permute-start.6 = (f32[8,128,128]{2,1,0:T(8,128)S(1)}, f32[8,128,128]{2,1,0:T(8,128)S(1)}, u32[]{:S(2)}, u32[]{:S(2)}) collective-permute-start(f32[8,128,128]{2,1,0:T(8,128)S(1)} %fusion.29), channel_id=1, source_target_pairs={{0,8},{8,0},{1,9},{9,1},{2,10},{10,2},{3,11},{11,3},{4,12},{12,4},... | collective-permute-start | bytes 1572872 | tf_op jit(solution)/shard_map/ppermute | solution.py:48
  13.3 1.5 collective-permute-start
  14.9 5.5 %collective-permute-start.3 = (f32[4]{0:T(128)S(1)}, f32[4]{0:T(128)S(1)}, u32[]{:S(2)}, u32[]{:S(2)}) collective-permute-start(f32[4]{0:T(128)S(1)} %dynamic_slice.6), channel_id=1, source_target_pairs={{0,16},{16,32},{32,48},{48,0},{1,17},{17,33},{33,49},{49,1},{2,18}... | collective-permute-start | bytes 56 | tf_op jit(solution)/shard_map/ppermute | solution.py:44
  14.9 7.4 %collective-permute-start.2 = (f32[4]{0:T(128)S(1)}, f32[4]{0:T(128)S(1)}, u32[]{:S(2)}, u32[]{:S(2)}) collective-permute-start(f32[4]{0:T(128)S(1)} %dynamic_slice.6), channel_id=1, source_target_pairs={{0,32},{16,48},{32,0},{48,16},{1,33},{17,49},{33,1},{49,17},{2,34}... | collective-permute-start | bytes 56 | tf_op jit(solution)/shard_map/ppermute | solution.py:44
  17.1 5.3 %collective-permute-start.1 = (f32[4]{0:T(128)S(1)}, f32[4]{0:T(128)S(1)}, u32[]{:S(2)}, u32[]{:S(2)}) collective-permute-start(f32[4]{0:T(128)S(1)} %dynamic_slice.6), channel_id=1, source_target_pairs={{0,48},{16,0},{32,16},{48,32},{1,49},{17,1},{33,17},{49,33},{2,50}... | collective-permute-start | bytes 56 | tf_op jit(solution)/shard_map/ppermute | solution.py:44
  18.4 6.7 %collective-permute-start.9 = (bf16[4,128,128]{2,1,0:T(8,128)(2,1)S(1)}, bf16[4,128,128]{2,1,0:T(8,128)(2,1)S(1)}, u32[]{:S(2)}, u32[]{:S(2)}) collective-permute-start(bf16[4,128,128]{2,1,0:T(8,128)(2,1)S(1)} %get-tuple-element.12), channel_id=1, source_target_pairs={{0,16},{16,32},{32,48},{48,0},{1,17},{17,33},{33,49},{49,1},{2,18}... | collective-permute-start | bytes 393224 | tf_op jit(solution)/shard_map/ppermute | solution.py:43
  18.9 7.0 %collective-permute-start.8 = (bf16[4,128,128]{2,1,0:T(8,128)(2,1)S(1)}, bf16[4,128,128]{2,1,0:T(8,128)(2,1)S(1)}, u32[]{:S(2)}, u32[]{:S(2)}) collective-permute-start(bf16[4,128,128]{2,1,0:T(8,128)(2,1)S(1)} %get-tuple-element.12), channel_id=1, source_target_pairs={{0,32},{16,48},{32,0},{48,16},{1,33},{17,49},{33,1},{49,17},{2,34}... | collective-permute-start | bytes 393224 | tf_op jit(solution)/shard_map/ppermute | solution.py:43
  20.4 6.2 %collective-permute-start.7 = (bf16[4,128,128]{2,1,0:T(8,128)(2,1)S(1)}, bf16[4,128,128]{2,1,0:T(8,128)(2,1)S(1)}, u32[]{:S(2)}, u32[]{:S(2)}) collective-permute-start(bf16[4,128,128]{2,1,0:T(8,128)(2,1)S(1)} %get-tuple-element.12), channel_id=1, source_target_pairs={{0,48},{16,0},{32,16},{48,32},{1,49},{17,1},{33,17},{49,33},{2,50}... | collective-permute-start | bytes 393224 | tf_op jit(solution)/shard_map/ppermute | solution.py:43
  22.5 9.8 %collective-permute-start.5 = (f32[4]{0:T(128)S(1)}, f32[4]{0:T(128)S(1)}, u32[]{:S(2)}, u32[]{:S(2)}) collective-permute-start(f32[4]{0:T(128)S(1)} %get-tuple-element.4), channel_id=1, source_target_pairs={{0,64},{64,128},{128,192},{192,0},{1,65},{65,129},{129,193},{193,1... | collective-permute-start | bytes 56 | tf_op jit(solution)/shard_map/ppermute | solution.py:44
  22.7 9.5 %collective-permute-start.4 = (f32[4]{0:T(128)S(1)}, f32[4]{0:T(128)S(1)}, u32[]{:S(2)}, u32[]{:S(2)}) collective-permute-start(f32[4]{0:T(128)S(1)} %get-tuple-element.4), channel_id=1, source_target_pairs={{0,128},{64,192},{128,0},{192,64},{1,129},{65,193},{129,1},{193,65... | collective-permute-start | bytes 56 | tf_op jit(solution)/shard_map/ppermute | solution.py:44
  27.1 5.1 %collective-permute-start.12 = (bf16[4,128,128]{2,1,0:T(8,128)(2,1)S(1)}, bf16[4,128,128]{2,1,0:T(8,128)(2,1)S(1)}, u32[]{:S(2)}, u32[]{:S(2)}) collective-permute-start(bf16[4,128,128]{2,1,0:T(8,128)(2,1)S(1)} %fusion.22), channel_id=1, source_target_pairs={{0,64},{64,128},{128,192},{192,0},{1,65},{65,129},{129,193},{193,1... | collective-permute-start | bytes 393224 | tf_op jit(solution)/shard_map/ppermute | solution.py:43
  28.6 6.3 %collective-permute-start.11 = (bf16[4,128,128]{2,1,0:T(8,128)(2,1)S(1)}, bf16[4,128,128]{2,1,0:T(8,128)(2,1)S(1)}, u32[]{:S(2)}, u32[]{:S(2)}) collective-permute-start(bf16[4,128,128]{2,1,0:T(8,128)(2,1)S(1)} %fusion.22), channel_id=1, source_target_pairs={{0,128},{64,192},{128,0},{192,64},{1,129},{65,193},{129,1},{193,65... | collective-permute-start | bytes 393224 | tf_op jit(solution)/shard_map/ppermute | solution.py:43
  31.1 4.4 %collective-permute-start.10 = (bf16[4,128,128]{2,1,0:T(8,128)(2,1)S(1)}, bf16[4,128,128]{2,1,0:T(8,128)(2,1)S(1)}, u32[]{:S(2)}, u32[]{:S(2)}) collective-permute-start(bf16[4,128,128]{2,1,0:T(8,128)(2,1)S(1)} %fusion.22), channel_id=1, source_target_pairs={{0,192},{64,0},{128,64},{192,128},{1,193},{65,1},{129,65},{193,129... | collective-permute-start | bytes 393224 | tf_op jit(solution)/shard_map/ppermute | solution.py:43
  35.9 4.8 %collective-permute-start.13 = (f32[4,128,128]{2,1,0:T(8,128)S(1)}, f32[4,128,128]{2,1,0:T(8,128)S(1)}, u32[]{:S(2)}, u32[]{:S(2)}) collective-permute-start(f32[4,128,128]{2,1,0:T(8,128)S(1)} %fusion.24), channel_id=1, source_target_pairs={{0,8},{8,0},{1,9},{9,1},{2,10},{10,2},{3,11},{11,3},{4,12},{12,4},... | collective-permute-start | bytes 786440 | tf_op jit(solution)/shard_map/ppermute | solution.py:48
  42.3 59.0 %copy-start.5 = (s32[256,2]{0,1:T(2,128)S(1)}, s32[256,2]{0,1:T(2,128)}, u32[]{:S(2)}) copy-start(s32[256,2]{0,1:T(2,128)} %param.15) | copy-start | bytes 6148
  42.3 94.7 %copy-start.3 = (bf16[256,192]{0,1:T(8,128)(2,1)S(1)}, bf16[256,192]{0,1:T(8,128)(2,1)}, u32[]{:S(2)}) copy-start(bf16[256,192]{0,1:T(8,128)(2,1)} %param.14) | copy-start | bytes 294916
  42.3 94.6 %reduce-scatter.2.cloned.1.call-start = ((), (), s32[]{:S(2)}) async-start(), calls=%async_computation.3 | async-start | bytes 1769472 | tf_op jit(solution)/shard_map/reduce_scatter | solution.py:138
  101.3 122.8 %all-gather.5.cloned.1.call-start = ((), (), s32[]{:S(2)}) async-start(), calls=%async_computation.4 | async-start | bytes 12976128 | tf_op jit(solution)/shard_map/all_gather | solution.py:171
  137.9 98.7 %copy-start.4 = (bf16[256,192]{0,1:T(8,128)(2,1)}, bf16[256,192]{0,1:T(8,128)(2,1)S(1)}, u32[]{:S(2)}) copy-start(bf16[256,192]{0,1:T(8,128)(2,1)S(1)} %fusion.33) | copy-start | bytes 294916
  154.8 6.1 %collective-permute-start.14 = (f32[1024]{0:T(1024)S(1)}, f32[1024]{0:T(1024)S(1)}, u32[]{:S(2)}, u32[]{:S(2)}) collective-permute-start(f32[1024]{0:T(1024)S(1)} %fusion.10), channel_id=1, source_target_pairs={{0,8},{8,0},{1,9},{9,1},{2,10},{10,2},{3,11},{11,3},{4,12},{12,4},... | collective-permute-start | bytes 12296 | tf_op jit(solution)/shard_map/ppermute | solution.py:55
  160.9 3.6 %collective-permute-start.17 = (f32[1024]{0:T(1024)S(1)}, f32[1024]{0:T(1024)S(1)}, u32[]{:S(2)}, u32[]{:S(2)}) collective-permute-start(f32[1024]{0:T(1024)S(1)} %add.115), channel_id=1, source_target_pairs={{0,48},{16,0},{32,16},{48,32},{1,49},{17,1},{33,17},{49,33},{2,50}... | collective-permute-start | bytes 12296 | tf_op jit(solution)/shard_map/ppermute | solution.py:55
  163.3 4.0 %collective-permute-start.16 = (f32[1024]{0:T(1024)S(1)}, f32[1024]{0:T(1024)S(1)}, u32[]{:S(2)}, u32[]{:S(2)}) collective-permute-start(f32[1024]{0:T(1024)S(1)} %add.115), channel_id=1, source_target_pairs={{0,32},{16,48},{32,0},{48,16},{1,33},{17,49},{33,1},{49,17},{2,34}... | collective-permute-start | bytes 12296 | tf_op jit(solution)/shard_map/ppermute | solution.py:55
  163.8 3.7 %collective-permute-start.15 = (f32[1024]{0:T(1024)S(1)}, f32[1024]{0:T(1024)S(1)}, u32[]{:S(2)}, u32[]{:S(2)}) collective-permute-start(f32[1024]{0:T(1024)S(1)} %add.115), channel_id=1, source_target_pairs={{0,16},{16,32},{32,48},{48,0},{1,17},{17,33},{33,49},{49,1},{2,18}... | collective-permute-start | bytes 12296 | tf_op jit(solution)/shard_map/ppermute | solution.py:55
  167.5 3.6 %collective-permute-start.20 = (f32[1024]{0:T(1024)S(1)}, f32[1024]{0:T(1024)S(1)}, u32[]{:S(2)}, u32[]{:S(2)}) collective-permute-start(f32[1024]{0:T(1024)S(1)} %add_add_fusion), channel_id=1, source_target_pairs={{0,192},{64,0},{128,64},{192,128},{1,193},{65,1},{129,65},{193,129... | collective-permute-start | bytes 12296 | tf_op jit(solution)/shard_map/ppermute | solution.py:55
  170.0 4.1 %collective-permute-start.19 = (f32[1024]{0:T(1024)S(1)}, f32[1024]{0:T(1024)S(1)}, u32[]{:S(2)}, u32[]{:S(2)}) collective-permute-start(f32[1024]{0:T(1024)S(1)} %add_add_fusion), channel_id=1, source_target_pairs={{0,128},{64,192},{128,0},{192,64},{1,129},{65,193},{129,1},{193,65... | collective-permute-start | bytes 12296 | tf_op jit(solution)/shard_map/ppermute | solution.py:55
  170.5 4.1 %collective-permute-start.18 = (f32[1024]{0:T(1024)S(1)}, f32[1024]{0:T(1024)S(1)}, u32[]{:S(2)}, u32[]{:S(2)}) collective-permute-start(f32[1024]{0:T(1024)S(1)} %add_add_fusion), channel_id=1, source_target_pairs={{0,64},{64,128},{128,192},{192,0},{1,65},{65,129},{129,193},{193,1... | collective-permute-start | bytes 12296 | tf_op jit(solution)/shard_map/ppermute | solution.py:55
Sparse Core Ops, SparseCore 0:
  42.4 53.8 all-gather.2
  101.4 35.5 reduce-scatter.1
  154.8 69.2 all-gather.4

commit v6 on v5

--- a/solution.py
+++ b/solution.py
@@ -38,14 +38,21 @@
     return (earlier[0] * later[0], later[0][:, None, None] * earlier[1] + later[1])
 
 
-def send(pair, axis, perm):
-    decay, state = pair
-    moved = lax.ppermute(state.astype(jnp.bfloat16), axis, perm)
-    return (lax.ppermute(decay, axis, perm), moved.astype(jnp.float32))
-
-
-def swap_cores(pair):
-    return jax.tree.map(lambda part: lax.ppermute(part, "seq_2", [(0, 1), (1, 0)]), pair)
+def ring_shifts(part, axis):
+    peers = lax.axis_size(axis)
+    return [part] + [
+        lax.ppermute(part, axis, [(i, (i + d) % peers) for i in range(peers)]) for d in range(1, peers)
+    ]
+
+
+def narrow_shifts(state, axis):
+    return [state] + [
+        moved.astype(jnp.float32) for moved in ring_shifts(state.astype(jnp.bfloat16), axis)[1:]
+    ]
+
+
+def swap_cores(part):
+    return lax.ppermute(part, "seq_2", [(0, 1), (1, 0)])
 
 
 def ring_sum(part, axis):
@@ -56,11 +63,9 @@
     return total
 
 
-def prefix_over(own, axis):
-    peers, place = (lax.axis_size(axis), lax.axis_index(axis))
-    shifted = [own] + [
-        send(own, axis, [(i, (i + d) % peers) for i in range(peers)]) for d in range(1, peers)
-    ]
+def prefix_over(shifted, place):
+    peers = len(shifted)
+    own = shifted[0]
     start = nothing_yet(own, (1.0, 0.0))
     before, after = (start, start)
     for d in range(1, peers):
@@ -76,22 +81,31 @@
 
 def entering_state(decay, state):
     core = lax.axis_index("seq_2")
-    other = swap_cores((decay, state))
-    first = jax.tree.map(lambda mine, theirs: jnp.where(core == 0, mine, theirs), (decay, state), other)
-    second = jax.tree.map(lambda mine, theirs: jnp.where(core == 0, theirs, mine), (decay, state), other)
-    chip = link_states(first, second)
     half = decay.shape[0] // 2
-    mine = jax.tree.map(lambda part: lax.dynamic_slice_in_dim(part, core * half, half, 0), chip)
-    along_y, row = prefix_over(mine, "seq_1")
-    along_x, _ = prefix_over(row, "seq_0")
-    chip_before = link_states(along_x, along_y)
+    other_decay = swap_cores(decay)
+    first_decay = jnp.where(core == 0, decay, other_decay)
+    second_decay = jnp.where(core == 0, other_decay, decay)
+    mine_decay = lax.dynamic_slice_in_dim(first_decay * second_decay, core * half, half, 0)
+    y_decays = ring_shifts(mine_decay, "seq_1")
+    row_decay = y_decays[0]
+    for part in y_decays[1:]:
+        row_decay = row_decay * part
+    x_decays = ring_shifts(row_decay, "seq_0")
+    other = swap_cores(state)
+    first = (first_decay, jnp.where(core == 0, state, other))
+    second = (second_decay, jnp.where(core == 0, other, state))
+    chip = link_states(first, second)[1]
+    mine = lax.dynamic_slice_in_dim(chip, core * half, half, 0)
+    y_states = narrow_shifts(mine, "seq_1")
+    along_y, row = prefix_over(list(zip(y_decays, y_states)), lax.axis_index("seq_1"))
+    x_states = narrow_shifts(row[1], "seq_0")
+    along_x, _ = prefix_over(list(zip(x_decays, x_states)), lax.axis_index("seq_0"))
+    chip_before = link_states(along_x, along_y)[1]
     theirs = swap_cores(chip_before)
-    whole = jax.tree.map(
-        lambda a, b: jnp.where(core == 0, jnp.concatenate([a, b], 0), jnp.concatenate([b, a], 0)),
-        chip_before,
-        theirs,
-    )
-    return jnp.where(core == 0, whole[1], first[0][:, None, None] * whole[1] + first[1])
+    whole = jnp.where(
+        core == 0, jnp.concatenate([chip_before, theirs], 0), jnp.concatenate([theirs, chip_before], 0)
+    )
+    return jnp.where(core == 0, whole, first[0][:, None, None] * whole + first[1])
 
 
 def finish_rows(gate_sum, up_sum, squares):

time: 245 us -> 245 us (level)
  no operation moved by 1% of the time
where the time goes in v6:
time: 245 us; the launch traced here: 244 us
  waiting for transfers between devices  151 us (62%)
  starting transfers between devices  34.6 us (14%)
  matrix products  20.8 us (8%)
  blocking collectives  15.4 us (6%)
  between operations  14 us (6%)
  other arithmetic  5.59 us (2%)
  local copies, waits for them, and re-layouts  2.99 us (1%)
    all_gather x1, waiting for transfers between devices, body(): gathered = lax.all_gather(normed, SEQ, axis=0, tiled=True)  54 us
    all_gather x1, waiting for transfers between devices, body(): row_block = lax.all_gather(slices, SEQ, axis=1, tiled=True)  49.5 us
    reduce_scatter x1, waiting for transfers between devices, body(): lax.psum_scatter(lax.dot_general(out_weight, row_block, (((0,), (1,)), ((...  33.4 us
    all_to_all x1, blocking collectives, body(): lax.all_to_all(buffer.reshape(experts, capacity, columns), 'exp', split_a...  15.4 us
    ppermute x11, starting transfers between devices, ring_shifts(): lax.ppermute(part, axis, [(i, (i + d) % peers) for i in range(peers)])  15 us
    dot_general x1, matrix products, body(): lax.dot_general(jnp.concatenate([w_gate, w_up], 0), row_block, contract_l...  12.5 us
    ppermute x7, starting transfers between devices, ring_sum(): lax.ppermute(part, axis, [(i, (i + d) % peers) for i in range(peers)])  12.4 us
    ppermute x7, waiting for transfers between devices, ring_sum(): lax.ppermute(part, axis, [(i, (i + d) % peers) for i in range(peers)])  7.37 us
  transfers between devices with their start and end apart: 24, of which 14 were waited for; matrix products, arithmetic and copies ran while one was open for 2% of the time, Pallas kernels for 0%

profile of v6, /device:TPU:1, one launch (start us, length us, event | category | flops | bytes accessed | tf_op | source)
XLA Modules:
  0.0 244.3 jit_solution(14135375985195706920)
XLA Ops:
  7.3 0.9 copy.85
  8.3 1.7 fusion.29
  10.0 3.3 %collective-permute-start.6 = (f32[8,128,128]{2,1,0:T(8,128)S(1)}, f32[8,128,128]{2,1,0:T(8,128)S(1)}, u32[]{:S(2)}, u32[]{:S(2)}) collective-permute-start(f32[8,128,128]{2,1,0:T(8,128)S(1)} %fusion.29), channel_id=1, source_target_pairs={{0,8},{8,0},{1,9},{9,1},{2,10},{10,2},{3,11},{11,3},{4,12},{12,4},... | collective-permute-start | bytes 1572872 | tf_op jit(solution)/shard_map/ppermute | solution.py:55
  13.5 1.3 collective-permute-done
  14.9 2.2 collective-permute-start.2
  17.1 1.1 collective-permute-start.1
  18.4 0.5 collective-permute-start.9
  18.9 1.5 collective-permute-start.8
  20.4 2.0 collective-permute-start.7
  22.5 0.3 collective-permute-start.5
  22.7 2.5 %collective-permute-start.4 = (f32[4]{0:T(128)S(1)}, f32[4]{0:T(128)S(1)}, u32[]{:S(2)}, u32[]{:S(2)}) collective-permute-start(f32[4]{0:T(128)S(1)} %get-tuple-element.16), channel_id=1, source_target_pairs={{0,128},{64,192},{128,0},{192,64},{1,129},{65,193},{129,1},{193,65... | collective-permute-start | bytes 56 | tf_op jit(solution)/shard_map/ppermute | solution.py:44
  25.2 0.8 collective-permute-done.8
  25.9 0.7 collective-permute-done.7
  26.6 0.5 fusion.22
  27.1 1.5 collective-permute-start.12
  28.6 2.5 %collective-permute-start.11 = (bf16[4,128,128]{2,1,0:T(8,128)(2,1)S(1)}, bf16[4,128,128]{2,1,0:T(8,128)(2,1)S(1)}, u32[]{:S(2)}, u32[]{:S(2)}) collective-permute-start(bf16[4,128,128]{2,1,0:T(8,128)(2,1)S(1)} %fusion.22), channel_id=1, source_target_pairs={{0,128},{64,192},{128,0},{192,64},{1,129},{65,193},{129,1},{193,65... | collective-permute-start | bytes 393224 | tf_op jit(solution)/shard_map/ppermute | solution.py:44
  31.1 1.2 collective-permute-start.10
  32.2 2.7 %collective-permute-done.11 = bf16[4,128,128]{2,1,0:T(8,128)(2,1)S(1)} collective-permute-done((bf16[4,128,128]{2,1,0:T(8,128)(2,1)S(1)}, bf16[4,128,128]{2,1,0:T(8,128)(2,1)S(1)}, u32[]{:S(2)}, u32[]{:S(2)}) %collective-permute-start.11) | collective-permute-done | bytes 131104 | tf_op jit(solution)/shard_map/ppermute | solution.py:44
  34.9 0.6 collective-permute-done.10
  35.5 0.4 fusion.24
  35.9 3.6 %collective-permute-start.13 = (f32[4,128,128]{2,1,0:T(8,128)S(1)}, f32[4,128,128]{2,1,0:T(8,128)S(1)}, u32[]{:S(2)}, u32[]{:S(2)}) collective-permute-start(f32[4,128,128]{2,1,0:T(8,128)S(1)} %fusion.24), channel_id=1, source_target_pairs={{0,8},{8,0},{1,9},{9,1},{2,10},{10,2},{3,11},{11,3},{4,12},{12,4},... | collective-permute-start | bytes 786440 | tf_op jit(solution)/shard_map/ppermute | solution.py:55
  39.8 0.3 convolution_bitcast_fusion.1
  40.0 0.6 collective-permute-done.13
  40.6 0.8 multiply_reduce_fusion
  41.5 0.8 copy_bitcast_fusion.2
  42.4 54.0 %all-gather.3.cloned.1.call-done = bf16[2048,1024]{1,0:T(8,128)(2,1)} async-done(((bf16[64,1024]{1,0:T(8,128)(2,1)}), bf16[2048,1024]{1,0:T(8,128)(2,1)}) %all-gather.3.cloned.1.call-update) | async-done | bytes 4194320 | tf_op jit(solution)/shard_map/all_gather | solution.py:150
  96.3 4.9 %convolution_bitcast_fusion = f32[192,2048]{1,0:T(8,128)} fusion(bf16[2048,1024]{1,0:T(8,128)(2,1)} %all-gather.3.cloned.1.call-done, bf16[1024,192]{0,1:T(8,128)(2,1)S(1)} %copy-done), kind=kOutput, calls=%fused_computation.4 | convolution fusion | flops 805306368 | bytes 6160384 | tf_op jit(solution)/shard_map/dot_general | solution.py:153
  101.8 1.1 reduce-window.6
  103.5 33.4 %reduce-scatter.2.cloned.1.call-done = f32[192,256]{1,0:T(8,128)} async-done(((f32[192,2048]{1,0:T(8,128)}), f32[192,256]{1,0:T(8,128)}) %reduce-scatter.2.cloned.1.call-update) | async-done | bytes 196624 | tf_op jit(solution)/shard_map/reduce_scatter | solution.py:152
  137.0 0.9 fusion.33
  137.9 0.4 fusion.4
  138.4 15.4 %all_to_all.5 = bf16[8,128,192]{1,2,0:T(8,128)(2,1)S(1)} all-to-all(bf16[8,128,192]{1,2,0:T(8,128)(2,1)S(1)} %bitcast.101), channel_id=1, replica_groups=mesh['seq_0'=4,'seq_1'=4,'seq_2'=2,'exp'=8] {'exp'}, dimensions={0} | all-to-all | bytes 786432 | tf_op jit(solution)/shard_map/all_to_all | solution.py:180
  153.9 0.8 copy_bitcast_fusion
  154.8 5.2 %collective-permute-start.14 = (f32[1024]{0:T(1024)S(1)}, f32[1024]{0:T(1024)S(1)}, u32[]{:S(2)}, u32[]{:S(2)}) collective-permute-start(f32[1024]{0:T(1024)S(1)} %fusion.10), channel_id=1, source_target_pairs={{0,8},{8,0},{1,9},{9,1},{2,10},{10,2},{3,11},{11,3},{4,12},{12,4},... | collective-permute-start | bytes 12296 | tf_op jit(solution)/shard_map/ppermute | solution.py:62
  160.0 0.8 collective-permute-done.14
  160.9 2.5 %collective-permute-start.17 = (f32[1024]{0:T(1024)S(1)}, f32[1024]{0:T(1024)S(1)}, u32[]{:S(2)}, u32[]{:S(2)}) collective-permute-start(f32[1024]{0:T(1024)S(1)} %add.115), channel_id=1, source_target_pairs={{0,48},{16,0},{32,16},{48,32},{1,49},{17,1},{33,17},{49,33},{2,50}... | collective-permute-start | bytes 12296 | tf_op jit(solution)/shard_map/ppermute | solution.py:62
  163.3 0.5 collective-permute-start.16
  163.8 0.6 collective-permute-start.15
  164.5 2.8 %collective-permute-done.16 = f32[1024]{0:T(1024)S(1)} collective-permute-done((f32[1024]{0:T(1024)S(1)}, f32[1024]{0:T(1024)S(1)}, u32[]{:S(2)}, u32[]{:S(2)}) %collective-permute-start.16) | collective-permute-done | bytes 4128 | tf_op jit(solution)/shard_map/ppermute | solution.py:62
  167.3 0.2 collective-permute-done.15
  167.5 2.5 %collective-permute-start.20 = (f32[1024]{0:T(1024)S(1)}, f32[1024]{0:T(1024)S(1)}, u32[]{:S(2)}, u32[]{:S(2)}) collective-permute-start(f32[1024]{0:T(1024)S(1)} %add_add_fusion), channel_id=1, source_target_pairs={{0,192},{64,0},{128,64},{192,128},{1,193},{65,1},{129,65},{193,129... | collective-permute-start | bytes 12296 | tf_op jit(solution)/shard_map/ppermute | solution.py:62
  170.0 0.5 collective-permute-start.19
  170.5 0.6 collective-permute-start.18
  171.1 3.0 %collective-permute-done.19 = f32[1024]{0:T(1024)S(1)} collective-permute-done((f32[1024]{0:T(1024)S(1)}, f32[1024]{0:T(1024)S(1)}, u32[]{:S(2)}, u32[]{:S(2)}) %collective-permute-start.19) | collective-permute-done | bytes 4128 | tf_op jit(solution)/shard_map/ppermute | solution.py:62
  174.1 0.5 collective-permute-done.18
  174.6 49.5 %all-gather.5.cloned.1.call-done = bf16[1024,6144]{0,1:T(8,128)(2,1)} async-done(((bf16[1024,192]{0,1:T(8,128)(2,1)}), bf16[1024,6144]{0,1:T(8,128)(2,1)}) %all-gather.5.cloned.1.call-update) | async-done | bytes 12582928 | tf_op jit(solution)/shard_map/all_gather | solution.py:185
  224.1 12.5 %fusion = f32[576,1024]{1,0:T(8,128)S(1)} fusion(bf16[1024,6144]{0,1:T(8,128)(2,1)} %all-gather.5.cloned.1.call-done, bf16[288,6144]{1,0:T(8,128)(2,1)} %bitcast.105, bf16[288,6144]{1,0:T(8,128)(2,1)} %bitcast.106), kind=kOutput, calls=%fused_computation | convolution fusion | flops 7261913088 | bytes 22020096 | tf_op jit(solution)/shard_map/dot_general | solution.py:189
  236.6 1.2 fusion.11
  (67 shorter events, 2.5 us)
Async XLA Ops:
  7.2 89.2 %copy-start = (bf16[1024,192]{0,1:T(8,128)(2,1)S(1)}, bf16[1024,192]{0,1:T(8,128)(2,1)}, u32[]{:S(2)}) copy-start(bf16[1024,192]{0,1:T(8,128)(2,1)} %param.13) | copy-start | bytes 1179652
  7.2 32.6 %copy-start.1 = (bf16[64,1024]{1,0:T(8,128)(2,1)S(1)}, bf16[64,1024]{1,0:T(8,128)(2,1)}, u32[]{:S(2)}) copy-start(bf16[64,1024]{1,0:T(8,128)(2,1)} %param.11) | copy-start | bytes 393220
  7.2 32.3 %copy-start.2 = (bf16[64,1024]{1,0:T(8,128)(2,1)S(1)}, bf16[64,1024]{1,0:T(8,128)(2,1)}, u32[]{:S(2)}) copy-start(bf16[64,1024]{1,0:T(8,128)(2,1)} %param.10) | copy-start | bytes 393220
  7.2 32.3 %copy-start.6 = (bf16[64,1024]{1,0:T(8,128)(2,1)S(1)}, bf16[64,1024]{1,0:T(8,128)(2,1)}, u32[]{:S(2)}) copy-start(bf16[64,1024]{1,0:T(8,128)(2,1)} %param.9) | copy-start | bytes 393220
  7.2 89.1 %all-gather.3.cloned.1.call-start = ((), (), s32[]{:S(2)}) async-start(), calls=%async_computation.2 | async-start | bytes 4325376 | tf_op jit(solution)/shard_map/all_gather | solution.py:150
  10.0 8.3 %collective-permute-start.6 = (f32[8,128,128]{2,1,0:T(8,128)S(1)}, f32[8,128,128]{2,1,0:T(8,128)S(1)}, u32[]{:S(2)}, u32[]{:S(2)}) collective-permute-start(f32[8,128,128]{2,1,0:T(8,128)S(1)} %fusion.29), channel_id=1, source_target_pairs={{0,8},{8,0},{1,9},{9,1},{2,10},{10,2},{3,11},{11,3},{4,12},{12,4},... | collective-permute-start | bytes 1572872 | tf_op jit(solution)/shard_map/ppermute | solution.py:55
  13.3 1.5 collective-permute-start
  14.9 5.5 %collective-permute-start.3 = (f32[4]{0:T(128)S(1)}, f32[4]{0:T(128)S(1)}, u32[]{:S(2)}, u32[]{:S(2)}) collective-permute-start(f32[4]{0:T(128)S(1)} %dynamic_slice.6), channel_id=1, source_target_pairs={{0,16},{16,32},{32,48},{48,0},{1,17},{17,33},{33,49},{49,1},{2,18}... | collective-permute-start | bytes 56 | tf_op jit(solution)/shard_map/ppermute | solution.py:44
  14.9 7.4 %collective-permute-start.2 = (f32[4]{0:T(128)S(1)}, f32[4]{0:T(128)S(1)}, u32[]{:S(2)}, u32[]{:S(2)}) collective-permute-start(f32[4]{0:T(128)S(1)} %dynamic_slice.6), channel_id=1, source_target_pairs={{0,32},{16,48},{32,0},{48,16},{1,33},{17,49},{33,1},{49,17},{2,34}... | collective-permute-start | bytes 56 | tf_op jit(solution)/shard_map/ppermute | solution.py:44
  17.1 5.3 %collective-permute-start.1 = (f32[4]{0:T(128)S(1)}, f32[4]{0:T(128)S(1)}, u32[]{:S(2)}, u32[]{:S(2)}) collective-permute-start(f32[4]{0:T(128)S(1)} %dynamic_slice.6), channel_id=1, source_target_pairs={{0,48},{16,0},{32,16},{48,32},{1,49},{17,1},{33,17},{49,33},{2,50}... | collective-permute-start | bytes 56 | tf_op jit(solution)/shard_map/ppermute | solution.py:44
  18.4 6.7 %collective-permute-start.9 = (bf16[4,128,128]{2,1,0:T(8,128)(2,1)S(1)}, bf16[4,128,128]{2,1,0:T(8,128)(2,1)S(1)}, u32[]{:S(2)}, u32[]{:S(2)}) collective-permute-start(bf16[4,128,128]{2,1,0:T(8,128)(2,1)S(1)} %get-tuple-element.10), channel_id=1, source_target_pairs={{0,16},{16,32},{32,48},{48,0},{1,17},{17,33},{33,49},{49,1},{2,18}... | collective-permute-start | bytes 393224 | tf_op jit(solution)/shard_map/ppermute | solution.py:44
  18.9 7.0 %collective-permute-start.8 = (bf16[4,128,128]{2,1,0:T(8,128)(2,1)S(1)}, bf16[4,128,128]{2,1,0:T(8,128)(2,1)S(1)}, u32[]{:S(2)}, u32[]{:S(2)}) collective-permute-start(bf16[4,128,128]{2,1,0:T(8,128)(2,1)S(1)} %get-tuple-element.10), channel_id=1, source_target_pairs={{0,32},{16,48},{32,0},{48,16},{1,33},{17,49},{33,1},{49,17},{2,34}... | collective-permute-start | bytes 393224 | tf_op jit(solution)/shard_map/ppermute | solution.py:44
  20.4 6.2 %collective-permute-start.7 = (bf16[4,128,128]{2,1,0:T(8,128)(2,1)S(1)}, bf16[4,128,128]{2,1,0:T(8,128)(2,1)S(1)}, u32[]{:S(2)}, u32[]{:S(2)}) collective-permute-start(bf16[4,128,128]{2,1,0:T(8,128)(2,1)S(1)} %get-tuple-element.10), channel_id=1, source_target_pairs={{0,48},{16,0},{32,16},{48,32},{1,49},{17,1},{33,17},{49,33},{2,50}... | collective-permute-start | bytes 393224 | tf_op jit(solution)/shard_map/ppermute | solution.py:44
  22.5 9.8 %collective-permute-start.5 = (f32[4]{0:T(128)S(1)}, f32[4]{0:T(128)S(1)}, u32[]{:S(2)}, u32[]{:S(2)}) collective-permute-start(f32[4]{0:T(128)S(1)} %get-tuple-element.16), channel_id=1, source_target_pairs={{0,64},{64,128},{128,192},{192,0},{1,65},{65,129},{129,193},{193,1... | collective-permute-start | bytes 56 | tf_op jit(solution)/shard_map/ppermute | solution.py:44
  22.7 9.5 %collective-permute-start.4 = (f32[4]{0:T(128)S(1)}, f32[4]{0:T(128)S(1)}, u32[]{:S(2)}, u32[]{:S(2)}) collective-permute-start(f32[4]{0:T(128)S(1)} %get-tuple-element.16), channel_id=1, source_target_pairs={{0,128},{64,192},{128,0},{192,64},{1,129},{65,193},{129,1},{193,65... | collective-permute-start | bytes 56 | tf_op jit(solution)/shard_map/ppermute | solution.py:44
  27.1 5.1 %collective-permute-start.12 = (bf16[4,128,128]{2,1,0:T(8,128)(2,1)S(1)}, bf16[4,128,128]{2,1,0:T(8,128)(2,1)S(1)}, u32[]{:S(2)}, u32[]{:S(2)}) collective-permute-start(bf16[4,128,128]{2,1,0:T(8,128)(2,1)S(1)} %fusion.22), channel_id=1, source_target_pairs={{0,64},{64,128},{128,192},{192,0},{1,65},{65,129},{129,193},{193,1... | collective-permute-start | bytes 393224 | tf_op jit(solution)/shard_map/ppermute | solution.py:44
  28.6 6.3 %collective-permute-start.11 = (bf16[4,128,128]{2,1,0:T(8,128)(2,1)S(1)}, bf16[4,128,128]{2,1,0:T(8,128)(2,1)S(1)}, u32[]{:S(2)}, u32[]{:S(2)}) collective-permute-start(bf16[4,128,128]{2,1,0:T(8,128)(2,1)S(1)} %fusion.22), channel_id=1, source_target_pairs={{0,128},{64,192},{128,0},{192,64},{1,129},{65,193},{129,1},{193,65... | collective-permute-start | bytes 393224 | tf_op jit(solution)/shard_map/ppermute | solution.py:44
  31.1 4.4 %collective-permute-start.10 = (bf16[4,128,128]{2,1,0:T(8,128)(2,1)S(1)}, bf16[4,128,128]{2,1,0:T(8,128)(2,1)S(1)}, u32[]{:S(2)}, u32[]{:S(2)}) collective-permute-start(bf16[4,128,128]{2,1,0:T(8,128)(2,1)S(1)} %fusion.22), channel_id=1, source_target_pairs={{0,192},{64,0},{128,64},{192,128},{1,193},{65,1},{129,65},{193,129... | collective-permute-start | bytes 393224 | tf_op jit(solution)/shard_map/ppermute | solution.py:44
  35.9 4.8 %collective-permute-start.13 = (f32[4,128,128]{2,1,0:T(8,128)S(1)}, f32[4,128,128]{2,1,0:T(8,128)S(1)}, u32[]{:S(2)}, u32[]{:S(2)}) collective-permute-start(f32[4,128,128]{2,1,0:T(8,128)S(1)} %fusion.24), channel_id=1, source_target_pairs={{0,8},{8,0},{1,9},{9,1},{2,10},{10,2},{3,11},{11,3},{4,12},{12,4},... | collective-permute-start | bytes 786440 | tf_op jit(solution)/shard_map/ppermute | solution.py:55
  42.3 59.0 %copy-start.5 = (s32[256,2]{0,1:T(2,128)S(1)}, s32[256,2]{0,1:T(2,128)}, u32[]{:S(2)}) copy-start(s32[256,2]{0,1:T(2,128)} %param.15) | copy-start | bytes 6148
  42.3 94.7 %copy-start.3 = (bf16[256,192]{0,1:T(8,128)(2,1)S(1)}, bf16[256,192]{0,1:T(8,128)(2,1)}, u32[]{:S(2)}) copy-start(bf16[256,192]{0,1:T(8,128)(2,1)} %param.14) | copy-start | bytes 294916
  42.3 94.6 %reduce-scatter.2.cloned.1.call-start = ((), (), s32[]{:S(2)}) async-start(), calls=%async_computation.3 | async-start | bytes 1769472 | tf_op jit(solution)/shard_map/reduce_scatter | solution.py:152
  101.3 122.8 %all-gather.5.cloned.1.call-start = ((), (), s32[]{:S(2)}) async-start(), calls=%async_computation.4 | async-start | bytes 12976128 | tf_op jit(solution)/shard_map/all_gather | solution.py:185
  137.9 98.7 %copy-start.4 = (bf16[256,192]{0,1:T(8,128)(2,1)}, bf16[256,192]{0,1:T(8,128)(2,1)S(1)}, u32[]{:S(2)}) copy-start(bf16[256,192]{0,1:T(8,128)(2,1)S(1)} %fusion.33) | copy-start | bytes 294916
  154.8 6.1 %collective-permute-start.14 = (f32[1024]{0:T(1024)S(1)}, f32[1024]{0:T(1024)S(1)}, u32[]{:S(2)}, u32[]{:S(2)}) collective-permute-start(f32[1024]{0:T(1024)S(1)} %fusion.10), channel_id=1, source_target_pairs={{0,8},{8,0},{1,9},{9,1},{2,10},{10,2},{3,11},{11,3},{4,12},{12,4},... | collective-permute-start | bytes 12296 | tf_op jit(solution)/shard_map/ppermute | solution.py:62
  160.9 3.6 %collective-permute-start.17 = (f32[1024]{0:T(1024)S(1)}, f32[1024]{0:T(1024)S(1)}, u32[]{:S(2)}, u32[]{:S(2)}) collective-permute-start(f32[1024]{0:T(1024)S(1)} %add.115), channel_id=1, source_target_pairs={{0,48},{16,0},{32,16},{48,32},{1,49},{17,1},{33,17},{49,33},{2,50}... | collective-permute-start | bytes 12296 | tf_op jit(solution)/shard_map/ppermute | solution.py:62
  163.3 4.0 %collective-permute-start.16 = (f32[1024]{0:T(1024)S(1)}, f32[1024]{0:T(1024)S(1)}, u32[]{:S(2)}, u32[]{:S(2)}) collective-permute-start(f32[1024]{0:T(1024)S(1)} %add.115), channel_id=1, source_target_pairs={{0,32},{16,48},{32,0},{48,16},{1,33},{17,49},{33,1},{49,17},{2,34}... | collective-permute-start | bytes 12296 | tf_op jit(solution)/shard_map/ppermute | solution.py:62
  163.8 3.7 %collective-permute-start.15 = (f32[1024]{0:T(1024)S(1)}, f32[1024]{0:T(1024)S(1)}, u32[]{:S(2)}, u32[]{:S(2)}) collective-permute-start(f32[1024]{0:T(1024)S(1)} %add.115), channel_id=1, source_target_pairs={{0,16},{16,32},{32,48},{48,0},{1,17},{17,33},{33,49},{49,1},{2,18}... | collective-permute-start | bytes 12296 | tf_op jit(solution)/shard_map/ppermute | solution.py:62
  167.5 3.6 %collective-permute-start.20 = (f32[1024]{0:T(1024)S(1)}, f32[1024]{0:T(1024)S(1)}, u32[]{:S(2)}, u32[]{:S(2)}) collective-permute-start(f32[1024]{0:T(1024)S(1)} %add_add_fusion), channel_id=1, source_target_pairs={{0,192},{64,0},{128,64},{192,128},{1,193},{65,1},{129,65},{193,129... | collective-permute-start | bytes 12296 | tf_op jit(solution)/shard_map/ppermute | solution.py:62
  170.0 4.1 %collective-permute-start.19 = (f32[1024]{0:T(1024)S(1)}, f32[1024]{0:T(1024)S(1)}, u32[]{:S(2)}, u32[]{:S(2)}) collective-permute-start(f32[1024]{0:T(1024)S(1)} %add_add_fusion), channel_id=1, source_target_pairs={{0,128},{64,192},{128,0},{192,64},{1,129},{65,193},{129,1},{193,65... | collective-permute-start | bytes 12296 | tf_op jit(solution)/shard_map/ppermute | solution.py:62
  170.5 4.1 %collective-permute-start.18 = (f32[1024]{0:T(1024)S(1)}, f32[1024]{0:T(1024)S(1)}, u32[]{:S(2)}, u32[]{:S(2)}) collective-permute-start(f32[1024]{0:T(1024)S(1)} %add_add_fusion), channel_id=1, source_target_pairs={{0,64},{64,128},{128,192},{192,0},{1,65},{65,129},{129,193},{193,1... | collective-permute-start | bytes 12296 | tf_op jit(solution)/shard_map/ppermute | solution.py:62
Sparse Core Ops, SparseCore 0:
  42.4 53.8 all-gather.2
  101.4 35.5 reduce-scatter.1
  154.8 69.2 all-gather.4

commit v7 on v6

--- a/solution.py
+++ b/solution.py
@@ -45,10 +45,24 @@
     ]
 
 
-def narrow_shifts(state, axis):
-    return [state] + [
-        moved.astype(jnp.float32) for moved in ring_shifts(state.astype(jnp.bfloat16), axis)[1:]
-    ]
+def packed_shifts(decay, state, axis):
+    heads, rows, cols = state.shape
+    high = decay.astype(jnp.bfloat16)
+    low = (decay - high.astype(jnp.float32)).astype(jnp.bfloat16)
+    tail = jnp.concatenate(
+        [
+            jnp.broadcast_to(high[:, None, None], (heads, 1, cols)),
+            jnp.broadcast_to(low[:, None, None], (heads, 1, cols)),
+            jnp.zeros((heads, 6, cols), jnp.bfloat16),
+        ],
+        axis=1,
+    )
+    packed = jnp.concatenate([state.astype(jnp.bfloat16), tail], axis=1)
+    pieces = [(decay, state)]
+    for moved in ring_shifts(packed, axis)[1:]:
+        whole = moved.astype(jnp.float32)
+        pieces.append((whole[:, rows, 0] + whole[:, rows + 1, 0], whole[:, :rows]))
+    return pieces
 
 
 def swap_cores(part):
@@ -82,24 +96,13 @@
 def entering_state(decay, state):
     core = lax.axis_index("seq_2")
     half = decay.shape[0] // 2
-    other_decay = swap_cores(decay)
-    first_decay = jnp.where(core == 0, decay, other_decay)
-    second_decay = jnp.where(core == 0, other_decay, decay)
-    mine_decay = lax.dynamic_slice_in_dim(first_decay * second_decay, core * half, half, 0)
-    y_decays = ring_shifts(mine_decay, "seq_1")
-    row_decay = y_decays[0]
-    for part in y_decays[1:]:
-        row_decay = row_decay * part
-    x_decays = ring_shifts(row_decay, "seq_0")
-    other = swap_cores(state)
-    first = (first_decay, jnp.where(core == 0, state, other))
-    second = (second_decay, jnp.where(core == 0, other, state))
-    chip = link_states(first, second)[1]
-    mine = lax.dynamic_slice_in_dim(chip, core * half, half, 0)
-    y_states = narrow_shifts(mine, "seq_1")
-    along_y, row = prefix_over(list(zip(y_decays, y_states)), lax.axis_index("seq_1"))
-    x_states = narrow_shifts(row[1], "seq_0")
-    along_x, _ = prefix_over(list(zip(x_decays, x_states)), lax.axis_index("seq_0"))
+    other = (swap_cores(decay), swap_cores(state))
+    first = jax.tree.map(lambda mine, theirs: jnp.where(core == 0, mine, theirs), (decay, state), other)
+    second = jax.tree.map(lambda mine, theirs: jnp.where(core == 0, theirs, mine), (decay, state), other)
+    chip = link_states(first, second)
+    mine = jax.tree.map(lambda part: lax.dynamic_slice_in_dim(part, core * half, half, 0), chip)
+    along_y, row = prefix_over(packed_shifts(*mine, "seq_1"), lax.axis_index("seq_1"))
+    along_x, _ = prefix_over(packed_shifts(*row, "seq_0"), lax.axis_index("seq_0"))
     chip_before = link_states(along_x, along_y)[1]
     theirs = swap_cores(chip_before)
     whole = jnp.where(

time: 245 us -> 241 us (0.984)
  starting transfers between devices: 34.6 us -> 25.5 us
  waiting for transfers between devices: 151 us -> 156 us
    ppermute x11 -> x6, starting transfers between devices: 15 us -> 7.48 us  [ring_shifts(): lax.ppermute(part, axis, [(i, (i + d) % peers) for i in range(peers)])]
    ppermute x11 -> x6, waiting for transfers between devices: 4.72 us -> 10.8 us  [ring_shifts(): lax.ppermute(part, axis, [(i, (i + d) % peers) for i in range(peers)])]
  transfers between devices with their start and end apart: 24 -> 19, of which waited for: 14 -> 15; matrix products, arithmetic and copies ran while one was open for 2% -> 2% of each run, Pallas kernels for 0% -> 0%
where the time goes in v7:
time: 241 us
  waiting for transfers between devices  156 us (65%)
  starting transfers between devices  25.5 us (11%)
  matrix products  20.7 us (9%)
  blocking collectives  15.6 us (6%)
  between operations  14 us (6%)
  other arithmetic  5.92 us (2%)
  local copies, waits for them, and re-layouts  3.24 us (1%)
    all_gather x1, waiting for transfers between devices, body(): gathered = lax.all_gather(normed, SEQ, axis=0, tiled=True)  52.7 us
    all_gather x1, waiting for transfers between devices, body(): row_block = lax.all_gather(slices, SEQ, axis=1, tiled=True)  49.3 us
    reduce_scatter x1, waiting for transfers between devices, body(): lax.psum_scatter(lax.dot_general(out_weight, row_block, (((0,), (1,)), ((...  33.4 us
    all_to_all x1, blocking collectives, body(): lax.all_to_all(buffer.reshape(experts, capacity, columns), 'exp', split_a...  15.6 us
    dot_general x1, matrix products, body(): lax.dot_general(jnp.concatenate([w_gate, w_up], 0), row_block, contract_l...  12.5 us
    ppermute x7, starting transfers between devices, ring_sum(): lax.ppermute(part, axis, [(i, (i + d) % peers) for i in range(peers)])  12.4 us
    ppermute x6, waiting for transfers between devices, ring_shifts(): lax.ppermute(part, axis, [(i, (i + d) % peers) for i in range(peers)])  10.8 us
    ppermute x6, starting transfers between devices, ring_shifts(): lax.ppermute(part, axis, [(i, (i + d) % peers) for i in range(peers)])  7.48 us
  transfers between devices with their start and end apart: 19, of which 15 were waited for; matrix products, arithmetic and copies ran while one was open for 2% of the time, Pallas kernels for 0%

profile of v7, /device:TPU:1, one launch (start us, length us, event | category | flops | bytes accessed | tf_op | source)
XLA Modules:
  0.0 241.0 jit_solution(1478433660680450020)
XLA Ops:
  7.2 0.8 copy.85
  8.1 3.3 %collective-permute-start = (f32[8]{0:T(128)S(1)}, f32[8]{0:T(128)S(1)}, u32[]{:S(2)}, u32[]{:S(2)}) collective-permute-start(f32[8]{0:T(128)S(1)} %fusion.53), channel_id=1, source_target_pairs={{0,8},{8,0},{1,9},{9,1},{2,10},{10,2},{3,11},{11,3},{4,12},{12,4},... | collective-permute-start | bytes 104 | tf_op jit(solution)/shard_map/ppermute | solution.py:69
  11.5 1.7 fusion.23
  13.6 1.6 collective-permute-done.1
  15.8 2.2 collective-permute-start.3
  17.9 1.1 collective-permute-start.2
  19.0 3.6 %collective-permute-done.4 = bf16[4,136,128]{2,1,0:T(8,128)(2,1)S(1)} collective-permute-done((bf16[4,136,128]{2,1,0:T(8,128)(2,1)S(1)}, bf16[4,136,128]{2,1,0:T(8,128)(2,1)S(1)}, u32[]{:S(2)}, u32[]{:S(2)}) %collective-permute-start.4) | collective-permute-done | bytes 139296 | tf_op jit(solution)/shard_map/ppermute | solution.py:44
  22.6 2.0 collective-permute-done.3
  24.7 0.7 collective-permute-done.2
  25.4 0.1 fusion.45
  25.6 0.3 add_convert_fusion
  26.2 0.6 collective-permute-start.6
  26.7 2.5 %collective-permute-start.5 = (bf16[4,136,128]{2,1,0:T(8,128)(2,1)S(1)}, bf16[4,136,128]{2,1,0:T(8,128)(2,1)S(1)}, u32[]{:S(2)}, u32[]{:S(2)}) collective-permute-start(bf16[4,136,128]{2,1,0:T(8,128)(2,1)S(1)} %maximum_maximum_fusion.1), channel_id=1, source_target_pairs={{0,128},{64,192},{128,0},{192,64},{1,129},{65,193},{129,1},{193,65... | collective-permute-start | bytes 417800 | tf_op jit(solution)/shard_map/ppermute | solution.py:44
  29.2 1.2 collective-permute-start.7
  30.4 1.0 collective-permute-done.6
  31.4 3.5 %collective-permute-done.5 = bf16[4,136,128]{2,1,0:T(8,128)(2,1)S(1)} collective-permute-done((bf16[4,136,128]{2,1,0:T(8,128)(2,1)S(1)}, bf16[4,136,128]{2,1,0:T(8,128)(2,1)S(1)}, u32[]{:S(2)}, u32[]{:S(2)}) %collective-permute-start.5) | collective-permute-done | bytes 139296 | tf_op jit(solution)/shard_map/ppermute | solution.py:44
  35.1 0.3 fusion.18
  35.4 2.1 collective-permute-start.8
  37.5 0.2 convolution_multiply_fusion
  37.8 0.3 convolution_bitcast_fusion.1
  38.0 0.6 collective-permute-done.8
  38.6 0.8 multiply_reduce_fusion
  39.5 0.8 copy_bitcast_fusion.2
  40.4 52.7 %all-gather.3.cloned.1.call-done = bf16[2048,1024]{1,0:T(8,128)(2,1)} async-done(((bf16[64,1024]{1,0:T(8,128)(2,1)}), bf16[2048,1024]{1,0:T(8,128)(2,1)}) %all-gather.3.cloned.1.call-update) | async-done | bytes 4194320 | tf_op jit(solution)/shard_map/all_gather | solution.py:153
  93.0 4.9 %convolution_bitcast_fusion = f32[192,2048]{1,0:T(8,128)} fusion(bf16[2048,1024]{1,0:T(8,128)(2,1)} %all-gather.3.cloned.1.call-done, bf16[1024,192]{0,1:T(8,128)(2,1)S(1)} %copy-done), kind=kOutput, calls=%fused_computation.4 | convolution fusion | flops 805306368 | bytes 6160384 | tf_op jit(solution)/shard_map/dot_general | solution.py:156
  98.5 1.1 reduce-window.6
  99.6 0.2 slice_reduce_fusion
  100.0 0.1 sub.45
  100.2 33.4 %reduce-scatter.2.cloned.1.call-done = f32[192,256]{1,0:T(8,128)} async-done(((f32[192,2048]{1,0:T(8,128)}), f32[192,256]{1,0:T(8,128)}) %reduce-scatter.2.cloned.1.call-update) | async-done | bytes 196624 | tf_op jit(solution)/shard_map/reduce_scatter | solution.py:155
  133.6 0.9 fusion.27
  134.6 0.4 fusion.4
  135.1 15.6 %all_to_all.5 = bf16[8,128,192]{1,2,0:T(8,128)(2,1)S(1)} all-to-all(bf16[8,128,192]{1,2,0:T(8,128)(2,1)S(1)} %bitcast.101), channel_id=1, replica_groups=mesh['seq_0'=4,'seq_1'=4,'seq_2'=2,'exp'=8] {'exp'}, dimensions={0} | all-to-all | bytes 786432 | tf_op jit(solution)/shard_map/all_to_all | solution.py:183
  150.7 0.8 copy_bitcast_fusion
  151.6 5.4 %collective-permute-start.9 = (f32[1024]{0:T(1024)S(1)}, f32[1024]{0:T(1024)S(1)}, u32[]{:S(2)}, u32[]{:S(2)}) collective-permute-start(f32[1024]{0:T(1024)S(1)} %fusion.10), channel_id=1, source_target_pairs={{0,8},{8,0},{1,9},{9,1},{2,10},{10,2},{3,11},{11,3},{4,12},{12,4},... | collective-permute-start | bytes 12296 | tf_op jit(solution)/shard_map/ppermute | solution.py:76
  157.0 0.8 collective-permute-done.9
  157.8 2.3 collective-permute-start.12
  160.2 0.5 collective-permute-start.11
  160.7 0.6 collective-permute-start.10
  161.3 2.8 %collective-permute-done.11 = f32[1024]{0:T(1024)S(1)} collective-permute-done((f32[1024]{0:T(1024)S(1)}, f32[1024]{0:T(1024)S(1)}, u32[]{:S(2)}, u32[]{:S(2)}) %collective-permute-start.11) | collective-permute-done | bytes 4128 | tf_op jit(solution)/shard_map/ppermute | solution.py:76
  164.1 0.2 collective-permute-done.10
  164.4 2.4 collective-permute-start.15
  166.8 0.6 collective-permute-start.14
  167.4 0.6 collective-permute-start.13
  167.9 2.9 %collective-permute-done.14 = f32[1024]{0:T(1024)S(1)} collective-permute-done((f32[1024]{0:T(1024)S(1)}, f32[1024]{0:T(1024)S(1)}, u32[]{:S(2)}, u32[]{:S(2)}) %collective-permute-start.14) | collective-permute-done | bytes 4128 | tf_op jit(solution)/shard_map/ppermute | solution.py:76
  170.8 0.6 collective-permute-done.13
  171.5 49.3 %all-gather.5.cloned.1.call-done = bf16[1024,6144]{0,1:T(8,128)(2,1)} async-done(((bf16[1024,192]{0,1:T(8,128)(2,1)}), bf16[1024,6144]{0,1:T(8,128)(2,1)}) %all-gather.5.cloned.1.call-update) | async-done | bytes 12582928 | tf_op jit(solution)/shard_map/all_gather | solution.py:188
  220.8 12.5 %fusion = f32[576,1024]{1,0:T(8,128)S(1)} fusion(bf16[1024,6144]{0,1:T(8,128)(2,1)} %all-gather.5.cloned.1.call-done, bf16[288,6144]{1,0:T(8,128)(2,1)} %bitcast.105, bf16[288,6144]{1,0:T(8,128)(2,1)} %bitcast.106), kind=kOutput, calls=%fused_computation | convolution fusion | flops 7261913088 | bytes 22020096 | tf_op jit(solution)/shard_map/dot_general | solution.py:192
  233.3 1.2 fusion.11
  (74 shorter events, 2.7 us)
Async XLA Ops:
  7.2 85.9 %copy-start = (bf16[1024,192]{0,1:T(8,128)(2,1)S(1)}, bf16[1024,192]{0,1:T(8,128)(2,1)}, u32[]{:S(2)}) copy-start(bf16[1024,192]{0,1:T(8,128)(2,1)} %param.13) | copy-start | bytes 1179652
  7.2 85.9 %all-gather.3.cloned.1.call-start = ((), (), s32[]{:S(2)}) async-start(), calls=%async_computation.2 | async-start | bytes 4325376 | tf_op jit(solution)/shard_map/all_gather | solution.py:153
  8.1 5.3 %collective-permute-start = (f32[8]{0:T(128)S(1)}, f32[8]{0:T(128)S(1)}, u32[]{:S(2)}, u32[]{:S(2)}) collective-permute-start(f32[8]{0:T(128)S(1)} %fusion.53), channel_id=1, source_target_pairs={{0,8},{8,0},{1,9},{9,1},{2,10},{10,2},{3,11},{11,3},{4,12},{12,4},... | collective-permute-start | bytes 104 | tf_op jit(solution)/shard_map/ppermute | solution.py:69
  13.2 2.0 collective-permute-start.1
  15.3 22.2 %copy-start.2 = (bf16[64,1024]{1,0:T(8,128)(2,1)S(1)}, bf16[64,1024]{1,0:T(8,128)(2,1)}, u32[]{:S(2)}) copy-start(bf16[64,1024]{1,0:T(8,128)(2,1)} %param.10) | copy-start | bytes 393220
  15.3 22.2 %copy-start.6 = (bf16[64,1024]{1,0:T(8,128)(2,1)S(1)}, bf16[64,1024]{1,0:T(8,128)(2,1)}, u32[]{:S(2)}) copy-start(bf16[64,1024]{1,0:T(8,128)(2,1)} %param.9) | copy-start | bytes 393220
  15.4 22.3 %copy-start.1 = (bf16[64,1024]{1,0:T(8,128)(2,1)S(1)}, bf16[64,1024]{1,0:T(8,128)(2,1)}, u32[]{:S(2)}) copy-start(bf16[64,1024]{1,0:T(8,128)(2,1)} %param.11) | copy-start | bytes 393220
  15.7 6.9 %collective-permute-start.4 = (bf16[4,136,128]{2,1,0:T(8,128)(2,1)S(1)}, bf16[4,136,128]{2,1,0:T(8,128)(2,1)S(1)}, u32[]{:S(2)}, u32[]{:S(2)}) collective-permute-start(bf16[4,136,128]{2,1,0:T(8,128)(2,1)S(1)} %maximum_maximum_fusion), channel_id=1, source_target_pairs={{0,16},{16,32},{32,48},{48,0},{1,17},{17,33},{33,49},{49,1},{2,18}... | collective-permute-start | bytes 417800 | tf_op jit(solution)/shard_map/ppermute | solution.py:44
  15.8 8.9 %collective-permute-start.3 = (bf16[4,136,128]{2,1,0:T(8,128)(2,1)S(1)}, bf16[4,136,128]{2,1,0:T(8,128)(2,1)S(1)}, u32[]{:S(2)}, u32[]{:S(2)}) collective-permute-start(bf16[4,136,128]{2,1,0:T(8,128)(2,1)S(1)} %maximum_maximum_fusion), channel_id=1, source_target_pairs={{0,32},{16,48},{32,0},{48,16},{1,33},{17,49},{33,1},{49,17},{2,34}... | collective-permute-start | bytes 417800 | tf_op jit(solution)/shard_map/ppermute | solution.py:44
  17.9 7.4 %collective-permute-start.2 = (bf16[4,136,128]{2,1,0:T(8,128)(2,1)S(1)}, bf16[4,136,128]{2,1,0:T(8,128)(2,1)S(1)}, u32[]{:S(2)}, u32[]{:S(2)}) collective-permute-start(bf16[4,136,128]{2,1,0:T(8,128)(2,1)S(1)} %maximum_maximum_fusion), channel_id=1, source_target_pairs={{0,48},{16,0},{32,16},{48,32},{1,49},{17,1},{33,17},{49,33},{2,50}... | collective-permute-start | bytes 417800 | tf_op jit(solution)/shard_map/ppermute | solution.py:44
  26.2 5.2 %collective-permute-start.6 = (bf16[4,136,128]{2,1,0:T(8,128)(2,1)S(1)}, bf16[4,136,128]{2,1,0:T(8,128)(2,1)S(1)}, u32[]{:S(2)}, u32[]{:S(2)}) collective-permute-start(bf16[4,136,128]{2,1,0:T(8,128)(2,1)S(1)} %maximum_maximum_fusion.1), channel_id=1, source_target_pairs={{0,64},{64,128},{128,192},{192,0},{1,65},{65,129},{129,193},{193,1... | collective-permute-start | bytes 417800 | tf_op jit(solution)/shard_map/ppermute | solution.py:44
  26.7 8.2 %collective-permute-start.5 = (bf16[4,136,128]{2,1,0:T(8,128)(2,1)S(1)}, bf16[4,136,128]{2,1,0:T(8,128)(2,1)S(1)}, u32[]{:S(2)}, u32[]{:S(2)}) collective-permute-start(bf16[4,136,128]{2,1,0:T(8,128)(2,1)S(1)} %maximum_maximum_fusion.1), channel_id=1, source_target_pairs={{0,128},{64,192},{128,0},{192,64},{1,129},{65,193},{129,1},{193,65... | collective-permute-start | bytes 417800 | tf_op jit(solution)/shard_map/ppermute | solution.py:44
  29.2 5.9 %collective-permute-start.7 = (bf16[4,136,128]{2,1,0:T(8,128)(2,1)S(1)}, bf16[4,136,128]{2,1,0:T(8,128)(2,1)S(1)}, u32[]{:S(2)}, u32[]{:S(2)}) collective-permute-start(bf16[4,136,128]{2,1,0:T(8,128)(2,1)S(1)} %maximum_maximum_fusion.1), channel_id=1, source_target_pairs={{0,192},{64,0},{128,64},{192,128},{1,193},{65,1},{129,65},{193,129... | collective-permute-start | bytes 417800 | tf_op jit(solution)/shard_map/ppermute | solution.py:44
  35.4 3.3 %collective-permute-start.8 = (f32[4,128,128]{2,1,0:T(8,128)S(1)}, f32[4,128,128]{2,1,0:T(8,128)S(1)}, u32[]{:S(2)}, u32[]{:S(2)}) collective-permute-start(f32[4,128,128]{2,1,0:T(8,128)S(1)} %fusion.18), channel_id=1, source_target_pairs={{0,8},{8,0},{1,9},{9,1},{2,10},{10,2},{3,11},{11,3},{4,12},{12,4},... | collective-permute-start | bytes 786440 | tf_op jit(solution)/shard_map/ppermute | solution.py:69
  40.3 57.7 %copy-start.5 = (s32[256,2]{0,1:T(2,128)S(1)}, s32[256,2]{0,1:T(2,128)}, u32[]{:S(2)}) copy-start(s32[256,2]{0,1:T(2,128)} %param.15) | copy-start | bytes 6148
  40.3 93.3 %copy-start.3 = (bf16[256,192]{0,1:T(8,128)(2,1)S(1)}, bf16[256,192]{0,1:T(8,128)(2,1)}, u32[]{:S(2)}) copy-start(bf16[256,192]{0,1:T(8,128)(2,1)} %param.14) | copy-start | bytes 294916
  40.3 93.3 %reduce-scatter.2.cloned.1.call-start = ((), (), s32[]{:S(2)}) async-start(), calls=%async_computation.3 | async-start | bytes 1769472 | tf_op jit(solution)/shard_map/reduce_scatter | solution.py:155
  98.0 122.8 %all-gather.5.cloned.1.call-start = ((), (), s32[]{:S(2)}) async-start(), calls=%async_computation.4 | async-start | bytes 12976128 | tf_op jit(solution)/shard_map/all_gather | solution.py:188
  134.6 98.7 %copy-start.4 = (bf16[256,192]{0,1:T(8,128)(2,1)}, bf16[256,192]{0,1:T(8,128)(2,1)S(1)}, u32[]{:S(2)}) copy-start(bf16[256,192]{0,1:T(8,128)(2,1)S(1)} %fusion.27) | copy-start | bytes 294916
  151.6 6.2 %collective-permute-start.9 = (f32[1024]{0:T(1024)S(1)}, f32[1024]{0:T(1024)S(1)}, u32[]{:S(2)}, u32[]{:S(2)}) collective-permute-start(f32[1024]{0:T(1024)S(1)} %fusion.10), channel_id=1, source_target_pairs={{0,8},{8,0},{1,9},{9,1},{2,10},{10,2},{3,11},{11,3},{4,12},{12,4},... | collective-permute-start | bytes 12296 | tf_op jit(solution)/shard_map/ppermute | solution.py:76
  157.8 3.5 %collective-permute-start.12 = (f32[1024]{0:T(1024)S(1)}, f32[1024]{0:T(1024)S(1)}, u32[]{:S(2)}, u32[]{:S(2)}) collective-permute-start(f32[1024]{0:T(1024)S(1)} %add.156), channel_id=1, source_target_pairs={{0,48},{16,0},{32,16},{48,32},{1,49},{17,1},{33,17},{49,33},{2,50}... | collective-permute-start | bytes 12296 | tf_op jit(solution)/shard_map/ppermute | solution.py:76
  160.2 4.0 %collective-permute-start.11 = (f32[1024]{0:T(1024)S(1)}, f32[1024]{0:T(1024)S(1)}, u32[]{:S(2)}, u32[]{:S(2)}) collective-permute-start(f32[1024]{0:T(1024)S(1)} %add.156), channel_id=1, source_target_pairs={{0,32},{16,48},{32,0},{48,16},{1,33},{17,49},{33,1},{49,17},{2,34}... | collective-permute-start | bytes 12296 | tf_op jit(solution)/shard_map/ppermute | solution.py:76
  160.7 3.7 %collective-permute-start.10 = (f32[1024]{0:T(1024)S(1)}, f32[1024]{0:T(1024)S(1)}, u32[]{:S(2)}, u32[]{:S(2)}) collective-permute-start(f32[1024]{0:T(1024)S(1)} %add.156), channel_id=1, source_target_pairs={{0,16},{16,32},{32,48},{48,0},{1,17},{17,33},{33,49},{49,1},{2,18}... | collective-permute-start | bytes 12296 | tf_op jit(solution)/shard_map/ppermute | solution.py:76
  164.4 3.6 %collective-permute-start.15 = (f32[1024]{0:T(1024)S(1)}, f32[1024]{0:T(1024)S(1)}, u32[]{:S(2)}, u32[]{:S(2)}) collective-permute-start(f32[1024]{0:T(1024)S(1)} %add_add_fusion), channel_id=1, source_target_pairs={{0,192},{64,0},{128,64},{192,128},{1,193},{65,1},{129,65},{193,129... | collective-permute-start | bytes 12296 | tf_op jit(solution)/shard_map/ppermute | solution.py:76
  166.8 4.1 %collective-permute-start.14 = (f32[1024]{0:T(1024)S(1)}, f32[1024]{0:T(1024)S(1)}, u32[]{:S(2)}, u32[]{:S(2)}) collective-permute-start(f32[1024]{0:T(1024)S(1)} %add_add_fusion), channel_id=1, source_target_pairs={{0,128},{64,192},{128,0},{192,64},{1,129},{65,193},{129,1},{193,65... | collective-permute-start | bytes 12296 | tf_op jit(solution)/shard_map/ppermute | solution.py:76
  167.4 4.1 %collective-permute-start.13 = (f32[1024]{0:T(1024)S(1)}, f32[1024]{0:T(1024)S(1)}, u32[]{:S(2)}, u32[]{:S(2)}) collective-permute-start(f32[1024]{0:T(1024)S(1)} %add_add_fusion), channel_id=1, source_target_pairs={{0,64},{64,128},{128,192},{192,0},{1,65},{65,129},{129,193},{193,1... | collective-permute-start | bytes 12296 | tf_op jit(solution)/shard_map/ppermute | solution.py:76
Sparse Core Ops, SparseCore 0:
  40.4 52.5 all-gather.2
  98.1 35.5 reduce-scatter.1
  151.7 69.0 all-gather.4

commit v8 on v7

--- a/solution.py
+++ b/solution.py
@@ -47,8 +47,10 @@
 
 def packed_shifts(decay, state, axis):
     heads, rows, cols = state.shape
-    high = decay.astype(jnp.bfloat16)
-    low = (decay - high.astype(jnp.float32)).astype(jnp.bfloat16)
+    scaled = decay * 65537.0
+    leading = scaled - (scaled - decay)
+    high = leading.astype(jnp.bfloat16)
+    low = (decay - leading).astype(jnp.bfloat16)
     tail = jnp.concatenate(
         [
             jnp.broadcast_to(high[:, None, None], (heads, 1, cols)),

time: 241 us -> 241 us (level)
  no operation moved by 1% of the time
where the time goes in v8:
time: 241 us
  waiting for transfers between devices  156 us (65%)
  starting transfers between devices  25.7 us (11%)
  matrix products  20.7 us (9%)
  blocking collectives  15.5 us (6%)
  between operations  14 us (6%)
  other arithmetic  5.93 us (2%)
  local copies, waits for them, and re-layouts  3.24 us (1%)
    all_gather x1, waiting for transfers between devices, body(): gathered = lax.all_gather(normed, SEQ, axis=0, tiled=True)  52.7 us
    all_gather x1, waiting for transfers between devices, body(): row_block = lax.all_gather(slices, SEQ, axis=1, tiled=True)  49.3 us
    reduce_scatter x1, waiting for transfers between devices, body(): lax.psum_scatter(lax.dot_general(out_weight, row_block, (((0,), (1,)), ((...  33.4 us
    all_to_all x1, blocking collectives, body(): lax.all_to_all(buffer.reshape(experts, capacity, columns), 'exp', split_a...  15.5 us
    ppermute x7, starting transfers between devices, ring_sum(): lax.ppermute(part, axis, [(i, (i + d) % peers) for i in range(peers)])  12.5 us
    dot_general x1, matrix products, body(): lax.dot_general(jnp.concatenate([w_gate, w_up], 0), row_block, contract_l...  12.5 us
    ppermute x6, waiting for transfers between devices, ring_shifts(): lax.ppermute(part, axis, [(i, (i + d) % peers) for i in range(peers)])  10.8 us
    ppermute x6, starting transfers between devices, ring_shifts(): lax.ppermute(part, axis, [(i, (i + d) % peers) for i in range(peers)])  7.48 us
  transfers between devices with their start and end apart: 19, of which 15 were waited for; matrix products, arithmetic and copies ran while one was open for 2% of the time, Pallas kernels for 0%

profile of v8, /device:TPU:1, one launch (start us, length us, event | category | flops | bytes accessed | tf_op | source)
XLA Modules:
  0.0 241.0 jit_solution(762130562205192642)
XLA Ops:
  7.2 0.8 copy.85
  8.1 3.3 %collective-permute-start = (f32[8]{0:T(128)S(1)}, f32[8]{0:T(128)S(1)}, u32[]{:S(2)}, u32[]{:S(2)}) collective-permute-start(f32[8]{0:T(128)S(1)} %fusion.55), channel_id=1, source_target_pairs={{0,8},{8,0},{1,9},{9,1},{2,10},{10,2},{3,11},{11,3},{4,12},{12,4},... | collective-permute-start | bytes 104 | tf_op jit(solution)/shard_map/ppermute | solution.py:71
  11.5 1.7 fusion.23
  13.6 1.6 collective-permute-done.1
  15.8 2.2 collective-permute-start.3
  17.9 1.1 collective-permute-start.2
  19.0 3.6 %collective-permute-done.4 = bf16[4,136,128]{2,1,0:T(8,128)(2,1)S(1)} collective-permute-done((bf16[4,136,128]{2,1,0:T(8,128)(2,1)S(1)}, bf16[4,136,128]{2,1,0:T(8,128)(2,1)S(1)}, u32[]{:S(2)}, u32[]{:S(2)}) %collective-permute-start.4) | collective-permute-done | bytes 139296 | tf_op jit(solution)/shard_map/ppermute | solution.py:44
  22.6 2.0 collective-permute-done.3
  24.7 0.7 collective-permute-done.2
  25.4 0.1 fusion.45
  25.6 0.3 add_convert_fusion
  26.2 0.6 collective-permute-start.6
  26.7 2.5 %collective-permute-start.5 = (bf16[4,136,128]{2,1,0:T(8,128)(2,1)S(1)}, bf16[4,136,128]{2,1,0:T(8,128)(2,1)S(1)}, u32[]{:S(2)}, u32[]{:S(2)}) collective-permute-start(bf16[4,136,128]{2,1,0:T(8,128)(2,1)S(1)} %maximum_maximum_fusion.1), channel_id=1, source_target_pairs={{0,128},{64,192},{128,0},{192,64},{1,129},{65,193},{129,1},{193,65... | collective-permute-start | bytes 417800 | tf_op jit(solution)/shard_map/ppermute | solution.py:44
  29.2 1.2 collective-permute-start.7
  30.4 1.0 collective-permute-done.6
  31.4 3.5 %collective-permute-done.5 = bf16[4,136,128]{2,1,0:T(8,128)(2,1)S(1)} collective-permute-done((bf16[4,136,128]{2,1,0:T(8,128)(2,1)S(1)}, bf16[4,136,128]{2,1,0:T(8,128)(2,1)S(1)}, u32[]{:S(2)}, u32[]{:S(2)}) %collective-permute-start.5) | collective-permute-done | bytes 139296 | tf_op jit(solution)/shard_map/ppermute | solution.py:44
  35.1 0.3 fusion.18
  35.4 2.1 collective-permute-start.8
  37.5 0.2 convolution_multiply_fusion
  37.8 0.3 convolution_bitcast_fusion.1
  38.0 0.6 collective-permute-done.8
  38.6 0.8 multiply_reduce_fusion
  39.5 0.8 copy_bitcast_fusion.2
  40.4 52.7 %all-gather.3.cloned.1.call-done = bf16[2048,1024]{1,0:T(8,128)(2,1)} async-done(((bf16[64,1024]{1,0:T(8,128)(2,1)}), bf16[2048,1024]{1,0:T(8,128)(2,1)}) %all-gather.3.cloned.1.call-update) | async-done | bytes 4194320 | tf_op jit(solution)/shard_map/all_gather | solution.py:155
  93.0 4.9 %convolution_bitcast_fusion = f32[192,2048]{1,0:T(8,128)} fusion(bf16[2048,1024]{1,0:T(8,128)(2,1)} %all-gather.3.cloned.1.call-done, bf16[1024,192]{0,1:T(8,128)(2,1)S(1)} %copy-done), kind=kOutput, calls=%fused_computation.4 | convolution fusion | flops 805306368 | bytes 6160384 | tf_op jit(solution)/shard_map/dot_general | solution.py:158
  98.5 1.1 reduce-window.6
  99.6 0.2 slice_reduce_fusion
  100.0 0.1 sub.61
  100.2 33.4 %reduce-scatter.2.cloned.1.call-done = f32[192,256]{1,0:T(8,128)} async-done(((f32[192,2048]{1,0:T(8,128)}), f32[192,256]{1,0:T(8,128)}) %reduce-scatter.2.cloned.1.call-update) | async-done | bytes 196624 | tf_op jit(solution)/shard_map/reduce_scatter | solution.py:157
  133.6 0.9 fusion.27
  134.6 0.4 fusion.4
  135.1 15.5 %all_to_all.5 = bf16[8,128,192]{1,2,0:T(8,128)(2,1)S(1)} all-to-all(bf16[8,128,192]{1,2,0:T(8,128)(2,1)S(1)} %bitcast.101), channel_id=1, replica_groups=mesh['seq_0'=4,'seq_1'=4,'seq_2'=2,'exp'=8] {'exp'}, dimensions={0} | all-to-all | bytes 786432 | tf_op jit(solution)/shard_map/all_to_all | solution.py:185
  150.6 0.8 copy_bitcast_fusion
  151.5 5.4 %collective-permute-start.9 = (f32[1024]{0:T(1024)S(1)}, f32[1024]{0:T(1024)S(1)}, u32[]{:S(2)}, u32[]{:S(2)}) collective-permute-start(f32[1024]{0:T(1024)S(1)} %fusion.10), channel_id=1, source_target_pairs={{0,8},{8,0},{1,9},{9,1},{2,10},{10,2},{3,11},{11,3},{4,12},{12,4},... | collective-permute-start | bytes 12296 | tf_op jit(solution)/shard_map/ppermute | solution.py:78
  156.9 0.8 collective-permute-done.9
  157.7 2.5 %collective-permute-start.12 = (f32[1024]{0:T(1024)S(1)}, f32[1024]{0:T(1024)S(1)}, u32[]{:S(2)}, u32[]{:S(2)}) collective-permute-start(f32[1024]{0:T(1024)S(1)} %add.156), channel_id=1, source_target_pairs={{0,48},{16,0},{32,16},{48,32},{1,49},{17,1},{33,17},{49,33},{2,50}... | collective-permute-start | bytes 12296 | tf_op jit(solution)/shard_map/ppermute | solution.py:78
  160.2 0.5 collective-permute-start.11
  160.7 0.6 collective-permute-start.10
  161.3 2.9 %collective-permute-done.11 = f32[1024]{0:T(1024)S(1)} collective-permute-done((f32[1024]{0:T(1024)S(1)}, f32[1024]{0:T(1024)S(1)}, u32[]{:S(2)}, u32[]{:S(2)}) %collective-permute-start.11) | collective-permute-done | bytes 4128 | tf_op jit(solution)/shard_map/ppermute | solution.py:78
  164.2 0.2 collective-permute-done.10
  164.4 2.4 collective-permute-start.15
  166.7 0.6 collective-permute-start.14
  167.4 0.6 collective-permute-start.13
  168.0 2.8 %collective-permute-done.14 = f32[1024]{0:T(1024)S(1)} collective-permute-done((f32[1024]{0:T(1024)S(1)}, f32[1024]{0:T(1024)S(1)}, u32[]{:S(2)}, u32[]{:S(2)}) %collective-permute-start.14) | collective-permute-done | bytes 4128 | tf_op jit(solution)/shard_map/ppermute | solution.py:78
  170.8 0.7 collective-permute-done.13
  171.5 49.3 %all-gather.5.cloned.1.call-done = bf16[1024,6144]{0,1:T(8,128)(2,1)} async-done(((bf16[1024,192]{0,1:T(8,128)(2,1)}), bf16[1024,6144]{0,1:T(8,128)(2,1)}) %all-gather.5.cloned.1.call-update) | async-done | bytes 12582928 | tf_op jit(solution)/shard_map/all_gather | solution.py:190
  220.8 12.5 %fusion = f32[576,1024]{1,0:T(8,128)S(1)} fusion(bf16[1024,6144]{0,1:T(8,128)(2,1)} %all-gather.5.cloned.1.call-done, bf16[288,6144]{1,0:T(8,128)(2,1)} %bitcast.105, bf16[288,6144]{1,0:T(8,128)(2,1)} %bitcast.106), kind=kOutput, calls=%fused_computation | convolution fusion | flops 7261913088 | bytes 22020096 | tf_op jit(solution)/shard_map/dot_general | solution.py:194
  233.3 1.2 fusion.11
  (74 shorter events, 2.8 us)
Async XLA Ops:
  7.2 85.9 %copy-start = (bf16[1024,192]{0,1:T(8,128)(2,1)S(1)}, bf16[1024,192]{0,1:T(8,128)(2,1)}, u32[]{:S(2)}) copy-start(bf16[1024,192]{0,1:T(8,128)(2,1)} %param.13) | copy-start | bytes 1179652
  7.2 85.9 %all-gather.3.cloned.1.call-start = ((), (), s32[]{:S(2)}) async-start(), calls=%async_computation.2 | async-start | bytes 4325376 | tf_op jit(solution)/shard_map/all_gather | solution.py:155
  8.1 5.3 %collective-permute-start = (f32[8]{0:T(128)S(1)}, f32[8]{0:T(128)S(1)}, u32[]{:S(2)}, u32[]{:S(2)}) collective-permute-start(f32[8]{0:T(128)S(1)} %fusion.55), channel_id=1, source_target_pairs={{0,8},{8,0},{1,9},{9,1},{2,10},{10,2},{3,11},{11,3},{4,12},{12,4},... | collective-permute-start | bytes 104 | tf_op jit(solution)/shard_map/ppermute | solution.py:71
  13.2 2.0 collective-permute-start.1
  15.3 22.2 %copy-start.2 = (bf16[64,1024]{1,0:T(8,128)(2,1)S(1)}, bf16[64,1024]{1,0:T(8,128)(2,1)}, u32[]{:S(2)}) copy-start(bf16[64,1024]{1,0:T(8,128)(2,1)} %param.10) | copy-start | bytes 393220
  15.3 22.2 %copy-start.6 = (bf16[64,1024]{1,0:T(8,128)(2,1)S(1)}, bf16[64,1024]{1,0:T(8,128)(2,1)}, u32[]{:S(2)}) copy-start(bf16[64,1024]{1,0:T(8,128)(2,1)} %param.9) | copy-start | bytes 393220
  15.4 22.3 %copy-start.1 = (bf16[64,1024]{1,0:T(8,128)(2,1)S(1)}, bf16[64,1024]{1,0:T(8,128)(2,1)}, u32[]{:S(2)}) copy-start(bf16[64,1024]{1,0:T(8,128)(2,1)} %param.11) | copy-start | bytes 393220
  15.7 6.9 %collective-permute-start.4 = (bf16[4,136,128]{2,1,0:T(8,128)(2,1)S(1)}, bf16[4,136,128]{2,1,0:T(8,128)(2,1)S(1)}, u32[]{:S(2)}, u32[]{:S(2)}) collective-permute-start(bf16[4,136,128]{2,1,0:T(8,128)(2,1)S(1)} %maximum_maximum_fusion), channel_id=1, source_target_pairs={{0,16},{16,32},{32,48},{48,0},{1,17},{17,33},{33,49},{49,1},{2,18}... | collective-permute-start | bytes 417800 | tf_op jit(solution)/shard_map/ppermute | solution.py:44
  15.8 8.9 %collective-permute-start.3 = (bf16[4,136,128]{2,1,0:T(8,128)(2,1)S(1)}, bf16[4,136,128]{2,1,0:T(8,128)(2,1)S(1)}, u32[]{:S(2)}, u32[]{:S(2)}) collective-permute-start(bf16[4,136,128]{2,1,0:T(8,128)(2,1)S(1)} %maximum_maximum_fusion), channel_id=1, source_target_pairs={{0,32},{16,48},{32,0},{48,16},{1,33},{17,49},{33,1},{49,17},{2,34}... | collective-permute-start | bytes 417800 | tf_op jit(solution)/shard_map/ppermute | solution.py:44
  17.9 7.4 %collective-permute-start.2 = (bf16[4,136,128]{2,1,0:T(8,128)(2,1)S(1)}, bf16[4,136,128]{2,1,0:T(8,128)(2,1)S(1)}, u32[]{:S(2)}, u32[]{:S(2)}) collective-permute-start(bf16[4,136,128]{2,1,0:T(8,128)(2,1)S(1)} %maximum_maximum_fusion), channel_id=1, source_target_pairs={{0,48},{16,0},{32,16},{48,32},{1,49},{17,1},{33,17},{49,33},{2,50}... | collective-permute-start | bytes 417800 | tf_op jit(solution)/shard_map/ppermute | solution.py:44
  26.2 5.2 %collective-permute-start.6 = (bf16[4,136,128]{2,1,0:T(8,128)(2,1)S(1)}, bf16[4,136,128]{2,1,0:T(8,128)(2,1)S(1)}, u32[]{:S(2)}, u32[]{:S(2)}) collective-permute-start(bf16[4,136,128]{2,1,0:T(8,128)(2,1)S(1)} %maximum_maximum_fusion.1), channel_id=1, source_target_pairs={{0,64},{64,128},{128,192},{192,0},{1,65},{65,129},{129,193},{193,1... | collective-permute-start | bytes 417800 | tf_op jit(solution)/shard_map/ppermute | solution.py:44
  26.7 8.2 %collective-permute-start.5 = (bf16[4,136,128]{2,1,0:T(8,128)(2,1)S(1)}, bf16[4,136,128]{2,1,0:T(8,128)(2,1)S(1)}, u32[]{:S(2)}, u32[]{:S(2)}) collective-permute-start(bf16[4,136,128]{2,1,0:T(8,128)(2,1)S(1)} %maximum_maximum_fusion.1), channel_id=1, source_target_pairs={{0,128},{64,192},{128,0},{192,64},{1,129},{65,193},{129,1},{193,65... | collective-permute-start | bytes 417800 | tf_op jit(solution)/shard_map/ppermute | solution.py:44
  29.2 5.9 %collective-permute-start.7 = (bf16[4,136,128]{2,1,0:T(8,128)(2,1)S(1)}, bf16[4,136,128]{2,1,0:T(8,128)(2,1)S(1)}, u32[]{:S(2)}, u32[]{:S(2)}) collective-permute-start(bf16[4,136,128]{2,1,0:T(8,128)(2,1)S(1)} %maximum_maximum_fusion.1), channel_id=1, source_target_pairs={{0,192},{64,0},{128,64},{192,128},{1,193},{65,1},{129,65},{193,129... | collective-permute-start | bytes 417800 | tf_op jit(solution)/shard_map/ppermute | solution.py:44
  35.4 3.3 %collective-permute-start.8 = (f32[4,128,128]{2,1,0:T(8,128)S(1)}, f32[4,128,128]{2,1,0:T(8,128)S(1)}, u32[]{:S(2)}, u32[]{:S(2)}) collective-permute-start(f32[4,128,128]{2,1,0:T(8,128)S(1)} %fusion.18), channel_id=1, source_target_pairs={{0,8},{8,0},{1,9},{9,1},{2,10},{10,2},{3,11},{11,3},{4,12},{12,4},... | collective-permute-start | bytes 786440 | tf_op jit(solution)/shard_map/ppermute | solution.py:71
  40.3 57.7 %copy-start.5 = (s32[256,2]{0,1:T(2,128)S(1)}, s32[256,2]{0,1:T(2,128)}, u32[]{:S(2)}) copy-start(s32[256,2]{0,1:T(2,128)} %param.15) | copy-start | bytes 6148
  40.3 93.3 %copy-start.3 = (bf16[256,192]{0,1:T(8,128)(2,1)S(1)}, bf16[256,192]{0,1:T(8,128)(2,1)}, u32[]{:S(2)}) copy-start(bf16[256,192]{0,1:T(8,128)(2,1)} %param.14) | copy-start | bytes 294916
  40.3 93.3 %reduce-scatter.2.cloned.1.call-start = ((), (), s32[]{:S(2)}) async-start(), calls=%async_computation.3 | async-start | bytes 1769472 | tf_op jit(solution)/shard_map/reduce_scatter | solution.py:157
  98.0 122.8 %all-gather.5.cloned.1.call-start = ((), (), s32[]{:S(2)}) async-start(), calls=%async_computation.4 | async-start | bytes 12976128 | tf_op jit(solution)/shard_map/all_gather | solution.py:190
  134.6 98.7 %copy-start.4 = (bf16[256,192]{0,1:T(8,128)(2,1)}, bf16[256,192]{0,1:T(8,128)(2,1)S(1)}, u32[]{:S(2)}) copy-start(bf16[256,192]{0,1:T(8,128)(2,1)S(1)} %fusion.27) | copy-start | bytes 294916
  151.5 6.2 %collective-permute-start.9 = (f32[1024]{0:T(1024)S(1)}, f32[1024]{0:T(1024)S(1)}, u32[]{:S(2)}, u32[]{:S(2)}) collective-permute-start(f32[1024]{0:T(1024)S(1)} %fusion.10), channel_id=1, source_target_pairs={{0,8},{8,0},{1,9},{9,1},{2,10},{10,2},{3,11},{11,3},{4,12},{12,4},... | collective-permute-start | bytes 12296 | tf_op jit(solution)/shard_map/ppermute | solution.py:78
  157.7 3.6 %collective-permute-start.12 = (f32[1024]{0:T(1024)S(1)}, f32[1024]{0:T(1024)S(1)}, u32[]{:S(2)}, u32[]{:S(2)}) collective-permute-start(f32[1024]{0:T(1024)S(1)} %add.156), channel_id=1, source_target_pairs={{0,48},{16,0},{32,16},{48,32},{1,49},{17,1},{33,17},{49,33},{2,50}... | collective-permute-start | bytes 12296 | tf_op jit(solution)/shard_map/ppermute | solution.py:78
  160.2 4.0 %collective-permute-start.11 = (f32[1024]{0:T(1024)S(1)}, f32[1024]{0:T(1024)S(1)}, u32[]{:S(2)}, u32[]{:S(2)}) collective-permute-start(f32[1024]{0:T(1024)S(1)} %add.156), channel_id=1, source_target_pairs={{0,32},{16,48},{32,0},{48,16},{1,33},{17,49},{33,1},{49,17},{2,34}... | collective-permute-start | bytes 12296 | tf_op jit(solution)/shard_map/ppermute | solution.py:78
  160.7 3.7 %collective-permute-start.10 = (f32[1024]{0:T(1024)S(1)}, f32[1024]{0:T(1024)S(1)}, u32[]{:S(2)}, u32[]{:S(2)}) collective-permute-start(f32[1024]{0:T(1024)S(1)} %add.156), channel_id=1, source_target_pairs={{0,16},{16,32},{32,48},{48,0},{1,17},{17,33},{33,49},{49,1},{2,18}... | collective-permute-start | bytes 12296 | tf_op jit(solution)/shard_map/ppermute | solution.py:78
  164.4 3.6 %collective-permute-start.15 = (f32[1024]{0:T(1024)S(1)}, f32[1024]{0:T(1024)S(1)}, u32[]{:S(2)}, u32[]{:S(2)}) collective-permute-start(f32[1024]{0:T(1024)S(1)} %add_add_fusion), channel_id=1, source_target_pairs={{0,192},{64,0},{128,64},{192,128},{1,193},{65,1},{129,65},{193,129... | collective-permute-start | bytes 12296 | tf_op jit(solution)/shard_map/ppermute | solution.py:78
  166.7 4.1 %collective-permute-start.14 = (f32[1024]{0:T(1024)S(1)}, f32[1024]{0:T(1024)S(1)}, u32[]{:S(2)}, u32[]{:S(2)}) collective-permute-start(f32[1024]{0:T(1024)S(1)} %add_add_fusion), channel_id=1, source_target_pairs={{0,128},{64,192},{128,0},{192,64},{1,129},{65,193},{129,1},{193,65... | collective-permute-start | bytes 12296 | tf_op jit(solution)/shard_map/ppermute | solution.py:78
  167.4 4.1 %collective-permute-start.13 = (f32[1024]{0:T(1024)S(1)}, f32[1024]{0:T(1024)S(1)}, u32[]{:S(2)}, u32[]{:S(2)}) collective-permute-start(f32[1024]{0:T(1024)S(1)} %add_add_fusion), channel_id=1, source_target_pairs={{0,64},{64,128},{128,192},{192,0},{1,65},{65,129},{129,193},{193,1... | collective-permute-start | bytes 12296 | tf_op jit(solution)/shard_map/ppermute | solution.py:78
Sparse Core Ops, SparseCore 0:
  40.4 52.5 all-gather.2
  98.1 35.5 reduce-scatter.1
  151.5 69.1 all-gather.4

commit v9 on v8

--- a/solution.py
+++ b/solution.py
@@ -38,14 +38,15 @@
     return (earlier[0] * later[0], later[0][:, None, None] * earlier[1] + later[1])
 
 
-def ring_shifts(part, axis):
+def ring_shifts(part, axis, wrap=True):
     peers = lax.axis_size(axis)
     return [part] + [
-        lax.ppermute(part, axis, [(i, (i + d) % peers) for i in range(peers)]) for d in range(1, peers)
+        lax.ppermute(part, axis, [(i, (i + d) % peers) for i in range(peers if wrap else peers - d)])
+        for d in range(1, peers)
     ]
 
 
-def packed_shifts(decay, state, axis):
+def packed_shifts(decay, state, axis, wrap=True):
     heads, rows, cols = state.shape
     scaled = decay * 65537.0
     leading = scaled - (scaled - decay)
@@ -61,7 +62,7 @@
     )
     packed = jnp.concatenate([state.astype(jnp.bfloat16), tail], axis=1)
     pieces = [(decay, state)]
-    for moved in ring_shifts(packed, axis)[1:]:
+    for moved in ring_shifts(packed, axis, wrap)[1:]:
         whole = moved.astype(jnp.float32)
         pieces.append((whole[:, rows, 0] + whole[:, rows + 1, 0], whole[:, :rows]))
     return pieces
@@ -104,7 +105,7 @@
     chip = link_states(first, second)
     mine = jax.tree.map(lambda part: lax.dynamic_slice_in_dim(part, core * half, half, 0), chip)
     along_y, row = prefix_over(packed_shifts(*mine, "seq_1"), lax.axis_index("seq_1"))
-    along_x, _ = prefix_over(packed_shifts(*row, "seq_0"), lax.axis_index("seq_0"))
+    along_x, _ = prefix_over(packed_shifts(*row, "seq_0", wrap=False), lax.axis_index("seq_0"))
     chip_before = link_states(along_x, along_y)[1]
     theirs = swap_cores(chip_before)
     whole = jnp.where(

time: 241 us -> 244 us (1.012)
  starting transfers between devices: 25.7 us -> 29.3 us
    ppermute x6, starting transfers between devices: 7.48 us -> 11.4 us  [ring_shifts(): lax.ppermute(part, axis, [(i, (i + d) % peers) for i in range(peers if wr...]
    ppermute x6, waiting for transfers between devices: 10.8 us -> 8.19 us  [ring_shifts(): lax.ppermute(part, axis, [(i, (i + d) % peers) for i in range(peers if wr...]
where the time goes in v9:
time: 244 us
  waiting for transfers between devices  155 us (64%)
  starting transfers between devices  29.3 us (12%)
  matrix products  20.7 us (8%)
  blocking collectives  15.5 us (6%)
  between operations  14.1 us (6%)
  other arithmetic  5.94 us (2%)
  local copies, waits for them, and re-layouts  3.24 us (1%)
    all_gather x1, waiting for transfers between devices, body(): gathered = lax.all_gather(normed, SEQ, axis=0, tiled=True)  54.2 us
    all_gather x1, waiting for transfers between devices, body(): row_block = lax.all_gather(slices, SEQ, axis=1, tiled=True)  49.5 us
    reduce_scatter x1, waiting for transfers between devices, body(): lax.psum_scatter(lax.dot_general(out_weight, row_block, (((0,), (1,)), ((...  33.4 us
    all_to_all x1, blocking collectives, body(): lax.all_to_all(buffer.reshape(experts, capacity, columns), 'exp', split_a...  15.5 us
    dot_general x1, matrix products, body(): lax.dot_general(jnp.concatenate([w_gate, w_up], 0), row_block, contract_l...  12.5 us
    ppermute x7, starting transfers between devices, ring_sum(): lax.ppermute(part, axis, [(i, (i + d) % peers) for i in range(peers)])  12.3 us
    ppermute x6, starting transfers between devices, ring_shifts(): lax.ppermute(part, axis, [(i, (i + d) % peers) for i in range(peers if wr...  11.4 us
    ppermute x6, waiting for transfers between devices, ring_shifts(): lax.ppermute(part, axis, [(i, (i + d) % peers) for i in range(peers if wr...  8.19 us
  transfers between devices with their start and end apart: 19, of which 15 were waited for; matrix products, arithmetic and copies ran while one was open for 2% of the time, Pallas kernels for 0%

profile of v9, /device:TPU:1, one launch (start us, length us, event | category | flops | bytes accessed | tf_op | source)
XLA Modules:
  0.0 243.7 jit_solution(9188557273490537094)
XLA Ops:
  7.2 0.8 copy.85
  8.1 3.3 %collective-permute-start = (f32[8]{0:T(128)S(1)}, f32[8]{0:T(128)S(1)}, u32[]{:S(2)}, u32[]{:S(2)}) collective-permute-start(f32[8]{0:T(128)S(1)} %fusion.55), channel_id=1, source_target_pairs={{0,8},{8,0},{1,9},{9,1},{2,10},{10,2},{3,11},{11,3},{4,12},{12,4},... | collective-permute-start | bytes 104 | tf_op jit(solution)/shard_map/ppermute | solution.py:72
  11.5 1.7 fusion.23
  13.6 1.6 collective-permute-done.1
  15.8 2.2 collective-permute-start.3
  17.9 1.1 collective-permute-start.2
  19.0 3.6 %collective-permute-done.4 = bf16[4,136,128]{2,1,0:T(8,128)(2,1)S(1)} collective-permute-done((bf16[4,136,128]{2,1,0:T(8,128)(2,1)S(1)}, bf16[4,136,128]{2,1,0:T(8,128)(2,1)S(1)}, u32[]{:S(2)}, u32[]{:S(2)}) %collective-permute-start.4) | collective-permute-done | bytes 139296 | tf_op jit(solution)/shard_map/ppermute | solution.py:44
  22.6 2.0 collective-permute-done.3
  24.7 0.7 collective-permute-done.2
  25.4 0.1 fusion.45
  25.6 0.3 add_convert_fusion
  26.2 2.4 collective-permute-start.6
  28.6 4.4 %collective-permute-start.5 = (bf16[4,136,128]{2,1,0:T(8,128)(2,1)S(1)}, bf16[4,136,128]{2,1,0:T(8,128)(2,1)S(1)}, u32[]{:S(2)}, u32[]{:S(2)}) collective-permute-start(bf16[4,136,128]{2,1,0:T(8,128)(2,1)S(1)} %maximum_maximum_fusion.1), channel_id=1, source_target_pairs={{0,128},{64,192},{1,129},{65,193},{2,130},{66,194},{3,131},{67,195... | collective-permute-start | bytes 417800 | tf_op jit(solution)/shard_map/ppermute | solution.py:44
  33.0 1.3 collective-permute-start.7
  34.4 0.6 collective-permute-done.5
  35.1 1.3 collective-permute-done.7
  36.4 0.3 fusion.18
  36.7 2.0 collective-permute-start.8
  38.7 0.2 convolution_multiply_fusion
  39.0 0.3 convolution_bitcast_fusion.1
  39.2 0.6 collective-permute-done.8
  39.9 0.8 multiply_reduce_fusion
  40.7 0.8 copy_bitcast_fusion.2
  41.6 54.2 %all-gather.3.cloned.1.call-done = bf16[2048,1024]{1,0:T(8,128)(2,1)} async-done(((bf16[64,1024]{1,0:T(8,128)(2,1)}), bf16[2048,1024]{1,0:T(8,128)(2,1)}) %all-gather.3.cloned.1.call-update) | async-done | bytes 4194320 | tf_op jit(solution)/shard_map/all_gather | solution.py:156
  95.8 4.9 %convolution_bitcast_fusion = f32[192,2048]{1,0:T(8,128)} fusion(bf16[2048,1024]{1,0:T(8,128)(2,1)} %all-gather.3.cloned.1.call-done, bf16[1024,192]{0,1:T(8,128)(2,1)S(1)} %copy-done), kind=kOutput, calls=%fused_computation.4 | convolution fusion | flops 805306368 | bytes 6160384 | tf_op jit(solution)/shard_map/dot_general | solution.py:159
  101.2 1.1 reduce-window.6
  102.4 0.2 slice_reduce_fusion
  102.8 0.1 sub.61
  103.0 33.4 %reduce-scatter.2.cloned.1.call-done = f32[192,256]{1,0:T(8,128)} async-done(((f32[192,2048]{1,0:T(8,128)}), f32[192,256]{1,0:T(8,128)}) %reduce-scatter.2.cloned.1.call-update) | async-done | bytes 196624 | tf_op jit(solution)/shard_map/reduce_scatter | solution.py:158
  136.4 0.9 fusion.27
  137.4 0.4 fusion.4
  137.9 15.5 %all_to_all.5 = bf16[8,128,192]{1,2,0:T(8,128)(2,1)S(1)} all-to-all(bf16[8,128,192]{1,2,0:T(8,128)(2,1)S(1)} %bitcast.101), channel_id=1, replica_groups=mesh['seq_0'=4,'seq_1'=4,'seq_2'=2,'exp'=8] {'exp'}, dimensions={0} | all-to-all | bytes 786432 | tf_op jit(solution)/shard_map/all_to_all | solution.py:186
  153.4 0.8 copy_bitcast_fusion
  154.3 5.2 %collective-permute-start.9 = (f32[1024]{0:T(1024)S(1)}, f32[1024]{0:T(1024)S(1)}, u32[]{:S(2)}, u32[]{:S(2)}) collective-permute-start(f32[1024]{0:T(1024)S(1)} %fusion.10), channel_id=1, source_target_pairs={{0,8},{8,0},{1,9},{9,1},{2,10},{10,2},{3,11},{11,3},{4,12},{12,4},... | collective-permute-start | bytes 12296 | tf_op jit(solution)/shard_map/ppermute | solution.py:79
  159.5 0.8 collective-permute-done.9
  160.3 2.5 %collective-permute-start.12 = (f32[1024]{0:T(1024)S(1)}, f32[1024]{0:T(1024)S(1)}, u32[]{:S(2)}, u32[]{:S(2)}) collective-permute-start(f32[1024]{0:T(1024)S(1)} %add.156), channel_id=1, source_target_pairs={{0,48},{16,0},{32,16},{48,32},{1,49},{17,1},{33,17},{49,33},{2,50}... | collective-permute-start | bytes 12296 | tf_op jit(solution)/shard_map/ppermute | solution.py:79
  162.8 0.5 collective-permute-start.11
  163.3 0.6 collective-permute-start.10
  163.9 2.8 %collective-permute-done.11 = f32[1024]{0:T(1024)S(1)} collective-permute-done((f32[1024]{0:T(1024)S(1)}, f32[1024]{0:T(1024)S(1)}, u32[]{:S(2)}, u32[]{:S(2)}) %collective-permute-start.11) | collective-permute-done | bytes 4128 | tf_op jit(solution)/shard_map/ppermute | solution.py:79
  166.7 0.2 collective-permute-done.10
  167.0 2.4 collective-permute-start.15
  169.4 0.6 collective-permute-start.14
  170.0 0.6 collective-permute-start.13
  170.6 2.8 %collective-permute-done.14 = f32[1024]{0:T(1024)S(1)} collective-permute-done((f32[1024]{0:T(1024)S(1)}, f32[1024]{0:T(1024)S(1)}, u32[]{:S(2)}, u32[]{:S(2)}) %collective-permute-start.14) | collective-permute-done | bytes 4128 | tf_op jit(solution)/shard_map/ppermute | solution.py:79
  173.4 0.6 collective-permute-done.13
  174.1 49.5 %all-gather.5.cloned.1.call-done = bf16[1024,6144]{0,1:T(8,128)(2,1)} async-done(((bf16[1024,192]{0,1:T(8,128)(2,1)}), bf16[1024,6144]{0,1:T(8,128)(2,1)}) %all-gather.5.cloned.1.call-update) | async-done | bytes 12582928 | tf_op jit(solution)/shard_map/all_gather | solution.py:191
  223.6 12.5 %fusion = f32[576,1024]{1,0:T(8,128)S(1)} fusion(bf16[1024,6144]{0,1:T(8,128)(2,1)} %all-gather.5.cloned.1.call-done, bf16[288,6144]{1,0:T(8,128)(2,1)} %bitcast.105, bf16[288,6144]{1,0:T(8,128)(2,1)} %bitcast.106), kind=kOutput, calls=%fused_computation | convolution fusion | flops 7261913088 | bytes 22020096 | tf_op jit(solution)/shard_map/dot_general | solution.py:195
  236.0 1.2 fusion.11
  (74 shorter events, 2.8 us)
Async XLA Ops:
  7.2 88.7 %copy-start = (bf16[1024,192]{0,1:T(8,128)(2,1)S(1)}, bf16[1024,192]{0,1:T(8,128)(2,1)}, u32[]{:S(2)}) copy-start(bf16[1024,192]{0,1:T(8,128)(2,1)} %param.13) | copy-start | bytes 1179652
  7.2 88.7 %all-gather.3.cloned.1.call-start = ((), (), s32[]{:S(2)}) async-start(), calls=%async_computation.2 | async-start | bytes 4325376 | tf_op jit(solution)/shard_map/all_gather | solution.py:156
  8.1 5.3 %collective-permute-start = (f32[8]{0:T(128)S(1)}, f32[8]{0:T(128)S(1)}, u32[]{:S(2)}, u32[]{:S(2)}) collective-permute-start(f32[8]{0:T(128)S(1)} %fusion.55), channel_id=1, source_target_pairs={{0,8},{8,0},{1,9},{9,1},{2,10},{10,2},{3,11},{11,3},{4,12},{12,4},... | collective-permute-start | bytes 104 | tf_op jit(solution)/shard_map/ppermute | solution.py:72
  13.2 2.0 collective-permute-start.1
  15.3 23.4 %copy-start.2 = (bf16[64,1024]{1,0:T(8,128)(2,1)S(1)}, bf16[64,1024]{1,0:T(8,128)(2,1)}, u32[]{:S(2)}) copy-start(bf16[64,1024]{1,0:T(8,128)(2,1)} %param.10) | copy-start | bytes 393220
  15.3 23.4 %copy-start.6 = (bf16[64,1024]{1,0:T(8,128)(2,1)S(1)}, bf16[64,1024]{1,0:T(8,128)(2,1)}, u32[]{:S(2)}) copy-start(bf16[64,1024]{1,0:T(8,128)(2,1)} %param.9) | copy-start | bytes 393220
  15.4 23.6 %copy-start.1 = (bf16[64,1024]{1,0:T(8,128)(2,1)S(1)}, bf16[64,1024]{1,0:T(8,128)(2,1)}, u32[]{:S(2)}) copy-start(bf16[64,1024]{1,0:T(8,128)(2,1)} %param.11) | copy-start | bytes 393220
  15.7 6.9 %collective-permute-start.4 = (bf16[4,136,128]{2,1,0:T(8,128)(2,1)S(1)}, bf16[4,136,128]{2,1,0:T(8,128)(2,1)S(1)}, u32[]{:S(2)}, u32[]{:S(2)}) collective-permute-start(bf16[4,136,128]{2,1,0:T(8,128)(2,1)S(1)} %maximum_maximum_fusion), channel_id=1, source_target_pairs={{0,16},{16,32},{32,48},{48,0},{1,17},{17,33},{33,49},{49,1},{2,18}... | collective-permute-start | bytes 417800 | tf_op jit(solution)/shard_map/ppermute | solution.py:44
  15.8 8.9 %collective-permute-start.3 = (bf16[4,136,128]{2,1,0:T(8,128)(2,1)S(1)}, bf16[4,136,128]{2,1,0:T(8,128)(2,1)S(1)}, u32[]{:S(2)}, u32[]{:S(2)}) collective-permute-start(bf16[4,136,128]{2,1,0:T(8,128)(2,1)S(1)} %maximum_maximum_fusion), channel_id=1, source_target_pairs={{0,32},{16,48},{32,0},{48,16},{1,33},{17,49},{33,1},{49,17},{2,34}... | collective-permute-start | bytes 417800 | tf_op jit(solution)/shard_map/ppermute | solution.py:44
  17.9 7.4 %collective-permute-start.2 = (bf16[4,136,128]{2,1,0:T(8,128)(2,1)S(1)}, bf16[4,136,128]{2,1,0:T(8,128)(2,1)S(1)}, u32[]{:S(2)}, u32[]{:S(2)}) collective-permute-start(bf16[4,136,128]{2,1,0:T(8,128)(2,1)S(1)} %maximum_maximum_fusion), channel_id=1, source_target_pairs={{0,48},{16,0},{32,16},{48,32},{1,49},{17,1},{33,17},{49,33},{2,50}... | collective-permute-start | bytes 417800 | tf_op jit(solution)/shard_map/ppermute | solution.py:44
  26.2 8.2 %collective-permute-start.6 = (bf16[4,136,128]{2,1,0:T(8,128)(2,1)S(1)}, bf16[4,136,128]{2,1,0:T(8,128)(2,1)S(1)}, u32[]{:S(2)}, u32[]{:S(2)}) collective-permute-start(bf16[4,136,128]{2,1,0:T(8,128)(2,1)S(1)} %maximum_maximum_fusion.1), channel_id=1, source_target_pairs={{0,64},{64,128},{128,192},{1,65},{65,129},{129,193},{2,66},{66,130... | collective-permute-start | bytes 417800 | tf_op jit(solution)/shard_map/ppermute | solution.py:44
  28.6 6.4 %collective-permute-start.5 = (bf16[4,136,128]{2,1,0:T(8,128)(2,1)S(1)}, bf16[4,136,128]{2,1,0:T(8,128)(2,1)S(1)}, u32[]{:S(2)}, u32[]{:S(2)}) collective-permute-start(bf16[4,136,128]{2,1,0:T(8,128)(2,1)S(1)} %maximum_maximum_fusion.1), channel_id=1, source_target_pairs={{0,128},{64,192},{1,129},{65,193},{2,130},{66,194},{3,131},{67,195... | collective-permute-start | bytes 417800 | tf_op jit(solution)/shard_map/ppermute | solution.py:44
  33.0 3.5 %collective-permute-start.7 = (bf16[4,136,128]{2,1,0:T(8,128)(2,1)S(1)}, bf16[4,136,128]{2,1,0:T(8,128)(2,1)S(1)}, u32[]{:S(2)}, u32[]{:S(2)}) collective-permute-start(bf16[4,136,128]{2,1,0:T(8,128)(2,1)S(1)} %maximum_maximum_fusion.1), channel_id=1, source_target_pairs={{0,192},{1,193},{2,194},{3,195},{4,196},{5,197},{6,198},{7,199},{8... | collective-permute-start | bytes 417800 | tf_op jit(solution)/shard_map/ppermute | solution.py:44
  36.7 3.2 %collective-permute-start.8 = (f32[4,128,128]{2,1,0:T(8,128)S(1)}, f32[4,128,128]{2,1,0:T(8,128)S(1)}, u32[]{:S(2)}, u32[]{:S(2)}) collective-permute-start(f32[4,128,128]{2,1,0:T(8,128)S(1)} %fusion.18), channel_id=1, source_target_pairs={{0,8},{8,0},{1,9},{9,1},{2,10},{10,2},{3,11},{11,3},{4,12},{12,4},... | collective-permute-start | bytes 786440 | tf_op jit(solution)/shard_map/ppermute | solution.py:72
  41.5 59.3 %copy-start.5 = (s32[256,2]{0,1:T(2,128)S(1)}, s32[256,2]{0,1:T(2,128)}, u32[]{:S(2)}) copy-start(s32[256,2]{0,1:T(2,128)} %param.15) | copy-start | bytes 6148
  41.5 94.9 %copy-start.3 = (bf16[256,192]{0,1:T(8,128)(2,1)S(1)}, bf16[256,192]{0,1:T(8,128)(2,1)}, u32[]{:S(2)}) copy-start(bf16[256,192]{0,1:T(8,128)(2,1)} %param.14) | copy-start | bytes 294916
  41.6 94.9 %reduce-scatter.2.cloned.1.call-start = ((), (), s32[]{:S(2)}) async-start(), calls=%async_computation.3 | async-start | bytes 1769472 | tf_op jit(solution)/shard_map/reduce_scatter | solution.py:158
  100.7 122.8 %all-gather.5.cloned.1.call-start = ((), (), s32[]{:S(2)}) async-start(), calls=%async_computation.4 | async-start | bytes 12976128 | tf_op jit(solution)/shard_map/all_gather | solution.py:191
  137.4 98.7 %copy-start.4 = (bf16[256,192]{0,1:T(8,128)(2,1)}, bf16[256,192]{0,1:T(8,128)(2,1)S(1)}, u32[]{:S(2)}) copy-start(bf16[256,192]{0,1:T(8,128)(2,1)S(1)} %fusion.27) | copy-start | bytes 294916
  154.3 6.0 %collective-permute-start.9 = (f32[1024]{0:T(1024)S(1)}, f32[1024]{0:T(1024)S(1)}, u32[]{:S(2)}, u32[]{:S(2)}) collective-permute-start(f32[1024]{0:T(1024)S(1)} %fusion.10), channel_id=1, source_target_pairs={{0,8},{8,0},{1,9},{9,1},{2,10},{10,2},{3,11},{11,3},{4,12},{12,4},... | collective-permute-start | bytes 12296 | tf_op jit(solution)/shard_map/ppermute | solution.py:79
  160.3 3.6 %collective-permute-start.12 = (f32[1024]{0:T(1024)S(1)}, f32[1024]{0:T(1024)S(1)}, u32[]{:S(2)}, u32[]{:S(2)}) collective-permute-start(f32[1024]{0:T(1024)S(1)} %add.156), channel_id=1, source_target_pairs={{0,48},{16,0},{32,16},{48,32},{1,49},{17,1},{33,17},{49,33},{2,50}... | collective-permute-start | bytes 12296 | tf_op jit(solution)/shard_map/ppermute | solution.py:79
  162.8 4.0 %collective-permute-start.11 = (f32[1024]{0:T(1024)S(1)}, f32[1024]{0:T(1024)S(1)}, u32[]{:S(2)}, u32[]{:S(2)}) collective-permute-start(f32[1024]{0:T(1024)S(1)} %add.156), channel_id=1, source_target_pairs={{0,32},{16,48},{32,0},{48,16},{1,33},{17,49},{33,1},{49,17},{2,34}... | collective-permute-start | bytes 12296 | tf_op jit(solution)/shard_map/ppermute | solution.py:79
  163.3 3.7 %collective-permute-start.10 = (f32[1024]{0:T(1024)S(1)}, f32[1024]{0:T(1024)S(1)}, u32[]{:S(2)}, u32[]{:S(2)}) collective-permute-start(f32[1024]{0:T(1024)S(1)} %add.156), channel_id=1, source_target_pairs={{0,16},{16,32},{32,48},{48,0},{1,17},{17,33},{33,49},{49,1},{2,18}... | collective-permute-start | bytes 12296 | tf_op jit(solution)/shard_map/ppermute | solution.py:79
  167.0 3.6 %collective-permute-start.15 = (f32[1024]{0:T(1024)S(1)}, f32[1024]{0:T(1024)S(1)}, u32[]{:S(2)}, u32[]{:S(2)}) collective-permute-start(f32[1024]{0:T(1024)S(1)} %add_add_fusion), channel_id=1, source_target_pairs={{0,192},{64,0},{128,64},{192,128},{1,193},{65,1},{129,65},{193,129... | collective-permute-start | bytes 12296 | tf_op jit(solution)/shard_map/ppermute | solution.py:79
  169.4 4.1 %collective-permute-start.14 = (f32[1024]{0:T(1024)S(1)}, f32[1024]{0:T(1024)S(1)}, u32[]{:S(2)}, u32[]{:S(2)}) collective-permute-start(f32[1024]{0:T(1024)S(1)} %add_add_fusion), channel_id=1, source_target_pairs={{0,128},{64,192},{128,0},{192,64},{1,129},{65,193},{129,1},{193,65... | collective-permute-start | bytes 12296 | tf_op jit(solution)/shard_map/ppermute | solution.py:79
  170.0 4.1 %collective-permute-start.13 = (f32[1024]{0:T(1024)S(1)}, f32[1024]{0:T(1024)S(1)}, u32[]{:S(2)}, u32[]{:S(2)}) collective-permute-start(f32[1024]{0:T(1024)S(1)} %add_add_fusion), channel_id=1, source_target_pairs={{0,64},{64,128},{128,192},{192,0},{1,65},{65,129},{129,193},{193,1... | collective-permute-start | bytes 12296 | tf_op jit(solution)/shard_map/ppermute | solution.py:79
Sparse Core Ops, SparseCore 0:
  41.6 54.1 all-gather.2
  100.9 35.5 reduce-scatter.1
  154.4 69.1 all-gather.4

commit v10 on v8

--- a/solution.py
+++ b/solution.py
@@ -98,11 +98,21 @@
 def entering_state(decay, state):
     core = lax.axis_index("seq_2")
     half = decay.shape[0] // 2
-    other = (swap_cores(decay), swap_cores(state))
-    first = jax.tree.map(lambda mine, theirs: jnp.where(core == 0, mine, theirs), (decay, state), other)
-    second = jax.tree.map(lambda mine, theirs: jnp.where(core == 0, theirs, mine), (decay, state), other)
-    chip = link_states(first, second)
-    mine = jax.tree.map(lambda part: lax.dynamic_slice_in_dim(part, core * half, half, 0), chip)
+    other_decay = swap_cores(decay)
+    first_decay = jnp.where(core == 0, decay, other_decay)
+    second_decay = jnp.where(core == 0, other_decay, decay)
+    got = swap_cores(lax.dynamic_slice_in_dim(state, (1 - core) * half, half, 0))
+    kept = lax.dynamic_slice_in_dim(state, core * half, half, 0)
+    late = lax.ppermute(state[:half], "seq_2", [(0, 1)])
+    first = (
+        lax.dynamic_slice_in_dim(first_decay, core * half, half, 0),
+        jnp.where(core == 0, kept, got),
+    )
+    second = (
+        lax.dynamic_slice_in_dim(second_decay, core * half, half, 0),
+        jnp.where(core == 0, got, kept),
+    )
+    mine = link_states(first, second)
     along_y, row = prefix_over(packed_shifts(*mine, "seq_1"), lax.axis_index("seq_1"))
     along_x, _ = prefix_over(packed_shifts(*row, "seq_0"), lax.axis_index("seq_0"))
     chip_before = link_states(along_x, along_y)[1]
@@ -110,7 +120,8 @@
     whole = jnp.where(
         core == 0, jnp.concatenate([chip_before, theirs], 0), jnp.concatenate([theirs, chip_before], 0)
     )
-    return jnp.where(core == 0, whole, first[0][:, None, None] * whole + first[1])
+    first_state = jnp.concatenate([late, got], 0)
+    return jnp.where(core == 0, whole, first_decay[:, None, None] * whole + first_state)
 
 
 def finish_rows(gate_sum, up_sum, squares):

time: 241 us -> 241 us (level)
  transfers between devices with their start and end apart: 19 -> 20, of which waited for: 15 -> 14; matrix products, arithmetic and copies ran while one was open for 2% -> 2% of each run, Pallas kernels for 0% -> 0%
where the time goes in v10:
time: 241 us
  waiting for transfers between devices  155 us (64%)
  starting transfers between devices  26.9 us (11%)
  matrix products  20.8 us (9%)
  blocking collectives  15.4 us (6%)
  between operations  14.1 us (6%)
  other arithmetic  5.86 us (2%)
  local copies, waits for them, and re-layouts  3.18 us (1%)
    all_gather x1, waiting for transfers between devices, body(): gathered = lax.all_gather(normed, SEQ, axis=0, tiled=True)  52.7 us
    all_gather x1, waiting for transfers between devices, body(): row_block = lax.all_gather(slices, SEQ, axis=1, tiled=True)  49.3 us
    reduce_scatter x1, waiting for transfers between devices, body(): lax.psum_scatter(lax.dot_general(out_weight, row_block, (((0,), (1,)), ((...  33.5 us
    all_to_all x1, blocking collectives, body(): lax.all_to_all(buffer.reshape(experts, capacity, columns), 'exp', split_a...  15.4 us
    ppermute x7, starting transfers between devices, ring_sum(): lax.ppermute(part, axis, [(i, (i + d) % peers) for i in range(peers)])  12.5 us
    dot_general x1, matrix products, body(): lax.dot_general(jnp.concatenate([w_gate, w_up], 0), row_block, contract_l...  12.5 us
    ppermute x6, waiting for transfers between devices, ring_shifts(): lax.ppermute(part, axis, [(i, (i + d) % peers) for i in range(peers)])  9.57 us
    ppermute x6, starting transfers between devices, ring_shifts(): lax.ppermute(part, axis, [(i, (i + d) % peers) for i in range(peers)])  7.48 us
  transfers between devices with their start and end apart: 20, of which 14 were waited for; matrix products, arithmetic and copies ran while one was open for 2% of the time, Pallas kernels for 0%

profile of v10, /device:TPU:1, one launch (start us, length us, event | category | flops | bytes accessed | tf_op | source)
XLA Modules:
  0.0 240.9 jit_solution(6649644137927364437)
XLA Ops:
  7.2 0.8 copy.85
  8.1 3.3 %collective-permute-start = (f32[8]{0:T(128)S(1)}, f32[8]{0:T(128)S(1)}, u32[]{:S(2)}, u32[]{:S(2)}) collective-permute-start(f32[8]{0:T(128)S(1)} %fusion.56), channel_id=1, source_target_pairs={{0,8},{8,0},{1,9},{9,1},{2,10},{10,2},{3,11},{11,3},{4,12},{12,4},... | collective-permute-start | bytes 104 | tf_op jit(solution)/shard_map/ppermute | solution.py:71
  11.5 1.7 fusion.24
  13.5 1.3 collective-permute-done.1
  15.3 2.2 collective-permute-start.3
  17.5 1.1 collective-permute-start.2
  18.6 3.6 %collective-permute-done.4 = bf16[4,136,128]{2,1,0:T(8,128)(2,1)S(1)} collective-permute-done((bf16[4,136,128]{2,1,0:T(8,128)(2,1)S(1)}, bf16[4,136,128]{2,1,0:T(8,128)(2,1)S(1)}, u32[]{:S(2)}, u32[]{:S(2)}) %collective-permute-start.4) | collective-permute-done | bytes 139296 | tf_op jit(solution)/shard_map/ppermute | solution.py:44
  22.2 2.0 collective-permute-done.3
  24.2 0.7 collective-permute-done.2
  25.0 0.1 fusion.46
  25.2 0.4 add_convert_fusion
  25.8 0.6 collective-permute-start.6
  26.3 2.5 %collective-permute-start.5 = (bf16[4,136,128]{2,1,0:T(8,128)(2,1)S(1)}, bf16[4,136,128]{2,1,0:T(8,128)(2,1)S(1)}, u32[]{:S(2)}, u32[]{:S(2)}) collective-permute-start(bf16[4,136,128]{2,1,0:T(8,128)(2,1)S(1)} %maximum_maximum_fusion.1), channel_id=1, source_target_pairs={{0,128},{64,192},{128,0},{192,64},{1,129},{65,193},{129,1},{193,65... | collective-permute-start | bytes 417800 | tf_op jit(solution)/shard_map/ppermute | solution.py:44
  28.8 1.2 collective-permute-start.7
  29.9 1.3 collective-permute-start.9
  31.3 3.3 %collective-permute-done.5 = bf16[4,136,128]{2,1,0:T(8,128)(2,1)S(1)} collective-permute-done((bf16[4,136,128]{2,1,0:T(8,128)(2,1)S(1)}, bf16[4,136,128]{2,1,0:T(8,128)(2,1)S(1)}, u32[]{:S(2)}, u32[]{:S(2)}) %collective-permute-start.5) | collective-permute-done | bytes 139296 | tf_op jit(solution)/shard_map/ppermute | solution.py:44
  34.7 0.3 fusion.20
  34.9 2.1 collective-permute-start.8
  37.2 0.2 convolution_multiply_fusion
  37.4 0.8 collective-permute-done.8
  38.2 0.7 convolution_bitcast_fusion.2
  39.0 0.4 multiply_reduce_fusion
  39.4 0.8 copy_bitcast_fusion.2
  40.2 52.7 %all-gather.3.cloned.1.call-done = bf16[2048,1024]{1,0:T(8,128)(2,1)} async-done(((bf16[64,1024]{1,0:T(8,128)(2,1)}), bf16[2048,1024]{1,0:T(8,128)(2,1)}) %all-gather.3.cloned.1.call-update) | async-done | bytes 4194320 | tf_op jit(solution)/shard_map/all_gather | solution.py:166
  92.9 4.9 %convolution_bitcast_fusion = f32[192,2048]{1,0:T(8,128)} fusion(bf16[2048,1024]{1,0:T(8,128)(2,1)} %all-gather.3.cloned.1.call-done, bf16[1024,192]{0,1:T(8,128)(2,1)S(1)} %copy-done), kind=kOutput, calls=%fused_computation.4 | convolution fusion | flops 805306368 | bytes 6160384 | tf_op jit(solution)/shard_map/dot_general | solution.py:169
  98.3 1.1 reduce-window.6
  99.5 0.2 slice_reduce_fusion
  99.8 0.1 sub.65
  100.1 33.5 %reduce-scatter.2.cloned.1.call-done = f32[192,256]{1,0:T(8,128)} async-done(((f32[192,2048]{1,0:T(8,128)}), f32[192,256]{1,0:T(8,128)}) %reduce-scatter.2.cloned.1.call-update) | async-done | bytes 196624 | tf_op jit(solution)/shard_map/reduce_scatter | solution.py:168
  133.6 0.9 fusion.28
  134.5 0.4 fusion.4
  135.0 15.4 %all_to_all.5 = bf16[8,128,192]{1,2,0:T(8,128)(2,1)S(1)} all-to-all(bf16[8,128,192]{1,2,0:T(8,128)(2,1)S(1)} %bitcast.99), channel_id=1, replica_groups=mesh['seq_0'=4,'seq_1'=4,'seq_2'=2,'exp'=8] {'exp'}, dimensions={0} | all-to-all | bytes 786432 | tf_op jit(solution)/shard_map/all_to_all | solution.py:196
  150.5 0.8 copy_bitcast_fusion
  151.4 5.3 %collective-permute-start.10 = (f32[1024]{0:T(1024)S(1)}, f32[1024]{0:T(1024)S(1)}, u32[]{:S(2)}, u32[]{:S(2)}) collective-permute-start(f32[1024]{0:T(1024)S(1)} %fusion.10), channel_id=1, source_target_pairs={{0,8},{8,0},{1,9},{9,1},{2,10},{10,2},{3,11},{11,3},{4,12},{12,4},... | collective-permute-start | bytes 12296 | tf_op jit(solution)/shard_map/ppermute | solution.py:78
  156.7 0.8 collective-permute-done.10
  157.6 2.5 %collective-permute-start.13 = (f32[1024]{0:T(1024)S(1)}, f32[1024]{0:T(1024)S(1)}, u32[]{:S(2)}, u32[]{:S(2)}) collective-permute-start(f32[1024]{0:T(1024)S(1)} %add.161), channel_id=1, source_target_pairs={{0,48},{16,0},{32,16},{48,32},{1,49},{17,1},{33,17},{49,33},{2,50}... | collective-permute-start | bytes 12296 | tf_op jit(solution)/shard_map/ppermute | solution.py:78
  160.0 0.5 collective-permute-start.12
  160.6 0.6 collective-permute-start.11
  161.2 2.8 %collective-permute-done.12 = f32[1024]{0:T(1024)S(1)} collective-permute-done((f32[1024]{0:T(1024)S(1)}, f32[1024]{0:T(1024)S(1)}, u32[]{:S(2)}, u32[]{:S(2)}) %collective-permute-start.12) | collective-permute-done | bytes 4128 | tf_op jit(solution)/shard_map/ppermute | solution.py:78
  164.0 0.2 collective-permute-done.11
  164.3 2.4 collective-permute-start.16
  166.6 0.6 collective-permute-start.15
  167.2 0.6 collective-permute-start.14
  167.8 2.9 %collective-permute-done.15 = f32[1024]{0:T(1024)S(1)} collective-permute-done((f32[1024]{0:T(1024)S(1)}, f32[1024]{0:T(1024)S(1)}, u32[]{:S(2)}, u32[]{:S(2)}) %collective-permute-start.15) | collective-permute-done | bytes 4128 | tf_op jit(solution)/shard_map/ppermute | solution.py:78
  170.7 0.6 collective-permute-done.14
  171.3 49.3 %all-gather.5.cloned.1.call-done = bf16[1024,6144]{0,1:T(8,128)(2,1)} async-done(((bf16[1024,192]{0,1:T(8,128)(2,1)}), bf16[1024,6144]{0,1:T(8,128)(2,1)}) %all-gather.5.cloned.1.call-update) | async-done | bytes 12582928 | tf_op jit(solution)/shard_map/all_gather | solution.py:201
  220.7 12.5 %fusion = f32[576,1024]{1,0:T(8,128)S(1)} fusion(bf16[1024,6144]{0,1:T(8,128)(2,1)} %all-gather.5.cloned.1.call-done, bf16[288,6144]{1,0:T(8,128)(2,1)} %bitcast.103, bf16[288,6144]{1,0:T(8,128)(2,1)} %bitcast.104), kind=kOutput, calls=%fused_computation | convolution fusion | flops 7261913088 | bytes 22020096 | tf_op jit(solution)/shard_map/dot_general | solution.py:205
  233.1 1.2 fusion.11
  (75 shorter events, 2.6 us)
Async XLA Ops:
  7.2 85.7 %copy-start = (bf16[1024,192]{0,1:T(8,128)(2,1)S(1)}, bf16[1024,192]{0,1:T(8,128)(2,1)}, u32[]{:S(2)}) copy-start(bf16[1024,192]{0,1:T(8,128)(2,1)} %param.13) | copy-start | bytes 1179652
  7.2 85.7 %all-gather.3.cloned.1.call-start = ((), (), s32[]{:S(2)}) async-start(), calls=%async_computation.2 | async-start | bytes 4325376 | tf_op jit(solution)/shard_map/all_gather | solution.py:166
  8.1 5.3 %collective-permute-start = (f32[8]{0:T(128)S(1)}, f32[8]{0:T(128)S(1)}, u32[]{:S(2)}, u32[]{:S(2)}) collective-permute-start(f32[8]{0:T(128)S(1)} %fusion.56), channel_id=1, source_target_pairs={{0,8},{8,0},{1,9},{9,1},{2,10},{10,2},{3,11},{11,3},{4,12},{12,4},... | collective-permute-start | bytes 104 | tf_op jit(solution)/shard_map/ppermute | solution.py:71
  13.2 1.6 collective-permute-start.1
  14.9 22.3 %copy-start.2 = (bf16[64,1024]{1,0:T(8,128)(2,1)S(1)}, bf16[64,1024]{1,0:T(8,128)(2,1)}, u32[]{:S(2)}) copy-start(bf16[64,1024]{1,0:T(8,128)(2,1)} %param.10) | copy-start | bytes 393220
  14.9 22.3 %copy-start.6 = (bf16[64,1024]{1,0:T(8,128)(2,1)S(1)}, bf16[64,1024]{1,0:T(8,128)(2,1)}, u32[]{:S(2)}) copy-start(bf16[64,1024]{1,0:T(8,128)(2,1)} %param.9) | copy-start | bytes 393220
  15.2 6.9 %collective-permute-start.4 = (bf16[4,136,128]{2,1,0:T(8,128)(2,1)S(1)}, bf16[4,136,128]{2,1,0:T(8,128)(2,1)S(1)}, u32[]{:S(2)}, u32[]{:S(2)}) collective-permute-start(bf16[4,136,128]{2,1,0:T(8,128)(2,1)S(1)} %maximum_maximum_fusion), channel_id=1, source_target_pairs={{0,16},{16,32},{32,48},{48,0},{1,17},{17,33},{33,49},{49,1},{2,18}... | collective-permute-start | bytes 417800 | tf_op jit(solution)/shard_map/ppermute | solution.py:44
  15.3 8.9 %collective-permute-start.3 = (bf16[4,136,128]{2,1,0:T(8,128)(2,1)S(1)}, bf16[4,136,128]{2,1,0:T(8,128)(2,1)S(1)}, u32[]{:S(2)}, u32[]{:S(2)}) collective-permute-start(bf16[4,136,128]{2,1,0:T(8,128)(2,1)S(1)} %maximum_maximum_fusion), channel_id=1, source_target_pairs={{0,32},{16,48},{32,0},{48,16},{1,33},{17,49},{33,1},{49,17},{2,34}... | collective-permute-start | bytes 417800 | tf_op jit(solution)/shard_map/ppermute | solution.py:44
  17.5 7.4 %collective-permute-start.2 = (bf16[4,136,128]{2,1,0:T(8,128)(2,1)S(1)}, bf16[4,136,128]{2,1,0:T(8,128)(2,1)S(1)}, u32[]{:S(2)}, u32[]{:S(2)}) collective-permute-start(bf16[4,136,128]{2,1,0:T(8,128)(2,1)S(1)} %maximum_maximum_fusion), channel_id=1, source_target_pairs={{0,48},{16,0},{32,16},{48,32},{1,49},{17,1},{33,17},{49,33},{2,50}... | collective-permute-start | bytes 417800 | tf_op jit(solution)/shard_map/ppermute | solution.py:44
  25.1 13.8 %copy-start.1 = (bf16[64,1024]{1,0:T(8,128)(2,1)S(1)}, bf16[64,1024]{1,0:T(8,128)(2,1)}, u32[]{:S(2)}) copy-start(bf16[64,1024]{1,0:T(8,128)(2,1)} %param.11) | copy-start | bytes 393220
  25.8 5.5 %collective-permute-start.6 = (bf16[4,136,128]{2,1,0:T(8,128)(2,1)S(1)}, bf16[4,136,128]{2,1,0:T(8,128)(2,1)S(1)}, u32[]{:S(2)}, u32[]{:S(2)}) collective-permute-start(bf16[4,136,128]{2,1,0:T(8,128)(2,1)S(1)} %maximum_maximum_fusion.1), channel_id=1, source_target_pairs={{0,64},{64,128},{128,192},{192,0},{1,65},{65,129},{129,193},{193,1... | collective-permute-start | bytes 417800 | tf_op jit(solution)/shard_map/ppermute | solution.py:44
  26.3 8.2 %collective-permute-start.5 = (bf16[4,136,128]{2,1,0:T(8,128)(2,1)S(1)}, bf16[4,136,128]{2,1,0:T(8,128)(2,1)S(1)}, u32[]{:S(2)}, u32[]{:S(2)}) collective-permute-start(bf16[4,136,128]{2,1,0:T(8,128)(2,1)S(1)} %maximum_maximum_fusion.1), channel_id=1, source_target_pairs={{0,128},{64,192},{128,0},{192,64},{1,129},{65,193},{129,1},{193,65... | collective-permute-start | bytes 417800 | tf_op jit(solution)/shard_map/ppermute | solution.py:44
  28.8 5.9 %collective-permute-start.7 = (bf16[4,136,128]{2,1,0:T(8,128)(2,1)S(1)}, bf16[4,136,128]{2,1,0:T(8,128)(2,1)S(1)}, u32[]{:S(2)}, u32[]{:S(2)}) collective-permute-start(bf16[4,136,128]{2,1,0:T(8,128)(2,1)S(1)} %maximum_maximum_fusion.1), channel_id=1, source_target_pairs={{0,192},{64,0},{128,64},{192,128},{1,193},{65,1},{129,65},{193,129... | collective-permute-start | bytes 417800 | tf_op jit(solution)/shard_map/ppermute | solution.py:44
  29.9 7.5 %collective-permute-start.9 = (f32[4,128,128]{2,1,0:T(8,128)S(1)}, f32[4,128,128]{2,1,0:T(8,128)S(1)}, u32[]{:S(2)}, u32[]{:S(2)}) collective-permute-start(f32[4,128,128]{2,1,0:T(8,128)S(1)} %get-tuple-element.20), channel_id=1, source_target_pairs={{0,8},{1,9},{2,10},{3,11},{4,12},{5,13},{6,14},{7,15},{16,24},{17,... | collective-permute-start | bytes 786440 | tf_op jit(solution)/shard_map/ppermute | solution.py:106
  34.9 3.3 %collective-permute-start.8 = (f32[4,128,128]{2,1,0:T(8,128)S(1)}, f32[4,128,128]{2,1,0:T(8,128)S(1)}, u32[]{:S(2)}, u32[]{:S(2)}) collective-permute-start(f32[4,128,128]{2,1,0:T(8,128)S(1)} %fusion.20), channel_id=1, source_target_pairs={{0,8},{8,0},{1,9},{9,1},{2,10},{10,2},{3,11},{11,3},{4,12},{12,4},... | collective-permute-start | bytes 786440 | tf_op jit(solution)/shard_map/ppermute | solution.py:71
  40.2 57.7 %copy-start.5 = (s32[256,2]{0,1:T(2,128)S(1)}, s32[256,2]{0,1:T(2,128)}, u32[]{:S(2)}) copy-start(s32[256,2]{0,1:T(2,128)} %param.15) | copy-start | bytes 6148
  40.2 93.4 %copy-start.3 = (bf16[256,192]{0,1:T(8,128)(2,1)S(1)}, bf16[256,192]{0,1:T(8,128)(2,1)}, u32[]{:S(2)}) copy-start(bf16[256,192]{0,1:T(8,128)(2,1)} %param.14) | copy-start | bytes 294916
  40.2 93.4 %reduce-scatter.2.cloned.1.call-start = ((), (), s32[]{:S(2)}) async-start(), calls=%async_computation.3 | async-start | bytes 1769472 | tf_op jit(solution)/shard_map/reduce_scatter | solution.py:168
  97.8 122.8 %all-gather.5.cloned.1.call-start = ((), (), s32[]{:S(2)}) async-start(), calls=%async_computation.4 | async-start | bytes 12976128 | tf_op jit(solution)/shard_map/all_gather | solution.py:201
  134.5 98.6 %copy-start.4 = (bf16[256,192]{0,1:T(8,128)(2,1)}, bf16[256,192]{0,1:T(8,128)(2,1)S(1)}, u32[]{:S(2)}) copy-start(bf16[256,192]{0,1:T(8,128)(2,1)S(1)} %fusion.28) | copy-start | bytes 294916
  151.4 6.2 %collective-permute-start.10 = (f32[1024]{0:T(1024)S(1)}, f32[1024]{0:T(1024)S(1)}, u32[]{:S(2)}, u32[]{:S(2)}) collective-permute-start(f32[1024]{0:T(1024)S(1)} %fusion.10), channel_id=1, source_target_pairs={{0,8},{8,0},{1,9},{9,1},{2,10},{10,2},{3,11},{11,3},{4,12},{12,4},... | collective-permute-start | bytes 12296 | tf_op jit(solution)/shard_map/ppermute | solution.py:78
  157.6 3.6 %collective-permute-start.13 = (f32[1024]{0:T(1024)S(1)}, f32[1024]{0:T(1024)S(1)}, u32[]{:S(2)}, u32[]{:S(2)}) collective-permute-start(f32[1024]{0:T(1024)S(1)} %add.161), channel_id=1, source_target_pairs={{0,48},{16,0},{32,16},{48,32},{1,49},{17,1},{33,17},{49,33},{2,50}... | collective-permute-start | bytes 12296 | tf_op jit(solution)/shard_map/ppermute | solution.py:78
  160.0 4.0 %collective-permute-start.12 = (f32[1024]{0:T(1024)S(1)}, f32[1024]{0:T(1024)S(1)}, u32[]{:S(2)}, u32[]{:S(2)}) collective-permute-start(f32[1024]{0:T(1024)S(1)} %add.161), channel_id=1, source_target_pairs={{0,32},{16,48},{32,0},{48,16},{1,33},{17,49},{33,1},{49,17},{2,34}... | collective-permute-start | bytes 12296 | tf_op jit(solution)/shard_map/ppermute | solution.py:78
  160.6 3.7 %collective-permute-start.11 = (f32[1024]{0:T(1024)S(1)}, f32[1024]{0:T(1024)S(1)}, u32[]{:S(2)}, u32[]{:S(2)}) collective-permute-start(f32[1024]{0:T(1024)S(1)} %add.161), channel_id=1, source_target_pairs={{0,16},{16,32},{32,48},{48,0},{1,17},{17,33},{33,49},{49,1},{2,18}... | collective-permute-start | bytes 12296 | tf_op jit(solution)/shard_map/ppermute | solution.py:78
  164.3 3.6 %collective-permute-start.16 = (f32[1024]{0:T(1024)S(1)}, f32[1024]{0:T(1024)S(1)}, u32[]{:S(2)}, u32[]{:S(2)}) collective-permute-start(f32[1024]{0:T(1024)S(1)} %add_add_fusion), channel_id=1, source_target_pairs={{0,192},{64,0},{128,64},{192,128},{1,193},{65,1},{129,65},{193,129... | collective-permute-start | bytes 12296 | tf_op jit(solution)/shard_map/ppermute | solution.py:78
  166.6 4.1 %collective-permute-start.15 = (f32[1024]{0:T(1024)S(1)}, f32[1024]{0:T(1024)S(1)}, u32[]{:S(2)}, u32[]{:S(2)}) collective-permute-start(f32[1024]{0:T(1024)S(1)} %add_add_fusion), channel_id=1, source_target_pairs={{0,128},{64,192},{128,0},{192,64},{1,129},{65,193},{129,1},{193,65... | collective-permute-start | bytes 12296 | tf_op jit(solution)/shard_map/ppermute | solution.py:78
  167.2 4.1 %collective-permute-start.14 = (f32[1024]{0:T(1024)S(1)}, f32[1024]{0:T(1024)S(1)}, u32[]{:S(2)}, u32[]{:S(2)}) collective-permute-start(f32[1024]{0:T(1024)S(1)} %add_add_fusion), channel_id=1, source_target_pairs={{0,64},{64,128},{128,192},{192,0},{1,65},{65,129},{129,193},{193,1... | collective-permute-start | bytes 12296 | tf_op jit(solution)/shard_map/ppermute | solution.py:78
Sparse Core Ops, SparseCore 0:
  40.3 52.5 all-gather.2
  97.9 35.5 reduce-scatter.1
  151.4 69.1 all-gather.4

commit v11 on v8

--- a/solution.py
+++ b/solution.py
@@ -107,10 +107,13 @@
     along_x, _ = prefix_over(packed_shifts(*row, "seq_0"), lax.axis_index("seq_0"))
     chip_before = link_states(along_x, along_y)[1]
     theirs = swap_cores(chip_before)
-    whole = jnp.where(
-        core == 0, jnp.concatenate([chip_before, theirs], 0), jnp.concatenate([theirs, chip_before], 0)
-    )
-    return jnp.where(core == 0, whole, first[0][:, None, None] * whole + first[1])
+
+    def finish(part, start):
+        decay_part = lax.dynamic_slice_in_dim(first[0], start, half, 0)
+        state_part = lax.dynamic_slice_in_dim(first[1], start, half, 0)
+        return jnp.where(core == 0, part, decay_part[:, None, None] * part + state_part)
+
+    return (finish(chip_before, core * half), finish(theirs, (1 - core) * half))
 
 
 def finish_rows(gate_sum, up_sum, squares):
@@ -138,12 +141,24 @@
     closing = cumulative[-1]
     key_scaled = keys_here * jnp.exp(closing[None, :] - cumulative)[:, :, None]
     local_state = jnp.einsum("shd,she->hde", key_scaled, values_here, precision=precise)
-    entering = entering_state(jnp.exp(closing), local_state)
+    own_heads, other_heads = entering_state(jnp.exp(closing), local_state)
     later = lax.broadcasted_iota(jnp.int32, (positions, positions), 0)
     earlier = lax.broadcasted_iota(jnp.int32, (positions, positions), 1)
     causal = (later >= earlier)[None]
-    carried = jnp.einsum(
-        "thd,hde->the", queries * jnp.exp(cumulative)[:, :, None], entering, precision=precise
+    core = lax.axis_index("seq_2")
+    half = heads_here // 2
+    scaled = queries * jnp.exp(cumulative)[:, :, None]
+
+    def carry(part, start):
+        block = lax.dynamic_slice_in_dim(scaled, start, half, 1)
+        return jnp.einsum("thd,hde->the", block, part, precision=precise)
+
+    own_carried = carry(own_heads, core * half)
+    other_carried = carry(other_heads, (1 - core) * half)
+    carried = jnp.where(
+        core == 0,
+        jnp.concatenate([own_carried, other_carried], 1),
+        jnp.concatenate([other_carried, own_carried], 1),
     )
     scores = jnp.einsum("thd,shd->hts", queries, keys_here, precision=precise)
     spread = cumulative.T[:, :, None] - cumulative.T[:, None, :]

time: 241 us -> 241 us (level)
  transfers between devices with their start and end apart: 19 -> 19, of which waited for: 15 -> 14; matrix products, arithmetic and copies ran while one was open for 2% -> 2% of each run, Pallas kernels for 0% -> 0%
where the time goes in v11:
time: 241 us
  waiting for transfers between devices  155 us (64%)
  starting transfers between devices  26 us (11%)
  matrix products  20.9 us (9%)
  blocking collectives  15.5 us (6%)
  between operations  14.1 us (6%)
  other arithmetic  6.04 us (3%)
  local copies, waits for them, and re-layouts  3.36 us (1%)
    all_gather x1, waiting for transfers between devices, body(): gathered = lax.all_gather(normed, SEQ, axis=0, tiled=True)  51.3 us
    all_gather x1, waiting for transfers between devices, body(): row_block = lax.all_gather(slices, SEQ, axis=1, tiled=True)  49.3 us
    reduce_scatter x1, waiting for transfers between devices, body(): lax.psum_scatter(lax.dot_general(out_weight, row_block, (((0,), (1,)), ((...  33.5 us
    all_to_all x1, blocking collectives, body(): lax.all_to_all(buffer.reshape(experts, capacity, columns), 'exp', split_a...  15.5 us
    dot_general x1, matrix products, body(): lax.dot_general(jnp.concatenate([w_gate, w_up], 0), row_block, contract_l...  12.5 us
    ppermute x7, starting transfers between devices, ring_sum(): lax.ppermute(part, axis, [(i, (i + d) % peers) for i in range(peers)])  12.5 us
    ppermute x6, waiting for transfers between devices, ring_shifts(): lax.ppermute(part, axis, [(i, (i + d) % peers) for i in range(peers)])  11.4 us
    ppermute x7, waiting for transfers between devices, ring_sum(): lax.ppermute(part, axis, [(i, (i + d) % peers) for i in range(peers)])  7.46 us
  transfers between devices with their start and end apart: 19, of which 14 were waited for; matrix products, arithmetic and copies ran while one was open for 2% of the time, Pallas kernels for 0%

profile of v11, /device:TPU:1, one launch (start us, length us, event | category | flops | bytes accessed | tf_op | source)
XLA Modules:
  0.0 241.0 jit_solution(6042356797282345590)
XLA Ops:
  7.2 0.8 copy.84
  8.2 3.3 %collective-permute-start = (f32[8]{0:T(128)S(1)}, f32[8]{0:T(128)S(1)}, u32[]{:S(2)}, u32[]{:S(2)}) collective-permute-start(f32[8]{0:T(128)S(1)} %fusion.60), channel_id=1, source_target_pairs={{0,8},{8,0},{1,9},{9,1},{2,10},{10,2},{3,11},{11,3},{4,12},{12,4},... | collective-permute-start | bytes 104 | tf_op jit(solution)/shard_map/ppermute | solution.py:71
  11.6 1.7 fusion.24
  13.8 1.5 collective-permute-done.1
  15.8 2.2 collective-permute-start.3
  17.9 0.2 convolution_multiply_fusion
  18.1 1.1 collective-permute-start.2
  19.3 3.3 %collective-permute-done.4 = bf16[4,136,128]{2,1,0:T(8,128)(2,1)S(1)} collective-permute-done((bf16[4,136,128]{2,1,0:T(8,128)(2,1)S(1)}, bf16[4,136,128]{2,1,0:T(8,128)(2,1)S(1)}, u32[]{:S(2)}, u32[]{:S(2)}) %collective-permute-start.4) | collective-permute-done | bytes 139296 | tf_op jit(solution)/shard_map/ppermute | solution.py:44
  22.6 2.0 collective-permute-done.3
  24.7 0.7 collective-permute-done.2
  25.4 0.1 fusion.49
  25.6 0.3 add_convert_fusion
  26.2 1.9 collective-permute-start.7
  28.0 1.7 collective-permute-start.5
  29.9 5.5 %collective-permute-done.6 = bf16[4,136,128]{2,1,0:T(8,128)(2,1)S(1)} collective-permute-done((bf16[4,136,128]{2,1,0:T(8,128)(2,1)S(1)}, bf16[4,136,128]{2,1,0:T(8,128)(2,1)S(1)}, u32[]{:S(2)}, u32[]{:S(2)}) %collective-permute-start.6) | collective-permute-done | bytes 139296 | tf_op jit(solution)/shard_map/ppermute | solution.py:44
  35.5 0.3 fusion.15
  35.8 3.0 %collective-permute-start.8 = (f32[4,128,128]{2,1,0:T(8,128)S(1)}, f32[4,128,128]{2,1,0:T(8,128)S(1)}, u32[]{:S(2)}, u32[]{:S(2)}) collective-permute-start(f32[4,128,128]{2,1,0:T(8,128)S(1)} %fusion.15), channel_id=1, source_target_pairs={{0,8},{8,0},{1,9},{9,1},{2,10},{10,2},{3,11},{11,3},{4,12},{12,4},... | collective-permute-start | bytes 786440 | tf_op jit(solution)/shard_map/ppermute | solution.py:71
  38.9 0.4 convolution_bitcast_fusion.3
  39.4 0.6 collective-permute-done.8
  40.0 0.4 convolution_bitcast_fusion.2
  40.5 0.4 multiply_reduce_fusion
  40.8 0.8 copy_bitcast_fusion.2
  41.7 51.3 %all-gather.3.cloned.1.call-done = bf16[2048,1024]{1,0:T(8,128)(2,1)} async-done(((bf16[64,1024]{1,0:T(8,128)(2,1)}), bf16[2048,1024]{1,0:T(8,128)(2,1)}) %all-gather.3.cloned.1.call-update) | async-done | bytes 4194320 | tf_op jit(solution)/shard_map/all_gather | solution.py:170
  93.0 4.9 %convolution_bitcast_fusion = f32[192,2048]{1,0:T(8,128)} fusion(bf16[2048,1024]{1,0:T(8,128)(2,1)} %all-gather.3.cloned.1.call-done, bf16[1024,192]{0,1:T(8,128)(2,1)S(1)} %copy-done), kind=kOutput, calls=%fused_computation.4 | convolution fusion | flops 805306368 | bytes 6160384 | tf_op jit(solution)/shard_map/dot_general | solution.py:173
  98.1 0.1 eq.70
  98.4 1.1 reduce-window.6
  99.6 0.2 slice_reduce_fusion
  99.9 0.1 sub.66
  100.2 33.5 %reduce-scatter.2.cloned.1.call-done = f32[192,256]{1,0:T(8,128)} async-done(((f32[192,2048]{1,0:T(8,128)}), f32[192,256]{1,0:T(8,128)}) %reduce-scatter.2.cloned.1.call-update) | async-done | bytes 196624 | tf_op jit(solution)/shard_map/reduce_scatter | solution.py:172
  133.6 0.9 fusion.28
  134.6 0.4 fusion.4
  135.1 15.5 %all_to_all.5 = bf16[8,128,192]{1,2,0:T(8,128)(2,1)S(1)} all-to-all(bf16[8,128,192]{1,2,0:T(8,128)(2,1)S(1)} %bitcast.99), channel_id=1, replica_groups=mesh['seq_0'=4,'seq_1'=4,'seq_2'=2,'exp'=8] {'exp'}, dimensions={0} | all-to-all | bytes 786432 | tf_op jit(solution)/shard_map/all_to_all | solution.py:200
  150.6 0.8 copy_bitcast_fusion
  151.5 5.3 %collective-permute-start.9 = (f32[1024]{0:T(1024)S(1)}, f32[1024]{0:T(1024)S(1)}, u32[]{:S(2)}, u32[]{:S(2)}) collective-permute-start(f32[1024]{0:T(1024)S(1)} %fusion.10), channel_id=1, source_target_pairs={{0,8},{8,0},{1,9},{9,1},{2,10},{10,2},{3,11},{11,3},{4,12},{12,4},... | collective-permute-start | bytes 12296 | tf_op jit(solution)/shard_map/ppermute | solution.py:78
  156.8 0.8 collective-permute-done.9
  157.7 2.5 %collective-permute-start.12 = (f32[1024]{0:T(1024)S(1)}, f32[1024]{0:T(1024)S(1)}, u32[]{:S(2)}, u32[]{:S(2)}) collective-permute-start(f32[1024]{0:T(1024)S(1)} %add.169), channel_id=1, source_target_pairs={{0,48},{16,0},{32,16},{48,32},{1,49},{17,1},{33,17},{49,33},{2,50}... | collective-permute-start | bytes 12296 | tf_op jit(solution)/shard_map/ppermute | solution.py:78
  160.2 0.5 collective-permute-start.11
  160.7 0.6 collective-permute-start.10
  161.3 2.9 %collective-permute-done.11 = f32[1024]{0:T(1024)S(1)} collective-permute-done((f32[1024]{0:T(1024)S(1)}, f32[1024]{0:T(1024)S(1)}, u32[]{:S(2)}, u32[]{:S(2)}) %collective-permute-start.11) | collective-permute-done | bytes 4128 | tf_op jit(solution)/shard_map/ppermute | solution.py:78
  164.1 0.2 collective-permute-done.10
  164.4 2.5 %collective-permute-start.15 = (f32[1024]{0:T(1024)S(1)}, f32[1024]{0:T(1024)S(1)}, u32[]{:S(2)}, u32[]{:S(2)}) collective-permute-start(f32[1024]{0:T(1024)S(1)} %add_add_fusion), channel_id=1, source_target_pairs={{0,192},{64,0},{128,64},{192,128},{1,193},{65,1},{129,65},{193,129... | collective-permute-start | bytes 12296 | tf_op jit(solution)/shard_map/ppermute | solution.py:78
  166.9 0.4 collective-permute-start.14
  167.3 0.6 collective-permute-start.13
  167.9 3.0 %collective-permute-done.14 = f32[1024]{0:T(1024)S(1)} collective-permute-done((f32[1024]{0:T(1024)S(1)}, f32[1024]{0:T(1024)S(1)}, u32[]{:S(2)}, u32[]{:S(2)}) %collective-permute-start.14) | collective-permute-done | bytes 4128 | tf_op jit(solution)/shard_map/ppermute | solution.py:78
  171.0 0.5 collective-permute-done.13
  171.5 49.3 %all-gather.5.cloned.1.call-done = bf16[1024,6144]{0,1:T(8,128)(2,1)} async-done(((bf16[1024,192]{0,1:T(8,128)(2,1)}), bf16[1024,6144]{0,1:T(8,128)(2,1)}) %all-gather.5.cloned.1.call-update) | async-done | bytes 12582928 | tf_op jit(solution)/shard_map/all_gather | solution.py:205
  220.8 12.5 %fusion = f32[576,1024]{1,0:T(8,128)S(1)} fusion(bf16[1024,6144]{0,1:T(8,128)(2,1)} %all-gather.5.cloned.1.call-done, bf16[288,6144]{1,0:T(8,128)(2,1)} %bitcast.103, bf16[288,6144]{1,0:T(8,128)(2,1)} %bitcast.104), kind=kOutput, calls=%fused_computation | convolution fusion | flops 7261913088 | bytes 22020096 | tf_op jit(solution)/shard_map/dot_general | solution.py:209
  233.3 1.2 fusion.11
  (77 shorter events, 2.8 us)
Async XLA Ops:
  7.2 85.8 %copy-start = (bf16[1024,192]{0,1:T(8,128)(2,1)S(1)}, bf16[1024,192]{0,1:T(8,128)(2,1)}, u32[]{:S(2)}) copy-start(bf16[1024,192]{0,1:T(8,128)(2,1)} %param.13) | copy-start | bytes 1179652
  7.2 10.8 %copy-start.3 = (bf16[64,1024]{1,0:T(8,128)(2,1)S(1)}, bf16[64,1024]{1,0:T(8,128)(2,1)}, u32[]{:S(2)}) copy-start(bf16[64,1024]{1,0:T(8,128)(2,1)} %param.10) | copy-start | bytes 393220
  7.2 10.8 %copy-start.2 = (bf16[64,1024]{1,0:T(8,128)(2,1)S(1)}, bf16[64,1024]{1,0:T(8,128)(2,1)}, u32[]{:S(2)}) copy-start(bf16[64,1024]{1,0:T(8,128)(2,1)} %param.9) | copy-start | bytes 393220
  7.2 85.8 %all-gather.3.cloned.1.call-start = ((), (), s32[]{:S(2)}) async-start(), calls=%async_computation.2 | async-start | bytes 4325376 | tf_op jit(solution)/shard_map/all_gather | solution.py:170
  8.2 5.4 %collective-permute-start = (f32[8]{0:T(128)S(1)}, f32[8]{0:T(128)S(1)}, u32[]{:S(2)}, u32[]{:S(2)}) collective-permute-start(f32[8]{0:T(128)S(1)} %fusion.60), channel_id=1, source_target_pairs={{0,8},{8,0},{1,9},{9,1},{2,10},{10,2},{3,11},{11,3},{4,12},{12,4},... | collective-permute-start | bytes 104 | tf_op jit(solution)/shard_map/ppermute | solution.py:71
  13.3 2.0 collective-permute-start.1
  15.7 6.9 %collective-permute-start.4 = (bf16[4,136,128]{2,1,0:T(8,128)(2,1)S(1)}, bf16[4,136,128]{2,1,0:T(8,128)(2,1)S(1)}, u32[]{:S(2)}, u32[]{:S(2)}) collective-permute-start(bf16[4,136,128]{2,1,0:T(8,128)(2,1)S(1)} %maximum_maximum_fusion), channel_id=1, source_target_pairs={{0,16},{16,32},{32,48},{48,0},{1,17},{17,33},{33,49},{49,1},{2,18}... | collective-permute-start | bytes 417800 | tf_op jit(solution)/shard_map/ppermute | solution.py:44
  15.8 8.9 %collective-permute-start.3 = (bf16[4,136,128]{2,1,0:T(8,128)(2,1)S(1)}, bf16[4,136,128]{2,1,0:T(8,128)(2,1)S(1)}, u32[]{:S(2)}, u32[]{:S(2)}) collective-permute-start(bf16[4,136,128]{2,1,0:T(8,128)(2,1)S(1)} %maximum_maximum_fusion), channel_id=1, source_target_pairs={{0,32},{16,48},{32,0},{48,16},{1,33},{17,49},{33,1},{49,17},{2,34}... | collective-permute-start | bytes 417800 | tf_op jit(solution)/shard_map/ppermute | solution.py:44
  18.1 7.2 %collective-permute-start.2 = (bf16[4,136,128]{2,1,0:T(8,128)(2,1)S(1)}, bf16[4,136,128]{2,1,0:T(8,128)(2,1)S(1)}, u32[]{:S(2)}, u32[]{:S(2)}) collective-permute-start(bf16[4,136,128]{2,1,0:T(8,128)(2,1)S(1)} %maximum_maximum_fusion), channel_id=1, source_target_pairs={{0,48},{16,0},{32,16},{48,32},{1,49},{17,1},{33,17},{49,33},{2,50}... | collective-permute-start | bytes 417800 | tf_op jit(solution)/shard_map/ppermute | solution.py:44
  22.6 17.8 %copy-start.1 = (bf16[64,1024]{1,0:T(8,128)(2,1)S(1)}, bf16[64,1024]{1,0:T(8,128)(2,1)}, u32[]{:S(2)}) copy-start(bf16[64,1024]{1,0:T(8,128)(2,1)} %param.11) | copy-start | bytes 393220
  26.2 9.4 %collective-permute-start.7 = (bf16[4,136,128]{2,1,0:T(8,128)(2,1)S(1)}, bf16[4,136,128]{2,1,0:T(8,128)(2,1)S(1)}, u32[]{:S(2)}, u32[]{:S(2)}) collective-permute-start(bf16[4,136,128]{2,1,0:T(8,128)(2,1)S(1)} %maximum_maximum_fusion.1), channel_id=1, source_target_pairs={{0,192},{64,0},{128,64},{192,128},{1,193},{65,1},{129,65},{193,129... | collective-permute-start | bytes 417800 | tf_op jit(solution)/shard_map/ppermute | solution.py:44
  28.0 7.3 %collective-permute-start.6 = (bf16[4,136,128]{2,1,0:T(8,128)(2,1)S(1)}, bf16[4,136,128]{2,1,0:T(8,128)(2,1)S(1)}, u32[]{:S(2)}, u32[]{:S(2)}) collective-permute-start(bf16[4,136,128]{2,1,0:T(8,128)(2,1)S(1)} %maximum_maximum_fusion.1), channel_id=1, source_target_pairs={{0,64},{64,128},{128,192},{192,0},{1,65},{65,129},{129,193},{193,1... | collective-permute-start | bytes 417800 | tf_op jit(solution)/shard_map/ppermute | solution.py:44
  28.0 7.4 %collective-permute-start.5 = (bf16[4,136,128]{2,1,0:T(8,128)(2,1)S(1)}, bf16[4,136,128]{2,1,0:T(8,128)(2,1)S(1)}, u32[]{:S(2)}, u32[]{:S(2)}) collective-permute-start(bf16[4,136,128]{2,1,0:T(8,128)(2,1)S(1)} %maximum_maximum_fusion.1), channel_id=1, source_target_pairs={{0,128},{64,192},{128,0},{192,64},{1,129},{65,193},{129,1},{193,65... | collective-permute-start | bytes 417800 | tf_op jit(solution)/shard_map/ppermute | solution.py:44
  35.8 4.2 %collective-permute-start.8 = (f32[4,128,128]{2,1,0:T(8,128)S(1)}, f32[4,128,128]{2,1,0:T(8,128)S(1)}, u32[]{:S(2)}, u32[]{:S(2)}) collective-permute-start(f32[4,128,128]{2,1,0:T(8,128)S(1)} %fusion.15), channel_id=1, source_target_pairs={{0,8},{8,0},{1,9},{9,1},{2,10},{10,2},{3,11},{11,3},{4,12},{12,4},... | collective-permute-start | bytes 786440 | tf_op jit(solution)/shard_map/ppermute | solution.py:71
  41.7 56.3 %copy-start.6 = (s32[256,2]{0,1:T(2,128)S(1)}, s32[256,2]{0,1:T(2,128)}, u32[]{:S(2)}) copy-start(s32[256,2]{0,1:T(2,128)} %param.15) | copy-start | bytes 6148
  41.7 92.0 %copy-start.4 = (bf16[256,192]{0,1:T(8,128)(2,1)S(1)}, bf16[256,192]{0,1:T(8,128)(2,1)}, u32[]{:S(2)}) copy-start(bf16[256,192]{0,1:T(8,128)(2,1)} %param.14) | copy-start | bytes 294916
  41.7 92.0 %reduce-scatter.2.cloned.1.call-start = ((), (), s32[]{:S(2)}) async-start(), calls=%async_computation.3 | async-start | bytes 1769472 | tf_op jit(solution)/shard_map/reduce_scatter | solution.py:172
  97.9 122.8 %all-gather.5.cloned.1.call-start = ((), (), s32[]{:S(2)}) async-start(), calls=%async_computation.4 | async-start | bytes 12976128 | tf_op jit(solution)/shard_map/all_gather | solution.py:205
  134.6 98.7 %copy-start.5 = (bf16[256,192]{0,1:T(8,128)(2,1)}, bf16[256,192]{0,1:T(8,128)(2,1)S(1)}, u32[]{:S(2)}) copy-start(bf16[256,192]{0,1:T(8,128)(2,1)S(1)} %fusion.28) | copy-start | bytes 294916
  151.5 6.1 %collective-permute-start.9 = (f32[1024]{0:T(1024)S(1)}, f32[1024]{0:T(1024)S(1)}, u32[]{:S(2)}, u32[]{:S(2)}) collective-permute-start(f32[1024]{0:T(1024)S(1)} %fusion.10), channel_id=1, source_target_pairs={{0,8},{8,0},{1,9},{9,1},{2,10},{10,2},{3,11},{11,3},{4,12},{12,4},... | collective-permute-start | bytes 12296 | tf_op jit(solution)/shard_map/ppermute | solution.py:78
  157.7 3.6 %collective-permute-start.12 = (f32[1024]{0:T(1024)S(1)}, f32[1024]{0:T(1024)S(1)}, u32[]{:S(2)}, u32[]{:S(2)}) collective-permute-start(f32[1024]{0:T(1024)S(1)} %add.169), channel_id=1, source_target_pairs={{0,48},{16,0},{32,16},{48,32},{1,49},{17,1},{33,17},{49,33},{2,50}... | collective-permute-start | bytes 12296 | tf_op jit(solution)/shard_map/ppermute | solution.py:78
  160.2 4.0 %collective-permute-start.11 = (f32[1024]{0:T(1024)S(1)}, f32[1024]{0:T(1024)S(1)}, u32[]{:S(2)}, u32[]{:S(2)}) collective-permute-start(f32[1024]{0:T(1024)S(1)} %add.169), channel_id=1, source_target_pairs={{0,32},{16,48},{32,0},{48,16},{1,33},{17,49},{33,1},{49,17},{2,34}... | collective-permute-start | bytes 12296 | tf_op jit(solution)/shard_map/ppermute | solution.py:78
  160.7 3.7 %collective-permute-start.10 = (f32[1024]{0:T(1024)S(1)}, f32[1024]{0:T(1024)S(1)}, u32[]{:S(2)}, u32[]{:S(2)}) collective-permute-start(f32[1024]{0:T(1024)S(1)} %add.169), channel_id=1, source_target_pairs={{0,16},{16,32},{32,48},{48,0},{1,17},{17,33},{33,49},{49,1},{2,18}... | collective-permute-start | bytes 12296 | tf_op jit(solution)/shard_map/ppermute | solution.py:78
  164.4 3.6 %collective-permute-start.15 = (f32[1024]{0:T(1024)S(1)}, f32[1024]{0:T(1024)S(1)}, u32[]{:S(2)}, u32[]{:S(2)}) collective-permute-start(f32[1024]{0:T(1024)S(1)} %add_add_fusion), channel_id=1, source_target_pairs={{0,192},{64,0},{128,64},{192,128},{1,193},{65,1},{129,65},{193,129... | collective-permute-start | bytes 12296 | tf_op jit(solution)/shard_map/ppermute | solution.py:78
  166.9 4.1 %collective-permute-start.14 = (f32[1024]{0:T(1024)S(1)}, f32[1024]{0:T(1024)S(1)}, u32[]{:S(2)}, u32[]{:S(2)}) collective-permute-start(f32[1024]{0:T(1024)S(1)} %add_add_fusion), channel_id=1, source_target_pairs={{0,128},{64,192},{128,0},{192,64},{1,129},{65,193},{129,1},{193,65... | collective-permute-start | bytes 12296 | tf_op jit(solution)/shard_map/ppermute | solution.py:78
  167.3 4.1 %collective-permute-start.13 = (f32[1024]{0:T(1024)S(1)}, f32[1024]{0:T(1024)S(1)}, u32[]{:S(2)}, u32[]{:S(2)}) collective-permute-start(f32[1024]{0:T(1024)S(1)} %add_add_fusion), channel_id=1, source_target_pairs={{0,64},{64,128},{128,192},{192,0},{1,65},{65,129},{129,193},{193,1... | collective-permute-start | bytes 12296 | tf_op jit(solution)/shard_map/ppermute | solution.py:78
Sparse Core Ops, SparseCore 0:
  41.8 51.1 all-gather.2
  98.0 35.5 reduce-scatter.1
  151.5 69.1 all-gather.4

commit v12 on v8

--- a/solution.py
+++ b/solution.py
@@ -155,11 +155,13 @@
     gathered = lax.all_gather(normed, SEQ, axis=0, tiled=True)
     row_block = gathered
     attended = lax.psum_scatter(
-        lax.dot_general(out_weight, row_block, (((0,), (1,)), ((), ())), preferred_element_type=jnp.float32),
+        lax.dot_general(
+            out_weight, row_block, (((0,), (1,)), ((), ())), preferred_element_type=jnp.float32
+        ).astype(jnp.bfloat16),
         "exp",
         scatter_dimension=1,
         tiled=True,
-    ).T
+    ).T.astype(jnp.float32)
     residual_out = (residual.astype(jnp.float32) + attended).astype(jnp.bfloat16)
     group_rows = routes.shape[0]
     choices_each = routes.shape[1]

time: 241 us -> 238 us (0.988)
  waiting for transfers between devices: 156 us -> 152 us
    reduce_scatter x1, waiting for transfers between devices: 33.4 us -> 30 us  [body(): lax.psum_scatter(lax.dot_general(out_weight, row_block, (((0,), (1,)), ((...]
where the time goes in v12:
time: 238 us
  waiting for transfers between devices  152 us (64%)
  starting transfers between devices  27 us (11%)
  matrix products  20.4 us (9%)
  blocking collectives  15.1 us (6%)
  between operations  14 us (6%)
  other arithmetic  5.91 us (2%)
  local copies, waits for them, and re-layouts  3.24 us (1%)
    all_gather x1, waiting for transfers between devices, body(): gathered = lax.all_gather(normed, SEQ, axis=0, tiled=True)  52.7 us
    all_gather x1, waiting for transfers between devices, body(): row_block = lax.all_gather(slices, SEQ, axis=1, tiled=True)  49 us
    reduce_scatter x1, waiting for transfers between devices, body(): lax.psum_scatter(lax.dot_general(out_weight, row_block, (((0,), (1,)), ((...  30 us
    all_to_all x1, blocking collectives, body(): lax.all_to_all(buffer.reshape(experts, capacity, columns), 'exp', split_a...  15.1 us
    ppermute x7, starting transfers between devices, ring_sum(): lax.ppermute(part, axis, [(i, (i + d) % peers) for i in range(peers)])  13.9 us
    dot_general x1, matrix products, body(): lax.dot_general(jnp.concatenate([w_gate, w_up], 0), row_block, contract_l...  12.5 us
    ppermute x6, waiting for transfers between devices, ring_shifts(): lax.ppermute(part, axis, [(i, (i + d) % peers) for i in range(peers)])  10.8 us
    ppermute x6, starting transfers between devices, ring_shifts(): lax.ppermute(part, axis, [(i, (i + d) % peers) for i in range(peers)])  7.48 us
  transfers between devices with their start and end apart: 19, of which 15 were waited for; matrix products, arithmetic and copies ran while one was open for 2% of the time, Pallas kernels for 0%

profile of v12, /device:TPU:1, one launch (start us, length us, event | category | flops | bytes accessed | tf_op | source)
XLA Modules:
  0.0 237.9 jit_solution(18204027842935783083)
XLA Ops:
  7.2 0.8 copy.85
  8.1 3.3 %collective-permute-start = (f32[8]{0:T(128)S(1)}, f32[8]{0:T(128)S(1)}, u32[]{:S(2)}, u32[]{:S(2)}) collective-permute-start(f32[8]{0:T(128)S(1)} %fusion.56), channel_id=1, source_target_pairs={{0,8},{8,0},{1,9},{9,1},{2,10},{10,2},{3,11},{11,3},{4,12},{12,4},... | collective-permute-start | bytes 104 | tf_op jit(solution)/shard_map/ppermute | solution.py:71
  11.5 1.7 fusion.24
  13.6 1.6 collective-permute-done.1
  15.8 2.2 collective-permute-start.3
  17.9 1.1 collective-permute-start.2
  19.0 3.6 %collective-permute-done.4 = bf16[4,136,128]{2,1,0:T(8,128)(2,1)S(1)} collective-permute-done((bf16[4,136,128]{2,1,0:T(8,128)(2,1)S(1)}, bf16[4,136,128]{2,1,0:T(8,128)(2,1)S(1)}, u32[]{:S(2)}, u32[]{:S(2)}) %collective-permute-start.4) | collective-permute-done | bytes 139296 | tf_op jit(solution)/shard_map/ppermute | solution.py:44
  22.6 2.0 collective-permute-done.3
  24.7 0.7 collective-permute-done.2
  25.4 0.1 fusion.46
  25.6 0.3 add_convert_fusion
  26.2 0.6 collective-permute-start.6
  26.7 2.5 %collective-permute-start.5 = (bf16[4,136,128]{2,1,0:T(8,128)(2,1)S(1)}, bf16[4,136,128]{2,1,0:T(8,128)(2,1)S(1)}, u32[]{:S(2)}, u32[]{:S(2)}) collective-permute-start(bf16[4,136,128]{2,1,0:T(8,128)(2,1)S(1)} %maximum_maximum_fusion.1), channel_id=1, source_target_pairs={{0,128},{64,192},{128,0},{192,64},{1,129},{65,193},{129,1},{193,65... | collective-permute-start | bytes 417800 | tf_op jit(solution)/shard_map/ppermute | solution.py:44
  29.2 1.2 collective-permute-start.7
  30.4 1.0 collective-permute-done.6
  31.4 3.5 %collective-permute-done.5 = bf16[4,136,128]{2,1,0:T(8,128)(2,1)S(1)} collective-permute-done((bf16[4,136,128]{2,1,0:T(8,128)(2,1)S(1)}, bf16[4,136,128]{2,1,0:T(8,128)(2,1)S(1)}, u32[]{:S(2)}, u32[]{:S(2)}) %collective-permute-start.5) | collective-permute-done | bytes 139296 | tf_op jit(solution)/shard_map/ppermute | solution.py:44
  35.1 0.3 fusion.19
  35.4 2.1 collective-permute-start.8
  37.5 0.2 convolution_multiply_fusion
  37.8 0.3 convolution_bitcast_fusion
  38.0 0.6 collective-permute-done.8
  38.6 0.8 multiply_reduce_fusion
  39.5 0.8 copy_bitcast_fusion.2
  40.4 52.7 %all-gather.3.cloned.1.call-done = bf16[2048,1024]{1,0:T(8,128)(2,1)} async-done(((bf16[64,1024]{1,0:T(8,128)(2,1)}), bf16[2048,1024]{1,0:T(8,128)(2,1)}) %all-gather.3.cloned.1.call-update) | async-done | bytes 4194320 | tf_op jit(solution)/shard_map/all_gather | solution.py:155
  93.0 4.6 %fusion.4 = bf16[192,2048]{1,0:T(8,128)(2,1)} fusion(bf16[2048,1024]{1,0:T(8,128)(2,1)} %all-gather.3.cloned.1.call-done, bf16[1024,192]{0,1:T(8,128)(2,1)S(1)} %copy-done), kind=kOutput, calls=%fused_computation.5 | convolution fusion | flops 805699584 | bytes 5373952 | tf_op jit(solution)/shard_map/dot_general | solution.py:158
  98.2 1.1 reduce-window.6
  99.3 0.2 slice_reduce_fusion
  99.7 0.1 sub.61
  99.9 30.0 %reduce-scatter.2.cloned.1.call-done = bf16[192,256]{1,0:T(8,128)(2,1)} async-done(((bf16[192,2048]{1,0:T(8,128)(2,1)}), bf16[192,256]{1,0:T(8,128)(2,1)}) %reduce-scatter.2.cloned.1.call-update) | async-done | bytes 98320 | tf_op jit(solution)/shard_map/reduce_scatter | solution.py:157
  129.9 0.9 fusion.28
  130.8 0.4 fusion.5
  131.3 15.1 %all_to_all.5 = bf16[8,128,192]{1,2,0:T(8,128)(2,1)S(1)} all-to-all(bf16[8,128,192]{1,2,0:T(8,128)(2,1)S(1)} %bitcast.101), channel_id=1, replica_groups=mesh['seq_0'=4,'seq_1'=4,'seq_2'=2,'exp'=8] {'exp'}, dimensions={0} | all-to-all | bytes 786432 | tf_op jit(solution)/shard_map/all_to_all | solution.py:187
  146.4 0.8 copy_bitcast_fusion
  147.4 6.8 %collective-permute-start.9 = (f32[1024]{0:T(1024)S(1)}, f32[1024]{0:T(1024)S(1)}, u32[]{:S(2)}, u32[]{:S(2)}) collective-permute-start(f32[1024]{0:T(1024)S(1)} %fusion.11), channel_id=1, source_target_pairs={{0,8},{8,0},{1,9},{9,1},{2,10},{10,2},{3,11},{11,3},{4,12},{12,4},... | collective-permute-start | bytes 12296 | tf_op jit(solution)/shard_map/ppermute | solution.py:78
  154.1 0.8 collective-permute-done.9
  155.0 2.4 collective-permute-start.12
  157.3 0.6 collective-permute-start.11
  157.9 0.6 collective-permute-start.10
  158.5 2.7 %collective-permute-done.11 = f32[1024]{0:T(1024)S(1)} collective-permute-done((f32[1024]{0:T(1024)S(1)}, f32[1024]{0:T(1024)S(1)}, u32[]{:S(2)}, u32[]{:S(2)}) %collective-permute-start.11) | collective-permute-done | bytes 4128 | tf_op jit(solution)/shard_map/ppermute | solution.py:78
  161.3 0.3 collective-permute-done.10
  161.6 2.4 %collective-permute-start.15 = (f32[1024]{0:T(1024)S(1)}, f32[1024]{0:T(1024)S(1)}, u32[]{:S(2)}, u32[]{:S(2)}) collective-permute-start(f32[1024]{0:T(1024)S(1)} %add_add_fusion), channel_id=1, source_target_pairs={{0,192},{64,0},{128,64},{192,128},{1,193},{65,1},{129,65},{193,129... | collective-permute-start | bytes 12296 | tf_op jit(solution)/shard_map/ppermute | solution.py:78
  164.0 0.6 collective-permute-start.14
  164.6 0.6 collective-permute-start.13
  165.1 3.0 %collective-permute-done.14 = f32[1024]{0:T(1024)S(1)} collective-permute-done((f32[1024]{0:T(1024)S(1)}, f32[1024]{0:T(1024)S(1)}, u32[]{:S(2)}, u32[]{:S(2)}) %collective-permute-start.14) | collective-permute-done | bytes 4128 | tf_op jit(solution)/shard_map/ppermute | solution.py:78
  168.1 0.5 collective-permute-done.13
  168.7 49.0 %all-gather.5.cloned.1.call-done = bf16[1024,6144]{0,1:T(8,128)(2,1)} async-done(((bf16[1024,192]{0,1:T(8,128)(2,1)}), bf16[1024,6144]{0,1:T(8,128)(2,1)}) %all-gather.5.cloned.1.call-update) | async-done | bytes 12582928 | tf_op jit(solution)/shard_map/all_gather | solution.py:192
  217.7 12.5 %fusion = f32[576,1024]{1,0:T(8,128)S(1)} fusion(bf16[1024,6144]{0,1:T(8,128)(2,1)} %all-gather.5.cloned.1.call-done, bf16[288,6144]{1,0:T(8,128)(2,1)} %bitcast.105, bf16[288,6144]{1,0:T(8,128)(2,1)} %bitcast.106), kind=kOutput, calls=%fused_computation | convolution fusion | flops 7261913088 | bytes 22020096 | tf_op jit(solution)/shard_map/dot_general | solution.py:196
  230.2 1.2 fusion.12
  (74 shorter events, 2.8 us)
Async XLA Ops:
  7.2 85.9 %copy-start = (bf16[1024,192]{0,1:T(8,128)(2,1)S(1)}, bf16[1024,192]{0,1:T(8,128)(2,1)}, u32[]{:S(2)}) copy-start(bf16[1024,192]{0,1:T(8,128)(2,1)} %param.13) | copy-start | bytes 1179652
  7.2 85.9 %all-gather.3.cloned.1.call-start = ((), (), s32[]{:S(2)}) async-start(), calls=%async_computation.2 | async-start | bytes 4325376 | tf_op jit(solution)/shard_map/all_gather | solution.py:155
  8.1 5.3 %collective-permute-start = (f32[8]{0:T(128)S(1)}, f32[8]{0:T(128)S(1)}, u32[]{:S(2)}, u32[]{:S(2)}) collective-permute-start(f32[8]{0:T(128)S(1)} %fusion.56), channel_id=1, source_target_pairs={{0,8},{8,0},{1,9},{9,1},{2,10},{10,2},{3,11},{11,3},{4,12},{12,4},... | collective-permute-start | bytes 104 | tf_op jit(solution)/shard_map/ppermute | solution.py:71
  13.2 2.0 collective-permute-start.1
  15.3 22.2 %copy-start.2 = (bf16[64,1024]{1,0:T(8,128)(2,1)S(1)}, bf16[64,1024]{1,0:T(8,128)(2,1)}, u32[]{:S(2)}) copy-start(bf16[64,1024]{1,0:T(8,128)(2,1)} %param.10) | copy-start | bytes 393220
  15.3 22.2 %copy-start.6 = (bf16[64,1024]{1,0:T(8,128)(2,1)S(1)}, bf16[64,1024]{1,0:T(8,128)(2,1)}, u32[]{:S(2)}) copy-start(bf16[64,1024]{1,0:T(8,128)(2,1)} %param.9) | copy-start | bytes 393220
  15.4 22.3 %copy-start.1 = (bf16[64,1024]{1,0:T(8,128)(2,1)S(1)}, bf16[64,1024]{1,0:T(8,128)(2,1)}, u32[]{:S(2)}) copy-start(bf16[64,1024]{1,0:T(8,128)(2,1)} %param.11) | copy-start | bytes 393220
  15.7 6.9 %collective-permute-start.4 = (bf16[4,136,128]{2,1,0:T(8,128)(2,1)S(1)}, bf16[4,136,128]{2,1,0:T(8,128)(2,1)S(1)}, u32[]{:S(2)}, u32[]{:S(2)}) collective-permute-start(bf16[4,136,128]{2,1,0:T(8,128)(2,1)S(1)} %maximum_maximum_fusion), channel_id=1, source_target_pairs={{0,16},{16,32},{32,48},{48,0},{1,17},{17,33},{33,49},{49,1},{2,18}... | collective-permute-start | bytes 417800 | tf_op jit(solution)/shard_map/ppermute | solution.py:44
  15.8 8.9 %collective-permute-start.3 = (bf16[4,136,128]{2,1,0:T(8,128)(2,1)S(1)}, bf16[4,136,128]{2,1,0:T(8,128)(2,1)S(1)}, u32[]{:S(2)}, u32[]{:S(2)}) collective-permute-start(bf16[4,136,128]{2,1,0:T(8,128)(2,1)S(1)} %maximum_maximum_fusion), channel_id=1, source_target_pairs={{0,32},{16,48},{32,0},{48,16},{1,33},{17,49},{33,1},{49,17},{2,34}... | collective-permute-start | bytes 417800 | tf_op jit(solution)/shard_map/ppermute | solution.py:44
  17.9 7.4 %collective-permute-start.2 = (bf16[4,136,128]{2,1,0:T(8,128)(2,1)S(1)}, bf16[4,136,128]{2,1,0:T(8,128)(2,1)S(1)}, u32[]{:S(2)}, u32[]{:S(2)}) collective-permute-start(bf16[4,136,128]{2,1,0:T(8,128)(2,1)S(1)} %maximum_maximum_fusion), channel_id=1, source_target_pairs={{0,48},{16,0},{32,16},{48,32},{1,49},{17,1},{33,17},{49,33},{2,50}... | collective-permute-start | bytes 417800 | tf_op jit(solution)/shard_map/ppermute | solution.py:44
  26.2 5.2 %collective-permute-start.6 = (bf16[4,136,128]{2,1,0:T(8,128)(2,1)S(1)}, bf16[4,136,128]{2,1,0:T(8,128)(2,1)S(1)}, u32[]{:S(2)}, u32[]{:S(2)}) collective-permute-start(bf16[4,136,128]{2,1,0:T(8,128)(2,1)S(1)} %maximum_maximum_fusion.1), channel_id=1, source_target_pairs={{0,64},{64,128},{128,192},{192,0},{1,65},{65,129},{129,193},{193,1... | collective-permute-start | bytes 417800 | tf_op jit(solution)/shard_map/ppermute | solution.py:44
  26.7 8.2 %collective-permute-start.5 = (bf16[4,136,128]{2,1,0:T(8,128)(2,1)S(1)}, bf16[4,136,128]{2,1,0:T(8,128)(2,1)S(1)}, u32[]{:S(2)}, u32[]{:S(2)}) collective-permute-start(bf16[4,136,128]{2,1,0:T(8,128)(2,1)S(1)} %maximum_maximum_fusion.1), channel_id=1, source_target_pairs={{0,128},{64,192},{128,0},{192,64},{1,129},{65,193},{129,1},{193,65... | collective-permute-start | bytes 417800 | tf_op jit(solution)/shard_map/ppermute | solution.py:44
  29.2 5.9 %collective-permute-start.7 = (bf16[4,136,128]{2,1,0:T(8,128)(2,1)S(1)}, bf16[4,136,128]{2,1,0:T(8,128)(2,1)S(1)}, u32[]{:S(2)}, u32[]{:S(2)}) collective-permute-start(bf16[4,136,128]{2,1,0:T(8,128)(2,1)S(1)} %maximum_maximum_fusion.1), channel_id=1, source_target_pairs={{0,192},{64,0},{128,64},{192,128},{1,193},{65,1},{129,65},{193,129... | collective-permute-start | bytes 417800 | tf_op jit(solution)/shard_map/ppermute | solution.py:44
  35.4 3.3 %collective-permute-start.8 = (f32[4,128,128]{2,1,0:T(8,128)S(1)}, f32[4,128,128]{2,1,0:T(8,128)S(1)}, u32[]{:S(2)}, u32[]{:S(2)}) collective-permute-start(f32[4,128,128]{2,1,0:T(8,128)S(1)} %fusion.19), channel_id=1, source_target_pairs={{0,8},{8,0},{1,9},{9,1},{2,10},{10,2},{3,11},{11,3},{4,12},{12,4},... | collective-permute-start | bytes 786440 | tf_op jit(solution)/shard_map/ppermute | solution.py:71
  40.3 57.4 %copy-start.5 = (s32[256,2]{0,1:T(2,128)S(1)}, s32[256,2]{0,1:T(2,128)}, u32[]{:S(2)}) copy-start(s32[256,2]{0,1:T(2,128)} %param.15) | copy-start | bytes 6148
  40.3 89.6 %copy-start.3 = (bf16[256,192]{0,1:T(8,128)(2,1)S(1)}, bf16[256,192]{0,1:T(8,128)(2,1)}, u32[]{:S(2)}) copy-start(bf16[256,192]{0,1:T(8,128)(2,1)} %param.14) | copy-start | bytes 294916
  40.3 89.6 %reduce-scatter.2.cloned.1.call-start = ((), (), s32[]{:S(2)}) async-start(), calls=%async_computation.3 | async-start | bytes 884736 | tf_op jit(solution)/shard_map/reduce_scatter | solution.py:157
  97.7 120.0 %all-gather.5.cloned.1.call-start = ((), (), s32[]{:S(2)}) async-start(), calls=%async_computation.4 | async-start | bytes 12976128 | tf_op jit(solution)/shard_map/all_gather | solution.py:192
  130.8 99.4 %copy-start.4 = (bf16[256,192]{0,1:T(8,128)(2,1)}, bf16[256,192]{0,1:T(8,128)(2,1)S(1)}, u32[]{:S(2)}) copy-start(bf16[256,192]{0,1:T(8,128)(2,1)S(1)} %fusion.28) | copy-start | bytes 294916
  147.4 7.6 %collective-permute-start.9 = (f32[1024]{0:T(1024)S(1)}, f32[1024]{0:T(1024)S(1)}, u32[]{:S(2)}, u32[]{:S(2)}) collective-permute-start(f32[1024]{0:T(1024)S(1)} %fusion.11), channel_id=1, source_target_pairs={{0,8},{8,0},{1,9},{9,1},{2,10},{10,2},{3,11},{11,3},{4,12},{12,4},... | collective-permute-start | bytes 12296 | tf_op jit(solution)/shard_map/ppermute | solution.py:78
  155.0 3.6 %collective-permute-start.12 = (f32[1024]{0:T(1024)S(1)}, f32[1024]{0:T(1024)S(1)}, u32[]{:S(2)}, u32[]{:S(2)}) collective-permute-start(f32[1024]{0:T(1024)S(1)} %add.156), channel_id=1, source_target_pairs={{0,48},{16,0},{32,16},{48,32},{1,49},{17,1},{33,17},{49,33},{2,50}... | collective-permute-start | bytes 12296 | tf_op jit(solution)/shard_map/ppermute | solution.py:78
  157.3 4.0 %collective-permute-start.11 = (f32[1024]{0:T(1024)S(1)}, f32[1024]{0:T(1024)S(1)}, u32[]{:S(2)}, u32[]{:S(2)}) collective-permute-start(f32[1024]{0:T(1024)S(1)} %add.156), channel_id=1, source_target_pairs={{0,32},{16,48},{32,0},{48,16},{1,33},{17,49},{33,1},{49,17},{2,34}... | collective-permute-start | bytes 12296 | tf_op jit(solution)/shard_map/ppermute | solution.py:78
  157.9 3.7 %collective-permute-start.10 = (f32[1024]{0:T(1024)S(1)}, f32[1024]{0:T(1024)S(1)}, u32[]{:S(2)}, u32[]{:S(2)}) collective-permute-start(f32[1024]{0:T(1024)S(1)} %add.156), channel_id=1, source_target_pairs={{0,16},{16,32},{32,48},{48,0},{1,17},{17,33},{33,49},{49,1},{2,18}... | collective-permute-start | bytes 12296 | tf_op jit(solution)/shard_map/ppermute | solution.py:78
  161.6 3.5 %collective-permute-start.15 = (f32[1024]{0:T(1024)S(1)}, f32[1024]{0:T(1024)S(1)}, u32[]{:S(2)}, u32[]{:S(2)}) collective-permute-start(f32[1024]{0:T(1024)S(1)} %add_add_fusion), channel_id=1, source_target_pairs={{0,192},{64,0},{128,64},{192,128},{1,193},{65,1},{129,65},{193,129... | collective-permute-start | bytes 12296 | tf_op jit(solution)/shard_map/ppermute | solution.py:78
  164.0 4.1 %collective-permute-start.14 = (f32[1024]{0:T(1024)S(1)}, f32[1024]{0:T(1024)S(1)}, u32[]{:S(2)}, u32[]{:S(2)}) collective-permute-start(f32[1024]{0:T(1024)S(1)} %add_add_fusion), channel_id=1, source_target_pairs={{0,128},{64,192},{128,0},{192,64},{1,129},{65,193},{129,1},{193,65... | collective-permute-start | bytes 12296 | tf_op jit(solution)/shard_map/ppermute | solution.py:78
  164.6 4.1 %collective-permute-start.13 = (f32[1024]{0:T(1024)S(1)}, f32[1024]{0:T(1024)S(1)}, u32[]{:S(2)}, u32[]{:S(2)}) collective-permute-start(f32[1024]{0:T(1024)S(1)} %add_add_fusion), channel_id=1, source_target_pairs={{0,64},{64,128},{128,192},{192,0},{1,65},{65,129},{129,193},{193,1... | collective-permute-start | bytes 12296 | tf_op jit(solution)/shard_map/ppermute | solution.py:78
Sparse Core Ops, SparseCore 0:
  40.4 52.5 all-gather.2
  97.8 32.0 reduce-scatter.1
  147.4 70.2 all-gather.4

commit v13 on v8

--- a/solution.py
+++ b/solution.py
@@ -106,7 +106,7 @@
     along_y, row = prefix_over(packed_shifts(*mine, "seq_1"), lax.axis_index("seq_1"))
     along_x, _ = prefix_over(packed_shifts(*row, "seq_0"), lax.axis_index("seq_0"))
     chip_before = link_states(along_x, along_y)[1]
-    theirs = swap_cores(chip_before)
+    theirs = swap_cores(chip_before.astype(jnp.bfloat16)).astype(jnp.float32)
     whole = jnp.where(
         core == 0, jnp.concatenate([chip_before, theirs], 0), jnp.concatenate([theirs, chip_before], 0)
     )

time: 241 us -> 241 us (level)
  transfers between devices with their start and end apart: 19 -> 19, of which waited for: 15 -> 14; matrix products, arithmetic and copies ran while one was open for 2% -> 2% of each run, Pallas kernels for 0% -> 0%
where the time goes in v13:
time: 241 us
  waiting for transfers between devices  155 us (64%)
  starting transfers between devices  26 us (11%)
  matrix products  20.7 us (9%)
  blocking collectives  15.5 us (6%)
  between operations  14.1 us (6%)
  other arithmetic  5.94 us (2%)
  local copies, waits for them, and re-layouts  3.27 us (1%)
    all_gather x1, waiting for transfers between devices, body(): gathered = lax.all_gather(normed, SEQ, axis=0, tiled=True)  51.3 us
    all_gather x1, waiting for transfers between devices, body(): row_block = lax.all_gather(slices, SEQ, axis=1, tiled=True)  49.3 us
    reduce_scatter x1, waiting for transfers between devices, body(): lax.psum_scatter(lax.dot_general(out_weight, row_block, (((0,), (1,)), ((...  33.4 us
    all_to_all x1, blocking collectives, body(): lax.all_to_all(buffer.reshape(experts, capacity, columns), 'exp', split_a...  15.5 us
    dot_general x1, matrix products, body(): lax.dot_general(jnp.concatenate([w_gate, w_up], 0), row_block, contract_l...  12.5 us
    ppermute x7, starting transfers between devices, ring_sum(): lax.ppermute(part, axis, [(i, (i + d) % peers) for i in range(peers)])  12.5 us
    ppermute x6, waiting for transfers between devices, ring_shifts(): lax.ppermute(part, axis, [(i, (i + d) % peers) for i in range(peers)])  11.5 us
    ppermute x7, waiting for transfers between devices, ring_sum(): lax.ppermute(part, axis, [(i, (i + d) % peers) for i in range(peers)])  7.43 us
  transfers between devices with their start and end apart: 19, of which 14 were waited for; matrix products, arithmetic and copies ran while one was open for 2% of the time, Pallas kernels for 0%

profile of v13, /device:TPU:1, one launch (start us, length us, event | category | flops | bytes accessed | tf_op | source)
XLA Modules:
  0.0 240.8 jit_solution(35355261227646436)
XLA Ops:
  7.2 0.8 copy.85
  8.2 3.3 %collective-permute-start = (f32[8]{0:T(128)S(1)}, f32[8]{0:T(128)S(1)}, u32[]{:S(2)}, u32[]{:S(2)}) collective-permute-start(f32[8]{0:T(128)S(1)} %fusion.55), channel_id=1, source_target_pairs={{0,8},{8,0},{1,9},{9,1},{2,10},{10,2},{3,11},{11,3},{4,12},{12,4},... | collective-permute-start | bytes 104 | tf_op jit(solution)/shard_map/ppermute | solution.py:71
  11.6 1.7 fusion.23
  13.6 1.6 collective-permute-done.1
  15.8 2.2 collective-permute-start.3
  18.0 1.1 collective-permute-start.2
  19.2 3.4 %collective-permute-done.4 = bf16[4,136,128]{2,1,0:T(8,128)(2,1)S(1)} collective-permute-done((bf16[4,136,128]{2,1,0:T(8,128)(2,1)S(1)}, bf16[4,136,128]{2,1,0:T(8,128)(2,1)S(1)}, u32[]{:S(2)}, u32[]{:S(2)}) %collective-permute-start.4) | collective-permute-done | bytes 139296 | tf_op jit(solution)/shard_map/ppermute | solution.py:44
  22.6 2.0 collective-permute-done.3
  24.7 0.7 collective-permute-done.2
  25.4 0.1 fusion.45
  25.6 0.3 add_convert_fusion
  26.2 1.8 collective-permute-start.7
  28.0 1.7 collective-permute-start.5
  29.8 0.2 convolution_multiply_fusion
  30.0 5.3 %collective-permute-done.6 = bf16[4,136,128]{2,1,0:T(8,128)(2,1)S(1)} collective-permute-done((bf16[4,136,128]{2,1,0:T(8,128)(2,1)S(1)}, bf16[4,136,128]{2,1,0:T(8,128)(2,1)S(1)}, u32[]{:S(2)}, u32[]{:S(2)}) %collective-permute-start.6) | collective-permute-done | bytes 139296 | tf_op jit(solution)/shard_map/ppermute | solution.py:44
  35.6 0.3 fusion.56
  35.8 3.0 %collective-permute-start.8 = (bf16[4,128,128]{2,1,0:T(8,128)(2,1)S(1)}, bf16[4,128,128]{2,1,0:T(8,128)(2,1)S(1)}, u32[]{:S(2)}, u32[]{:S(2)}) collective-permute-start(bf16[4,128,128]{2,1,0:T(8,128)(2,1)S(1)} %get-tuple-element.12), channel_id=1, source_target_pairs={{0,8},{8,0},{1,9},{9,1},{2,10},{10,2},{3,11},{11,3},{4,12},{12,4},... | collective-permute-start | bytes 393224 | tf_op jit(solution)/shard_map/ppermute | solution.py:71
  38.9 0.3 convolution_bitcast_fusion.1
  39.1 0.7 collective-permute-done.8
  39.9 0.8 multiply_reduce_fusion
  40.7 0.8 copy_bitcast_fusion.2
  41.6 51.3 %all-gather.3.cloned.1.call-done = bf16[2048,1024]{1,0:T(8,128)(2,1)} async-done(((bf16[64,1024]{1,0:T(8,128)(2,1)}), bf16[2048,1024]{1,0:T(8,128)(2,1)}) %all-gather.3.cloned.1.call-update) | async-done | bytes 4194320 | tf_op jit(solution)/shard_map/all_gather | solution.py:155
  92.9 4.9 %convolution_bitcast_fusion = f32[192,2048]{1,0:T(8,128)} fusion(bf16[2048,1024]{1,0:T(8,128)(2,1)} %all-gather.3.cloned.1.call-done, bf16[1024,192]{0,1:T(8,128)(2,1)S(1)} %copy-done), kind=kOutput, calls=%fused_computation.4 | convolution fusion | flops 805306368 | bytes 6160384 | tf_op jit(solution)/shard_map/dot_general | solution.py:158
  98.0 0.1 eq.69
  98.1 0.1 eq.65
  98.3 1.1 reduce-window.6
  99.4 0.2 slice_reduce_fusion
  99.8 0.1 sub.61
  100.0 33.4 %reduce-scatter.2.cloned.1.call-done = f32[192,256]{1,0:T(8,128)} async-done(((f32[192,2048]{1,0:T(8,128)}), f32[192,256]{1,0:T(8,128)}) %reduce-scatter.2.cloned.1.call-update) | async-done | bytes 196624 | tf_op jit(solution)/shard_map/reduce_scatter | solution.py:157
  133.5 0.9 fusion.27
  134.4 0.4 fusion.4
  134.9 15.5 %all_to_all.5 = bf16[8,128,192]{1,2,0:T(8,128)(2,1)S(1)} all-to-all(bf16[8,128,192]{1,2,0:T(8,128)(2,1)S(1)} %bitcast.101), channel_id=1, replica_groups=mesh['seq_0'=4,'seq_1'=4,'seq_2'=2,'exp'=8] {'exp'}, dimensions={0} | all-to-all | bytes 786432 | tf_op jit(solution)/shard_map/all_to_all | solution.py:185
  150.4 0.8 copy_bitcast_fusion
  151.4 5.3 %collective-permute-start.9 = (f32[1024]{0:T(1024)S(1)}, f32[1024]{0:T(1024)S(1)}, u32[]{:S(2)}, u32[]{:S(2)}) collective-permute-start(f32[1024]{0:T(1024)S(1)} %fusion.10), channel_id=1, source_target_pairs={{0,8},{8,0},{1,9},{9,1},{2,10},{10,2},{3,11},{11,3},{4,12},{12,4},... | collective-permute-start | bytes 12296 | tf_op jit(solution)/shard_map/ppermute | solution.py:78
  156.7 0.8 collective-permute-done.9
  157.5 2.4 %collective-permute-start.12 = (f32[1024]{0:T(1024)S(1)}, f32[1024]{0:T(1024)S(1)}, u32[]{:S(2)}, u32[]{:S(2)}) collective-permute-start(f32[1024]{0:T(1024)S(1)} %add.156), channel_id=1, source_target_pairs={{0,48},{16,0},{32,16},{48,32},{1,49},{17,1},{33,17},{49,33},{2,50}... | collective-permute-start | bytes 12296 | tf_op jit(solution)/shard_map/ppermute | solution.py:78
  160.0 0.5 collective-permute-start.11
  160.5 0.6 collective-permute-start.10
  161.1 2.8 %collective-permute-done.11 = f32[1024]{0:T(1024)S(1)} collective-permute-done((f32[1024]{0:T(1024)S(1)}, f32[1024]{0:T(1024)S(1)}, u32[]{:S(2)}, u32[]{:S(2)}) %collective-permute-start.11) | collective-permute-done | bytes 4128 | tf_op jit(solution)/shard_map/ppermute | solution.py:78
  163.9 0.2 collective-permute-done.10
  164.2 2.5 %collective-permute-start.15 = (f32[1024]{0:T(1024)S(1)}, f32[1024]{0:T(1024)S(1)}, u32[]{:S(2)}, u32[]{:S(2)}) collective-permute-start(f32[1024]{0:T(1024)S(1)} %add_add_fusion), channel_id=1, source_target_pairs={{0,192},{64,0},{128,64},{192,128},{1,193},{65,1},{129,65},{193,129... | collective-permute-start | bytes 12296 | tf_op jit(solution)/shard_map/ppermute | solution.py:78
  166.6 0.6 collective-permute-start.14
  167.2 0.6 collective-permute-start.13
  167.7 3.0 %collective-permute-done.14 = f32[1024]{0:T(1024)S(1)} collective-permute-done((f32[1024]{0:T(1024)S(1)}, f32[1024]{0:T(1024)S(1)}, u32[]{:S(2)}, u32[]{:S(2)}) %collective-permute-start.14) | collective-permute-done | bytes 4128 | tf_op jit(solution)/shard_map/ppermute | solution.py:78
  170.7 0.6 collective-permute-done.13
  171.3 49.3 %all-gather.5.cloned.1.call-done = bf16[1024,6144]{0,1:T(8,128)(2,1)} async-done(((bf16[1024,192]{0,1:T(8,128)(2,1)}), bf16[1024,6144]{0,1:T(8,128)(2,1)}) %all-gather.5.cloned.1.call-update) | async-done | bytes 12582928 | tf_op jit(solution)/shard_map/all_gather | solution.py:190
  220.6 12.5 %fusion = f32[576,1024]{1,0:T(8,128)S(1)} fusion(bf16[1024,6144]{0,1:T(8,128)(2,1)} %all-gather.5.cloned.1.call-done, bf16[288,6144]{1,0:T(8,128)(2,1)} %bitcast.105, bf16[288,6144]{1,0:T(8,128)(2,1)} %bitcast.106), kind=kOutput, calls=%fused_computation | convolution fusion | flops 7261913088 | bytes 22020096 | tf_op jit(solution)/shard_map/dot_general | solution.py:194
  233.1 1.2 fusion.11
  (75 shorter events, 2.5 us)
Async XLA Ops:
  7.2 85.7 %copy-start = (bf16[1024,192]{0,1:T(8,128)(2,1)S(1)}, bf16[1024,192]{0,1:T(8,128)(2,1)}, u32[]{:S(2)}) copy-start(bf16[1024,192]{0,1:T(8,128)(2,1)} %param.13) | copy-start | bytes 1179652
  7.2 22.6 %copy-start.2 = (bf16[64,1024]{1,0:T(8,128)(2,1)S(1)}, bf16[64,1024]{1,0:T(8,128)(2,1)}, u32[]{:S(2)}) copy-start(bf16[64,1024]{1,0:T(8,128)(2,1)} %param.10) | copy-start | bytes 393220
  7.2 22.6 %copy-start.6 = (bf16[64,1024]{1,0:T(8,128)(2,1)S(1)}, bf16[64,1024]{1,0:T(8,128)(2,1)}, u32[]{:S(2)}) copy-start(bf16[64,1024]{1,0:T(8,128)(2,1)} %param.9) | copy-start | bytes 393220
  7.2 85.7 %all-gather.3.cloned.1.call-start = ((), (), s32[]{:S(2)}) async-start(), calls=%async_computation.2 | async-start | bytes 4325376 | tf_op jit(solution)/shard_map/all_gather | solution.py:155
  8.2 5.3 %collective-permute-start = (f32[8]{0:T(128)S(1)}, f32[8]{0:T(128)S(1)}, u32[]{:S(2)}, u32[]{:S(2)}) collective-permute-start(f32[8]{0:T(128)S(1)} %fusion.55), channel_id=1, source_target_pairs={{0,8},{8,0},{1,9},{9,1},{2,10},{10,2},{3,11},{11,3},{4,12},{12,4},... | collective-permute-start | bytes 104 | tf_op jit(solution)/shard_map/ppermute | solution.py:71
  13.3 2.0 collective-permute-start.1
  15.4 23.4 %copy-start.1 = (bf16[64,1024]{1,0:T(8,128)(2,1)S(1)}, bf16[64,1024]{1,0:T(8,128)(2,1)}, u32[]{:S(2)}) copy-start(bf16[64,1024]{1,0:T(8,128)(2,1)} %param.11) | copy-start | bytes 393220
  15.7 6.9 %collective-permute-start.4 = (bf16[4,136,128]{2,1,0:T(8,128)(2,1)S(1)}, bf16[4,136,128]{2,1,0:T(8,128)(2,1)S(1)}, u32[]{:S(2)}, u32[]{:S(2)}) collective-permute-start(bf16[4,136,128]{2,1,0:T(8,128)(2,1)S(1)} %maximum_maximum_fusion), channel_id=1, source_target_pairs={{0,16},{16,32},{32,48},{48,0},{1,17},{17,33},{33,49},{49,1},{2,18}... | collective-permute-start | bytes 417800 | tf_op jit(solution)/shard_map/ppermute | solution.py:44
  15.8 8.9 %collective-permute-start.3 = (bf16[4,136,128]{2,1,0:T(8,128)(2,1)S(1)}, bf16[4,136,128]{2,1,0:T(8,128)(2,1)S(1)}, u32[]{:S(2)}, u32[]{:S(2)}) collective-permute-start(bf16[4,136,128]{2,1,0:T(8,128)(2,1)S(1)} %maximum_maximum_fusion), channel_id=1, source_target_pairs={{0,32},{16,48},{32,0},{48,16},{1,33},{17,49},{33,1},{49,17},{2,34}... | collective-permute-start | bytes 417800 | tf_op jit(solution)/shard_map/ppermute | solution.py:44
  18.0 7.3 %collective-permute-start.2 = (bf16[4,136,128]{2,1,0:T(8,128)(2,1)S(1)}, bf16[4,136,128]{2,1,0:T(8,128)(2,1)S(1)}, u32[]{:S(2)}, u32[]{:S(2)}) collective-permute-start(bf16[4,136,128]{2,1,0:T(8,128)(2,1)S(1)} %maximum_maximum_fusion), channel_id=1, source_target_pairs={{0,48},{16,0},{32,16},{48,32},{1,49},{17,1},{33,17},{49,33},{2,50}... | collective-permute-start | bytes 417800 | tf_op jit(solution)/shard_map/ppermute | solution.py:44
  26.2 9.4 %collective-permute-start.7 = (bf16[4,136,128]{2,1,0:T(8,128)(2,1)S(1)}, bf16[4,136,128]{2,1,0:T(8,128)(2,1)S(1)}, u32[]{:S(2)}, u32[]{:S(2)}) collective-permute-start(bf16[4,136,128]{2,1,0:T(8,128)(2,1)S(1)} %maximum_maximum_fusion.1), channel_id=1, source_target_pairs={{0,192},{64,0},{128,64},{192,128},{1,193},{65,1},{129,65},{193,129... | collective-permute-start | bytes 417800 | tf_op jit(solution)/shard_map/ppermute | solution.py:44
  28.0 7.3 %collective-permute-start.6 = (bf16[4,136,128]{2,1,0:T(8,128)(2,1)S(1)}, bf16[4,136,128]{2,1,0:T(8,128)(2,1)S(1)}, u32[]{:S(2)}, u32[]{:S(2)}) collective-permute-start(bf16[4,136,128]{2,1,0:T(8,128)(2,1)S(1)} %maximum_maximum_fusion.1), channel_id=1, source_target_pairs={{0,64},{64,128},{128,192},{192,0},{1,65},{65,129},{129,193},{193,1... | collective-permute-start | bytes 417800 | tf_op jit(solution)/shard_map/ppermute | solution.py:44
  28.0 7.4 %collective-permute-start.5 = (bf16[4,136,128]{2,1,0:T(8,128)(2,1)S(1)}, bf16[4,136,128]{2,1,0:T(8,128)(2,1)S(1)}, u32[]{:S(2)}, u32[]{:S(2)}) collective-permute-start(bf16[4,136,128]{2,1,0:T(8,128)(2,1)S(1)} %maximum_maximum_fusion.1), channel_id=1, source_target_pairs={{0,128},{64,192},{128,0},{192,64},{1,129},{65,193},{129,1},{193,65... | collective-permute-start | bytes 417800 | tf_op jit(solution)/shard_map/ppermute | solution.py:44
  35.8 4.0 %collective-permute-start.8 = (bf16[4,128,128]{2,1,0:T(8,128)(2,1)S(1)}, bf16[4,128,128]{2,1,0:T(8,128)(2,1)S(1)}, u32[]{:S(2)}, u32[]{:S(2)}) collective-permute-start(bf16[4,128,128]{2,1,0:T(8,128)(2,1)S(1)} %get-tuple-element.12), channel_id=1, source_target_pairs={{0,8},{8,0},{1,9},{9,1},{2,10},{10,2},{3,11},{11,3},{4,12},{12,4},... | collective-permute-start | bytes 393224 | tf_op jit(solution)/shard_map/ppermute | solution.py:71
  41.5 56.3 %copy-start.5 = (s32[256,2]{0,1:T(2,128)S(1)}, s32[256,2]{0,1:T(2,128)}, u32[]{:S(2)}) copy-start(s32[256,2]{0,1:T(2,128)} %param.15) | copy-start | bytes 6148
  41.5 91.9 %copy-start.3 = (bf16[256,192]{0,1:T(8,128)(2,1)S(1)}, bf16[256,192]{0,1:T(8,128)(2,1)}, u32[]{:S(2)}) copy-start(bf16[256,192]{0,1:T(8,128)(2,1)} %param.14) | copy-start | bytes 294916
  41.5 91.9 %reduce-scatter.2.cloned.1.call-start = ((), (), s32[]{:S(2)}) async-start(), calls=%async_computation.3 | async-start | bytes 1769472 | tf_op jit(solution)/shard_map/reduce_scatter | solution.py:157
  97.8 122.8 %all-gather.5.cloned.1.call-start = ((), (), s32[]{:S(2)}) async-start(), calls=%async_computation.4 | async-start | bytes 12976128 | tf_op jit(solution)/shard_map/all_gather | solution.py:190
  134.4 98.7 %copy-start.4 = (bf16[256,192]{0,1:T(8,128)(2,1)}, bf16[256,192]{0,1:T(8,128)(2,1)S(1)}, u32[]{:S(2)}) copy-start(bf16[256,192]{0,1:T(8,128)(2,1)S(1)} %fusion.27) | copy-start | bytes 294916
  151.4 6.1 %collective-permute-start.9 = (f32[1024]{0:T(1024)S(1)}, f32[1024]{0:T(1024)S(1)}, u32[]{:S(2)}, u32[]{:S(2)}) collective-permute-start(f32[1024]{0:T(1024)S(1)} %fusion.10), channel_id=1, source_target_pairs={{0,8},{8,0},{1,9},{9,1},{2,10},{10,2},{3,11},{11,3},{4,12},{12,4},... | collective-permute-start | bytes 12296 | tf_op jit(solution)/shard_map/ppermute | solution.py:78
  157.5 3.6 %collective-permute-start.12 = (f32[1024]{0:T(1024)S(1)}, f32[1024]{0:T(1024)S(1)}, u32[]{:S(2)}, u32[]{:S(2)}) collective-permute-start(f32[1024]{0:T(1024)S(1)} %add.156), channel_id=1, source_target_pairs={{0,48},{16,0},{32,16},{48,32},{1,49},{17,1},{33,17},{49,33},{2,50}... | collective-permute-start | bytes 12296 | tf_op jit(solution)/shard_map/ppermute | solution.py:78
  160.0 4.0 %collective-permute-start.11 = (f32[1024]{0:T(1024)S(1)}, f32[1024]{0:T(1024)S(1)}, u32[]{:S(2)}, u32[]{:S(2)}) collective-permute-start(f32[1024]{0:T(1024)S(1)} %add.156), channel_id=1, source_target_pairs={{0,32},{16,48},{32,0},{48,16},{1,33},{17,49},{33,1},{49,17},{2,34}... | collective-permute-start | bytes 12296 | tf_op jit(solution)/shard_map/ppermute | solution.py:78
  160.5 3.7 %collective-permute-start.10 = (f32[1024]{0:T(1024)S(1)}, f32[1024]{0:T(1024)S(1)}, u32[]{:S(2)}, u32[]{:S(2)}) collective-permute-start(f32[1024]{0:T(1024)S(1)} %add.156), channel_id=1, source_target_pairs={{0,16},{16,32},{32,48},{48,0},{1,17},{17,33},{33,49},{49,1},{2,18}... | collective-permute-start | bytes 12296 | tf_op jit(solution)/shard_map/ppermute | solution.py:78
  164.2 3.6 %collective-permute-start.15 = (f32[1024]{0:T(1024)S(1)}, f32[1024]{0:T(1024)S(1)}, u32[]{:S(2)}, u32[]{:S(2)}) collective-permute-start(f32[1024]{0:T(1024)S(1)} %add_add_fusion), channel_id=1, source_target_pairs={{0,192},{64,0},{128,64},{192,128},{1,193},{65,1},{129,65},{193,129... | collective-permute-start | bytes 12296 | tf_op jit(solution)/shard_map/ppermute | solution.py:78
  166.6 4.1 %collective-permute-start.14 = (f32[1024]{0:T(1024)S(1)}, f32[1024]{0:T(1024)S(1)}, u32[]{:S(2)}, u32[]{:S(2)}) collective-permute-start(f32[1024]{0:T(1024)S(1)} %add_add_fusion), channel_id=1, source_target_pairs={{0,128},{64,192},{128,0},{192,64},{1,129},{65,193},{129,1},{193,65... | collective-permute-start | bytes 12296 | tf_op jit(solution)/shard_map/ppermute | solution.py:78
  167.2 4.1 %collective-permute-start.13 = (f32[1024]{0:T(1024)S(1)}, f32[1024]{0:T(1024)S(1)}, u32[]{:S(2)}, u32[]{:S(2)}) collective-permute-start(f32[1024]{0:T(1024)S(1)} %add_add_fusion), channel_id=1, source_target_pairs={{0,64},{64,128},{128,192},{192,0},{1,65},{65,129},{129,193},{193,1... | collective-permute-start | bytes 12296 | tf_op jit(solution)/shard_map/ppermute | solution.py:78
Sparse Core Ops, SparseCore 0:
  41.6 51.1 all-gather.2
  97.9 35.5 reduce-scatter.1
  151.4 69.1 all-gather.4
